TPU v7x, 512 devices: a whole 4x4x16 slice. The times are simulated.
512 devices in a mesh: blk: 32 (over z, y_lo), rep: 16 (over x, y_hi, core).
Axes of the slice: x: 4, y: 4 (y_hi: 2, y_lo: 2; y = y_hi * 2 + y_lo), z: 16, core: 2. Of those that a mesh axis runs over, the one named last changes fastest.
Arguments:
- feats: bfloat16 [32768, 256], P(('blk', 'rep')), may hold values from -6 to 6
- weight: bfloat16 [256, 256], replicated, may hold values from -0.375 to 0.375
- bias: float32 [256], replicated, may hold values from -4 to 4
- grad_out: bfloat16 [32768, 256], P(('blk', 'rep')), may hold values from -6 to 6
- tile_values: bfloat16 [32, 16, 2, 64, 128, 128], P('blk', 'rep'), may hold values from -0.03125 to 0.03125
- tile_rows: int32 [32, 16, 2, 64], P('blk', 'rep'), may hold values from 0 to 7, as said below
- tile_cols: int32 [32, 16, 2, 64], P('blk', 'rep'), may hold values from 0 to 7, as said below
- tile_count: int32 [32, 16, 2], P('blk', 'rep'), may hold values from 32 to 64, as said below
Outputs:
- out: bfloat16 [32768, 256], P(('blk', 'rep'))
- grad_feats: bfloat16 [32768, 256], P(('blk', 'rep'))
- grad_weight: float32 [256, 256], P('rep')
- grad_bias: float32 [256], replicated
Inputs may be any that keep to these rules, and one draw needn't show every extreme that they name: `tile_count`: some pair slot of some device holds exactly 64 live entries; slots past the count hold values that must be ignored. Within one pair slot the 64 entries name distinct (tile_rows, tile_cols) cells. `tile_cols`: see tile_rows: cells of one slot are distinct.
All inputs are finite; a program needn't handle non-finite values.
Results may differ from a plain program's by a relative error of at most 0.018.
Values may be sent and summed in bfloat16 or wider, within the bound.
No kernel may reach another device: no remote copies, remote signals or barrier semaphores. Data moves between devices by JAX's collectives and lax.ppermute only.
A program may use at most 64 MiB of HBM per device.

v0:
```python
import jax
import jax.numpy as jnp
from jax import lax
from jax.sharding import PartitionSpec as P


def passed_along(x, axis, by):
    devices = lax.axis_size(axis)
    return lax.ppermute(x, axis, [(i, (i + by) % devices) for i in range(devices)])


def forward_tiles(total, source, tile_vals, tile_row, tile_col, live, tile_size):

    def forward_one_tile(position, total):
        row_start = tile_row[position] * tile_size
        col_start = tile_col[position] * tile_size
        source_rows = lax.dynamic_slice_in_dim(source, col_start, tile_size, 0)
        current = lax.dynamic_slice_in_dim(total, row_start, tile_size, 0)
        current = current + jnp.dot(
            tile_vals[position], source_rows, preferred_element_type=jnp.float32
        )
        return lax.dynamic_update_slice_in_dim(total, current, row_start, 0)

    return lax.fori_loop(0, live, forward_one_tile, total)


def backward_tiles(total, grad_block, tile_vals, tile_row, tile_col, live, tile_size):

    def backward_one_tile(position, total):
        row_start = tile_row[position] * tile_size
        col_start = tile_col[position] * tile_size
        grad_rows = lax.dynamic_slice_in_dim(grad_block, row_start, tile_size, 0)
        term = lax.dot_general(
            tile_vals[position],
            grad_rows,
            (((0,), (0,)), ((), ())),
            preferred_element_type=jnp.float32,
        )
        current = lax.dynamic_slice_in_dim(total, col_start, tile_size, 0)
        return lax.dynamic_update_slice_in_dim(total, current + term, col_start, 0)

    return lax.fori_loop(0, live, backward_one_tile, total)


def activation(pre_act, cotangent):
    logistic = jax.nn.sigmoid(pre_act)
    result = (pre_act * logistic).astype(jnp.bfloat16)
    grad_pre = (
        cotangent.astype(jnp.float32) * logistic * (1.0 + pre_act * (1.0 - logistic))
    ).astype(jnp.bfloat16)
    return (result, grad_pre)


def body(feats, weight, bias, grad_out, tile_values, tile_rows, tile_cols, tile_count):
    replicas = lax.axis_size("rep")
    rep_index = lax.axis_index("rep")
    tile_size = tile_values.shape[-1]
    pair_slots = tile_values.shape[2]
    digit_count = (replicas - 1).bit_length()
    values_here = tile_values[0, 0]
    rows_here = tile_rows[0, 0]
    cols_here = tile_cols[0, 0]
    counts_here = tile_count[0, 0]
    hw_slice = jnp.dot(feats, weight, preferred_element_type=jnp.float32).astype(jnp.bfloat16)
    feature_block = lax.all_gather(hw_slice, "rep", axis=0, tiled=True)
    for level in range(digit_count):
        shifted = passed_along(feature_block, "blk", 1 << level)
        feature_block = jnp.where(rep_index // (1 << level) % 2 == 1, shifted, feature_block)
    aggregate = jnp.zeros(feature_block.shape, jnp.float32)
    for slot in range(pair_slots):
        aggregate = forward_tiles(
            aggregate,
            feature_block,
            values_here[slot],
            rows_here[slot],
            cols_here[slot],
            counts_here[slot],
            tile_size,
        )
        if slot + 1 < pair_slots:
            feature_block = passed_along(feature_block, "blk", replicas)
    aggregate_rows = lax.psum_scatter(
        aggregate.astype(jnp.bfloat16), "rep", scatter_dimension=0, tiled=True
    ).astype(jnp.float32)
    out, grad_rows = activation(aggregate_rows + bias, grad_out)
    grad_block = lax.all_gather(grad_rows, "rep", axis=0, tiled=True)
    partial_grad = jnp.zeros(grad_block.shape, jnp.float32)
    for slot in reversed(range(pair_slots)):
        partial_grad = backward_tiles(
            partial_grad,
            grad_block,
            values_here[slot],
            rows_here[slot],
            cols_here[slot],
            counts_here[slot],
            tile_size,
        )
        if slot > 0:
            partial_grad = passed_along(partial_grad.astype(jnp.bfloat16), "blk", -replicas).astype(
                partial_grad.dtype
            )
    for level in reversed(range(digit_count)):
        shifted = passed_along(partial_grad.astype(jnp.bfloat16), "blk", -(1 << level)).astype(
            partial_grad.dtype
        )
        partial_grad = jnp.where(rep_index // (1 << level) % 2 == 1, shifted, partial_grad)
    grad_hw = lax.psum_scatter(
        partial_grad.astype(jnp.bfloat16), "rep", scatter_dimension=0, tiled=True
    )
    grad_feats = lax.dot_general(
        grad_hw, weight, (((1,), (1,)), ((), ())), preferred_element_type=jnp.float32
    ).astype(jnp.bfloat16)
    weight_terms = lax.dot_general(
        feats, grad_hw, (((0,), (0,)), ((), ())), preferred_element_type=jnp.float32
    )
    weight_rows = weight.shape[0] // replicas
    bias_terms = jnp.sum(grad_rows.astype(jnp.float32), axis=0)
    weight_total, grad_bias = lax.psum((weight_terms, bias_terms), ("blk", "rep"))
    grad_weight = lax.dynamic_slice_in_dim(weight_total, rep_index * weight_rows, weight_rows, 0)
    return (out, grad_feats, grad_weight, grad_bias)


def solution(mesh):
    in_specs = (
        P(("blk", "rep"), None),
        P(),
        P(),
        P(("blk", "rep"), None),
        P("blk", "rep", None, None, None, None),
        P("blk", "rep", None, None),
        P("blk", "rep", None, None),
        P("blk", "rep", None),
    )
    out_specs = (P(("blk", "rep"), None), P(("blk", "rep"), None), P("rep", None), P())
    return jax.shard_map(body, mesh=mesh, in_specs=in_specs, out_specs=out_specs, check_vma=False)
```

profile of v0, /device:TPU:6, one launch (start us, length us, event | category | flops | bytes accessed | tf_op | source)
XLA Modules:
  0.0 1982.8 jit_solution(10087063126858691895)
XLA Ops:
  9.0 22.8 %all_gather.6 = bf16[1024,256]{1,0:T(8,128)(2,1)S(1)} all-gather(bf16[64,256]{1,0:T(8,128)(2,1)S(1)} %convolution_convert_fusion.1), channel_id=1, replica_groups=mesh['blk'=32,'rep'=16] {'rep'}, dimensions={0}, use_global_device_ids=true | all-gather | bytes 557056 | tf_op jit(solution)/shard_map/all_gather | solution.py:65
  31.8 2.4 collective-permute-start
  34.2 21.3 %collective-permute-done = bf16[1024,256]{1,0:T(8,128)(2,1)S(1)} collective-permute-done((bf16[1024,256]{1,0:T(8,128)(2,1)S(1)}, bf16[1024,256]{1,0:T(8,128)(2,1)S(1)}, u32[]{:S(2)}, u32[]{:S(2)}) %collective-permute-start) | collective-permute-done | bytes 524320 | tf_op jit(solution)/shard_map/ppermute | solution.py:9
  55.6 1.9 collective-permute-start.1
  57.6 14.7 collective-permute-done.1
  72.4 1.9 collective-permute-start.2
  74.4 25.1 %collective-permute-done.2 = bf16[1024,256]{1,0:T(8,128)(2,1)S(1)} collective-permute-done((bf16[1024,256]{1,0:T(8,128)(2,1)S(1)}, bf16[1024,256]{1,0:T(8,128)(2,1)S(1)}, u32[]{:S(2)}, u32[]{:S(2)}) %collective-permute-start.2) | collective-permute-done | bytes 524320 | tf_op jit(solution)/shard_map/ppermute | solution.py:9
  99.5 3.1 collective-permute-start.3
  102.7 4.0 slice_bitcast_fusion
  106.7 40.8 %collective-permute-done.3 = bf16[1024,256]{1,0:T(8,128)(2,1)S(1)} collective-permute-done((bf16[1024,256]{1,0:T(8,128)(2,1)S(1)}, bf16[1024,256]{1,0:T(8,128)(2,1)S(1)}, u32[]{:S(2)}, u32[]{:S(2)}) %collective-permute-start.3) | collective-permute-done | bytes 524320 | tf_op jit(solution)/shard_map/ppermute | solution.py:9
  148.3 4.8 collective-permute-start.4
  153.8 134.8 %while.40 = (s32[]{:T(128)}, f32[1024,256]{1,0:T(8,128)S(1)}, s32[]{:T(128)}, s32[64]{0:T(128)S(1)}, bf16[64,128,128]{2,1,0:T(8,128)(2,1)S(1)}, /*index=5*/s32[6...) while((s32[]{:T(128)}, f32[1024,256]{1,0:T(8,128)S(1)}, ...), condition=%wide.region_1.2_spmd, body=%wide.region_0.1_spmd.sunk | while | flops 8421389 | bytes 360727 | solution.py:24
  288.6 209.5 %while.41 = (s32[]{:T(128)}, f32[1024,256]{1,0:T(8,128)S(1)}, s32[]{:T(128)}, s32[64]{0:T(128)S(1)}, bf16[64,128,128]{2,1,0:T(8,128)(2,1)}, /*index=5*/s32[64]{0...) while((s32[]{:T(128)}, f32[1024,256]{1,0:T(8,128)S(1)}, ...), condition=%wide.region_3.4_spmd, body=%wide.region_2.3_spmd.sunk | while | flops 8421389 | bytes 360727 | solution.py:24
  499.1 279.8 %reduce-scatter.3.cloned.1.call-done = bf16[64,256]{1,0:T(8,128)(2,1)} async-done(((bf16[1024,256]{1,0:T(8,128)(2,1)}), bf16[64,256]{1,0:T(8,128)(2,1)}) %reduce-scatter.3.cloned.1.call-update) | async-done | bytes 32784 | tf_op jit(solution)/shard_map/reduce_scatter | solution.py:82
  778.8 1.4 convert_reduce_fusion
  780.2 21.6 %all_gather.7 = bf16[1024,256]{1,0:T(8,128)(2,1)} all-gather(bf16[64,256]{1,0:T(8,128)(2,1)S(1)} %get-tuple-element.221), channel_id=1, replica_groups=mesh['blk'=32,'rep'=16] {'rep'}, dimensions={0}, use_global_device_ids=true | all-gather | bytes 557056 | tf_op jit(solution)/shard_map/all_gather | solution.py:86
  801.9 211.9 %while.42 = (s32[]{:T(128)}, f32[1024,256]{1,0:T(8,128)S(1)}, s32[]{:T(128)}, s32[64]{0:T(128)S(1)}, bf16[64,128,128]{2,1,0:T(8,128)(2,1)}, /*index=5*/s32[64]{0...) while((s32[]{:T(128)}, f32[1024,256]{1,0:T(8,128)S(1)}, ...), condition=%wide.region_6.7_spmd, body=%wide.region_5.6_spmd.sunk | while | flops 8421389 | bytes 360727 | solution.py:42
  1014.6 1.9 collective-permute-start.5
  1016.5 19.1 collective-permute-done.5
  1036.7 136.4 %while.43 = (s32[]{:T(128)}, f32[1024,256]{1,0:T(8,128)S(1)}, s32[]{:T(128)}, s32[64]{0:T(128)S(1)}, bf16[64,128,128]{2,1,0:T(8,128)(2,1)S(1)}, /*index=5*/s32[6...) while((s32[]{:T(128)}, f32[1024,256]{1,0:T(8,128)S(1)}, ...), condition=%wide.region_8.9_spmd, body=%wide.region_7.8_spmd.sunk | while | flops 8421389 | bytes 360727 | solution.py:42
  1173.2 49.7 %collective-permute-start.6 = (bf16[1024,256]{1,0:T(8,128)(2,1)S(1)}, bf16[1024,256]{1,0:T(8,128)(2,1)S(1)}, u32[]{:S(2)}, u32[]{:S(2)}) collective-permute-start(bf16[1024,256]{1,0:T(8,128)(2,1)S(1)} %convert_element_type.65), channel_id=1, source_target_pairs={{0,384},{16,400},{32,416},{48,432},{64,448},{80,464},{96,480},{112... | collective-permute-start | bytes 1572872 | tf_op jit(solution)/shard_map/ppermute | solution.py:9
  1223.0 6.7 collective-permute-done.6
  1229.8 90.0 %collective-permute-start.7 = (bf16[1024,256]{1,0:T(8,128)(2,1)S(1)}, bf16[1024,256]{1,0:T(8,128)(2,1)S(1)}, u32[]{:S(2)}, u32[]{:S(2)}) collective-permute-start(bf16[1024,256]{1,0:T(8,128)(2,1)S(1)} %fusion.20), channel_id=1, source_target_pairs={{0,448},{16,464},{32,480},{48,496},{64,0},{80,16},{96,32},{112,48}... | collective-permute-start | bytes 1572872 | tf_op jit(solution)/shard_map/ppermute | solution.py:9
  1319.8 10.3 collective-permute-done.7
  1330.3 51.7 %collective-permute-start.8 = (bf16[1024,256]{1,0:T(8,128)(2,1)S(1)}, bf16[1024,256]{1,0:T(8,128)(2,1)S(1)}, u32[]{:S(2)}, u32[]{:S(2)}) collective-permute-start(bf16[1024,256]{1,0:T(8,128)(2,1)S(1)} %convert_select_fusion.1), channel_id=1, source_target_pairs={{0,480},{16,496},{32,0},{48,16},{64,32},{80,48},{96,64},{112,80},{... | collective-permute-start | bytes 1572872 | tf_op jit(solution)/shard_map/ppermute | solution.py:9
  1382.0 9.3 collective-permute-done.8
  1391.5 20.1 %collective-permute-start.9 = (bf16[1024,256]{1,0:T(8,128)(2,1)S(1)}, bf16[1024,256]{1,0:T(8,128)(2,1)S(1)}, u32[]{:S(2)}, u32[]{:S(2)}) collective-permute-start(bf16[1024,256]{1,0:T(8,128)(2,1)S(1)} %fusion.21), channel_id=1, source_target_pairs={{0,496},{16,0},{32,16},{48,32},{64,48},{80,64},{96,80},{112,96},{1... | collective-permute-start | bytes 1572872 | tf_op jit(solution)/shard_map/ppermute | solution.py:9
  1411.6 6.7 collective-permute-done.9
  1419.4 104.4 %psum.15 = f32[256]{0:T(256)} all-reduce(f32[256]{0:T(256)S(1)} %get-tuple-element.220), channel_id=1, replica_groups=mesh['blk'=32,'rep'=16] {'blk','rep'}, use_global_device_ids=true, to_apply=%region_12.13 | all-reduce | flops 256 | bytes 2048 | tf_op jit(solution)/shard_map/psum | solution.py:118
  1523.8 1.7 convolution_bitcast_fusion
  1525.5 1.6 convolution_convert_fusion
  1527.0 447.6 %all-reduce.2.cloned.1.call-done = f32[256,256]{0,1:T(8,128)} async-done(((f32[256,256]{0,1:T(8,128)}), f32[256,256]{0,1:T(8,128)}) %all-reduce.2.cloned.1.call-update) | async-done | bytes 262160 | tf_op jit(solution)/shard_map/psum | solution.py:118
  (539 shorter events, 375.8 us)
Async XLA Ops:
  7.2 0.9 copy-start
  7.2 771.6 %reduce-scatter.3.cloned.1.call-start = ((), (), s32[]{:S(2)}) async-start(), calls=%async_computation.2 | async-start | bytes 557056 | tf_op jit(solution)/shard_map/reduce_scatter | solution.py:82
  31.8 23.7 %collective-permute-start = (bf16[1024,256]{1,0:T(8,128)(2,1)S(1)}, bf16[1024,256]{1,0:T(8,128)(2,1)S(1)}, u32[]{:S(2)}, u32[]{:S(2)}) collective-permute-start(bf16[1024,256]{1,0:T(8,128)(2,1)S(1)} %all_gather.6), channel_id=1, source_target_pairs={{0,16},{16,32},{32,48},{48,64},{64,80},{80,96},{96,112},{112,128},... | collective-permute-start | bytes 1572872 | tf_op jit(solution)/shard_map/ppermute | solution.py:9
  34.2 68.4 %copy-start.5 = (s32[1,1,2,64]{3,2,1,0:T(2,128)S(1)}, s32[1,1,2,64]{3,2,1,0:T(2,128)}, u32[]{:S(2)}) copy-start(s32[1,1,2,64]{3,2,1,0:T(2,128)} %param.22) | copy-start | bytes 1540
  34.2 68.4 %copy-start.6 = (s32[1,1,2,64]{3,2,1,0:T(2,128)S(1)}, s32[1,1,2,64]{3,2,1,0:T(2,128)}, u32[]{:S(2)}) copy-start(s32[1,1,2,64]{3,2,1,0:T(2,128)} %param.21) | copy-start | bytes 1540
  55.6 16.7 collective-permute-start.1
  72.4 27.0 %collective-permute-start.2 = (bf16[1024,256]{1,0:T(8,128)(2,1)S(1)}, bf16[1024,256]{1,0:T(8,128)(2,1)S(1)}, u32[]{:S(2)}, u32[]{:S(2)}) collective-permute-start(bf16[1024,256]{1,0:T(8,128)(2,1)S(1)} %broadcast_select_fusion.1), channel_id=1, source_target_pairs={{0,64},{16,80},{32,96},{48,112},{64,128},{80,144},{96,160},{112,17... | collective-permute-start | bytes 1572872 | tf_op jit(solution)/shard_map/ppermute | solution.py:9
  99.5 48.0 %collective-permute-start.3 = (bf16[1024,256]{1,0:T(8,128)(2,1)S(1)}, bf16[1024,256]{1,0:T(8,128)(2,1)S(1)}, u32[]{:S(2)}, u32[]{:S(2)}) collective-permute-start(bf16[1024,256]{1,0:T(8,128)(2,1)S(1)} %broadcast_select_fusion.2), channel_id=1, source_target_pairs={{0,128},{16,144},{32,160},{48,176},{64,192},{80,208},{96,224},{112... | collective-permute-start | bytes 1572872 | tf_op jit(solution)/shard_map/ppermute | solution.py:9
  102.6 50.5 %copy-start.3 = (s32[1,1,2]{2,1,0:T(1,128)S(1)}, s32[1,1,2]{2,1,0:T(1,128)}, u32[]{:S(2)}) copy-start(s32[1,1,2]{2,1,0:T(1,128)} %param.23) | copy-start | bytes 28
  148.3 140.3 %collective-permute-start.4 = (bf16[1024,256]{1,0:T(8,128)(2,1)}, bf16[1024,256]{1,0:T(8,128)(2,1)}, u32[]{:S(2)}, u32[]{:S(2)}) collective-permute-start(bf16[1024,256]{1,0:T(8,128)(2,1)} %broadcast_select_fusion.3), channel_id=1, source_target_pairs={{0,256},{16,272},{32,288},{48,304},{64,320},{80,336},{96,352},{112... | collective-permute-start | bytes 1572872 | tf_op jit(solution)/shard_map/ppermute | solution.py:9
  288.6 490.2 %copy-start.2 = (bf16[64,256]{1,0:T(8,128)(2,1)S(1)}, bf16[64,256]{1,0:T(8,128)(2,1)}, u32[]{:S(2)}) copy-start(bf16[64,256]{1,0:T(8,128)(2,1)} %param.19) | copy-start | bytes 98308
  288.6 490.2 %copy-start.4 = (f32[256]{0:T(256)S(1)}, f32[256]{0:T(256)}, u32[]{:S(2)}) copy-start(f32[256]{0:T(256)} %param.18) | copy-start | bytes 3076
  499.0 1024.8 %reduce-scatter.5.cloned.1.call-start = ((), (), s32[]{:S(2)}) async-start(), calls=%async_computation.3 | async-start | bytes 557056 | tf_op jit(solution)/shard_map/reduce_scatter | solution.py:107
  1014.6 21.0 %collective-permute-start.5 = (bf16[1024,256]{1,0:T(8,128)(2,1)}, bf16[1024,256]{1,0:T(8,128)(2,1)}, u32[]{:S(2)}, u32[]{:S(2)}) collective-permute-start(bf16[1024,256]{1,0:T(8,128)(2,1)} %convert_element_type.63), channel_id=1, source_target_pairs={{0,256},{16,272},{32,288},{48,304},{64,320},{80,336},{96,352},{112... | collective-permute-start | bytes 1572872 | tf_op jit(solution)/shard_map/ppermute | solution.py:9
  1173.2 56.4 %collective-permute-start.6 = (bf16[1024,256]{1,0:T(8,128)(2,1)S(1)}, bf16[1024,256]{1,0:T(8,128)(2,1)S(1)}, u32[]{:S(2)}, u32[]{:S(2)}) collective-permute-start(bf16[1024,256]{1,0:T(8,128)(2,1)S(1)} %convert_element_type.65), channel_id=1, source_target_pairs={{0,384},{16,400},{32,416},{48,432},{64,448},{80,464},{96,480},{112... | collective-permute-start | bytes 1572872 | tf_op jit(solution)/shard_map/ppermute | solution.py:9
  1229.8 100.3 %collective-permute-start.7 = (bf16[1024,256]{1,0:T(8,128)(2,1)S(1)}, bf16[1024,256]{1,0:T(8,128)(2,1)S(1)}, u32[]{:S(2)}, u32[]{:S(2)}) collective-permute-start(bf16[1024,256]{1,0:T(8,128)(2,1)S(1)} %fusion.20), channel_id=1, source_target_pairs={{0,448},{16,464},{32,480},{48,496},{64,0},{80,16},{96,32},{112,48}... | collective-permute-start | bytes 1572872 | tf_op jit(solution)/shard_map/ppermute | solution.py:9
  1330.3 193.5 %copy-start.1 = (bf16[64,256]{1,0:T(8,128)(2,1)S(1)}, bf16[64,256]{1,0:T(8,128)(2,1)}, u32[]{:S(2)}) copy-start(bf16[64,256]{1,0:T(8,128)(2,1)} %param.16) | copy-start | bytes 98308
  1330.3 61.1 %collective-permute-start.8 = (bf16[1024,256]{1,0:T(8,128)(2,1)S(1)}, bf16[1024,256]{1,0:T(8,128)(2,1)S(1)}, u32[]{:S(2)}, u32[]{:S(2)}) collective-permute-start(bf16[1024,256]{1,0:T(8,128)(2,1)S(1)} %convert_select_fusion.1), channel_id=1, source_target_pairs={{0,480},{16,496},{32,0},{48,16},{64,32},{80,48},{96,64},{112,80},{... | collective-permute-start | bytes 1572872 | tf_op jit(solution)/shard_map/ppermute | solution.py:9
  1391.5 26.8 %collective-permute-start.9 = (bf16[1024,256]{1,0:T(8,128)(2,1)S(1)}, bf16[1024,256]{1,0:T(8,128)(2,1)S(1)}, u32[]{:S(2)}, u32[]{:S(2)}) collective-permute-start(bf16[1024,256]{1,0:T(8,128)(2,1)S(1)} %fusion.21), channel_id=1, source_target_pairs={{0,496},{16,0},{32,16},{48,32},{64,48},{80,64},{96,80},{112,96},{1... | collective-permute-start | bytes 1572872 | tf_op jit(solution)/shard_map/ppermute | solution.py:9
  1419.3 555.3 %all-reduce.2.cloned.1.call-start = ((), (), s32[]{:S(2)}) async-start(), calls=%async_computation.4 | async-start | bytes 524288 | tf_op jit(solution)/shard_map/psum | solution.py:118
Sparse Core Ops, SparseCore 0:
  499.1 279.6 reduce-scatter.2
  1419.4 84.6 reduce-scatter.4
  1525.6 448.9 all-reduce.1
where the time goes:
time: 2000 us; the launch traced here: 1980 us
  waiting for transfers between devices  881 us (44%)
  loops' own time  326 us (16%)
  starting transfers between devices  228 us (11%)
  local copies, waits for them, and re-layouts  202 us (10%)
  matrix products  175 us (9%)
  blocking collectives  149 us (7%)
    psum x1, waiting for transfers between devices, body(): lax.psum((weight_terms, bias_terms), ('blk', 'rep'))  448 us
    reduce_scatter x1, waiting for transfers between devices, body(): lax.psum_scatter(aggregate.astype(jnp.bfloat16), 'rep', scatter_dimension...  280 us
    ppermute x10, starting transfers between devices, passed_along(): lax.ppermute(x, axis, [(i, (i + by) % devices) for i in range(devices)])  228 us
    another operation x2, loops' own time, forward_tiles(): return lax.fori_loop(0, live, forward_one_tile, total)  163 us
    another operation x2, loops' own time, backward_tiles(): return lax.fori_loop(0, live, backward_one_tile, total)  163 us
    ppermute x10, waiting for transfers between devices, passed_along(): lax.ppermute(x, axis, [(i, (i + by) % devices) for i in range(devices)])  154 us
    psum x1, blocking collectives, body(): lax.psum((weight_terms, bias_terms), ('blk', 'rep'))  104 us
    dot_general x83, matrix products, backward_one_tile(): lax.dot_general(tile_vals[position], grad_rows, (((0,), (0,)), ((), ())),...  87.6 us
  transfers between devices with their start and end apart: 13, of which 11 were waited for; matrix products, arithmetic and copies ran while one was open for 4% of the time, Pallas kernels for 0%

commit v1 on v0

--- a/solution.py
+++ b/solution.py
@@ -9,37 +9,20 @@
     return lax.ppermute(x, axis, [(i, (i + by) % devices) for i in range(devices)])
 
 
-def forward_tiles(total, source, tile_vals, tile_row, tile_col, live, tile_size):
-
-    def forward_one_tile(position, total):
-        row_start = tile_row[position] * tile_size
-        col_start = tile_col[position] * tile_size
-        source_rows = lax.dynamic_slice_in_dim(source, col_start, tile_size, 0)
-        current = lax.dynamic_slice_in_dim(total, row_start, tile_size, 0)
-        current = current + jnp.dot(
-            tile_vals[position], source_rows, preferred_element_type=jnp.float32
-        )
-        return lax.dynamic_update_slice_in_dim(total, current, row_start, 0)
-
-    return lax.fori_loop(0, live, forward_one_tile, total)
-
-
-def backward_tiles(total, grad_block, tile_vals, tile_row, tile_col, live, tile_size):
-
-    def backward_one_tile(position, total):
-        row_start = tile_row[position] * tile_size
-        col_start = tile_col[position] * tile_size
-        grad_rows = lax.dynamic_slice_in_dim(grad_block, row_start, tile_size, 0)
-        term = lax.dot_general(
-            tile_vals[position],
-            grad_rows,
-            (((0,), (0,)), ((), ())),
-            preferred_element_type=jnp.float32,
-        )
-        current = lax.dynamic_slice_in_dim(total, col_start, tile_size, 0)
-        return lax.dynamic_update_slice_in_dim(total, current + term, col_start, 0)
-
-    return lax.fori_loop(0, live, backward_one_tile, total)
+def dense_adjacency(tile_vals, tile_row, tile_col, live, tiles_per_part):
+    entries, tile_size, _ = tile_vals.shape
+    cells = tiles_per_part * tiles_per_part
+    cell_of_entry = tile_row * tiles_per_part + tile_col
+    alive = jnp.arange(entries) < live
+    select = (cell_of_entry[None, :] == jnp.arange(cells)[:, None]) & alive[None, :]
+    placed = jnp.dot(
+        select.astype(tile_vals.dtype),
+        tile_vals.reshape(entries, tile_size * tile_size),
+        preferred_element_type=jnp.float32,
+    ).astype(tile_vals.dtype)
+    placed = placed.reshape(tiles_per_part, tiles_per_part, tile_size, tile_size)
+    side = tiles_per_part * tile_size
+    return placed.transpose(0, 2, 1, 3).reshape(side, side)
 
 
 def activation(pre_act, cotangent):
@@ -66,16 +49,17 @@
     for level in range(digit_count):
         shifted = passed_along(feature_block, "blk", 1 << level)
         feature_block = jnp.where(rep_index // (1 << level) % 2 == 1, shifted, feature_block)
+    tiles_per_part = feature_block.shape[0] // tile_size
+    adjacency = [
+        dense_adjacency(
+            values_here[slot], rows_here[slot], cols_here[slot], counts_here[slot], tiles_per_part
+        )
+        for slot in range(pair_slots)
+    ]
     aggregate = jnp.zeros(feature_block.shape, jnp.float32)
     for slot in range(pair_slots):
-        aggregate = forward_tiles(
-            aggregate,
-            feature_block,
-            values_here[slot],
-            rows_here[slot],
-            cols_here[slot],
-            counts_here[slot],
-            tile_size,
+        aggregate = aggregate + jnp.dot(
+            adjacency[slot], feature_block, preferred_element_type=jnp.float32
         )
         if slot + 1 < pair_slots:
             feature_block = passed_along(feature_block, "blk", replicas)
@@ -86,14 +70,11 @@
     grad_block = lax.all_gather(grad_rows, "rep", axis=0, tiled=True)
     partial_grad = jnp.zeros(grad_block.shape, jnp.float32)
     for slot in reversed(range(pair_slots)):
-        partial_grad = backward_tiles(
-            partial_grad,
+        partial_grad = partial_grad + lax.dot_general(
+            adjacency[slot],
             grad_block,
-            values_here[slot],
-            rows_here[slot],
-            cols_here[slot],
-            counts_here[slot],
-            tile_size,
+            (((0,), (0,)), ((), ())),
+            preferred_element_type=jnp.float32,
         )
         if slot > 0:
             partial_grad = passed_along(partial_grad.astype(jnp.bfloat16), "blk", -replicas).astype(

time: 2000 us -> 1050 us (0.53)
  loops' own time: 326 us -> 0 us
  local copies, waits for them, and re-layouts: 202 us -> 5.86 us
  matrix products: 175 us -> 12.9 us
  starting transfers between devices: 228 us -> 89.6 us
  waiting for transfers between devices: 881 us -> 778 us
    another operation x4 -> x0, loops' own time: 326 us -> none  [the longest x2 163 us: forward_tiles(): return lax.fori_loop(0, live, forward_one_tile, total)]
    dynamic_slice x332 -> x0, local copies, waits for them, and re-layouts: 195 us -> none  [the longest x83 48.9 us: backward_one_tile(): col_start = tile_col[position] * tile_size]
    reduce_scatter x1, waiting for transfers between devices: 280 us -> 108 us  [body(): lax.psum_scatter(aggregate.astype(jnp.bfloat16), 'rep', scatter_dimension...]
    dot_general x166 -> x6, matrix products: 171 us -> 8.76 us  [the longest x2 3.4 us: dense_adjacency(): jnp.dot(select.astype(tile_vals.dtype), tile_vals.reshape(entries, tile_s...]
    ppermute x10, starting transfers between devices: 228 us -> 89.5 us  [passed_along(): lax.ppermute(x, axis, [(i, (i + by) % devices) for i in range(devices)])]
    ppermute x10, waiting for transfers between devices: 154 us -> 221 us  [passed_along(): lax.ppermute(x, axis, [(i, (i + by) % devices) for i in range(devices)])]
  transfers between devices with their start and end apart: 13 -> 13, of which waited for: 11 -> 12; matrix products, arithmetic and copies ran while one was open for 4% -> 1% of each run, Pallas kernels for 0% -> 0%
where the time goes in v1:
time: 1050 us
  waiting for transfers between devices  778 us (74%)
  blocking collectives  143 us (14%)
  starting transfers between devices  89.6 us (9%)
  between operations  14.1 us (1%)
  matrix products  12.9 us (1%)
    psum x1, waiting for transfers between devices, body(): lax.psum((weight_terms, bias_terms), ('blk', 'rep'))  449 us
    ppermute x10, waiting for transfers between devices, passed_along(): lax.ppermute(x, axis, [(i, (i + by) % devices) for i in range(devices)])  221 us
    reduce_scatter x1, waiting for transfers between devices, body(): lax.psum_scatter(aggregate.astype(jnp.bfloat16), 'rep', scatter_dimension...  108 us
    psum x1, blocking collectives, body(): lax.psum((weight_terms, bias_terms), ('blk', 'rep'))  99.8 us
    ppermute x10, starting transfers between devices, passed_along(): lax.ppermute(x, axis, [(i, (i + by) % devices) for i in range(devices)])  89.5 us
    all_gather x1, blocking collectives, body(): feature_block = lax.all_gather(hw_slice, 'rep', axis=0, tiled=True)  22.8 us
  transfers between devices with their start and end apart: 13, of which 12 were waited for; matrix products, arithmetic and copies ran while one was open for 1% of the time, Pallas kernels for 0%

profile of v1, /device:TPU:6, one launch (start us, length us, event | category | flops | bytes accessed | tf_op | source)
XLA Modules:
  0.0 1048.1 jit_solution(11181954026101608006)
XLA Ops:
  9.0 22.8 %all_gather.6 = bf16[1024,256]{1,0:T(8,128)(2,1)S(1)} all-gather(bf16[64,256]{1,0:T(8,128)(2,1)S(1)} %convolution_convert_fusion.3), channel_id=1, replica_groups=mesh['blk'=32,'rep'=16] {'rep'}, dimensions={0}, use_global_device_ids=true | all-gather | bytes 557056 | tf_op jit(solution)/shard_map/all_gather | solution.py:48
  31.8 2.4 collective-permute-start
  34.2 21.3 %collective-permute-done = bf16[1024,256]{1,0:T(8,128)(2,1)S(1)} collective-permute-done((bf16[1024,256]{1,0:T(8,128)(2,1)S(1)}, bf16[1024,256]{1,0:T(8,128)(2,1)S(1)}, u32[]{:S(2)}, u32[]{:S(2)}) %collective-permute-start) | collective-permute-done | bytes 524320 | tf_op jit(solution)/shard_map/ppermute | solution.py:9
  55.6 1.9 collective-permute-start.1
  57.6 14.7 %collective-permute-done.1 = bf16[1024,256]{1,0:T(8,128)(2,1)S(1)} collective-permute-done((bf16[1024,256]{1,0:T(8,128)(2,1)S(1)}, bf16[1024,256]{1,0:T(8,128)(2,1)S(1)}, u32[]{:S(2)}, u32[]{:S(2)}) %collective-permute-start.1) | collective-permute-done | bytes 524320 | tf_op jit(solution)/shard_map/ppermute | solution.py:9
  72.4 1.9 collective-permute-start.2
  74.4 25.0 %collective-permute-done.2 = bf16[1024,256]{1,0:T(8,128)(2,1)S(1)} collective-permute-done((bf16[1024,256]{1,0:T(8,128)(2,1)S(1)}, bf16[1024,256]{1,0:T(8,128)(2,1)S(1)}, u32[]{:S(2)}, u32[]{:S(2)}) %collective-permute-start.2) | collective-permute-done | bytes 524320 | tf_op jit(solution)/shard_map/ppermute | solution.py:9
  99.5 3.1 collective-permute-start.3
  103.9 2.7 fusion.36
  106.6 40.9 %collective-permute-done.3 = bf16[1024,256]{1,0:T(8,128)(2,1)S(1)} collective-permute-done((bf16[1024,256]{1,0:T(8,128)(2,1)S(1)}, bf16[1024,256]{1,0:T(8,128)(2,1)S(1)}, u32[]{:S(2)}, u32[]{:S(2)}) %collective-permute-start.3) | collective-permute-done | bytes 524320 | tf_op jit(solution)/shard_map/ppermute | solution.py:9
  147.5 4.8 collective-permute-start.4
  152.4 1.7 convolution_convert_fusion.1
  154.7 1.7 convolution_convert_fusion
  156.4 28.3 %collective-permute-done.4 = bf16[1024,256]{1,0:T(8,128)(2,1)S(1)} collective-permute-done((bf16[1024,256]{1,0:T(8,128)(2,1)S(1)}, bf16[1024,256]{1,0:T(8,128)(2,1)S(1)}, u32[]{:S(2)}, u32[]{:S(2)}) %collective-permute-start.4) | collective-permute-done | bytes 524320 | tf_op jit(solution)/shard_map/ppermute | solution.py:9
  185.5 1.5 fusion.22
  187.1 107.5 %reduce-scatter.3.cloned.1.call-done = bf16[64,256]{1,0:T(8,128)(2,1)} async-done(((bf16[1024,256]{1,0:T(8,128)(2,1)}), bf16[64,256]{1,0:T(8,128)(2,1)}) %reduce-scatter.3.cloned.1.call-update) | async-done | bytes 32784 | tf_op jit(solution)/shard_map/reduce_scatter | solution.py:66
  296.0 20.5 %all_gather.7 = bf16[1024,256]{1,0:T(8,128)(2,1)S(1)} all-gather(bf16[64,256]{1,0:T(8,128)(2,1)S(1)} %get-tuple-element.9), channel_id=1, replica_groups=mesh['blk'=32,'rep'=16] {'rep'}, dimensions={0}, use_global_device_ids=true | all-gather | bytes 557056 | tf_op jit(solution)/shard_map/all_gather | solution.py:70
  316.5 2.4 fusion.19
  318.9 12.8 %collective-permute-start.5 = (bf16[1024,256]{1,0:T(8,128)(2,1)S(1)}, bf16[1024,256]{1,0:T(8,128)(2,1)S(1)}, u32[]{:S(2)}, u32[]{:S(2)}) collective-permute-start(bf16[1024,256]{1,0:T(8,128)(2,1)S(1)} %fusion.19), channel_id=1, source_target_pairs={{0,256},{16,272},{32,288},{48,304},{64,320},{80,336},{96,352},{112... | collective-permute-start | bytes 1572872 | tf_op jit(solution)/shard_map/ppermute | solution.py:9
  331.7 25.6 %collective-permute-done.5 = bf16[1024,256]{1,0:T(8,128)(2,1)S(1)} collective-permute-done((bf16[1024,256]{1,0:T(8,128)(2,1)S(1)}, bf16[1024,256]{1,0:T(8,128)(2,1)S(1)}, u32[]{:S(2)}, u32[]{:S(2)}) %collective-permute-start.5) | collective-permute-done | bytes 524320 | tf_op jit(solution)/shard_map/ppermute | solution.py:9
  358.1 16.8 %collective-permute-start.6 = (bf16[1024,256]{1,0:T(8,128)(2,1)S(1)}, bf16[1024,256]{1,0:T(8,128)(2,1)S(1)}, u32[]{:S(2)}, u32[]{:S(2)}) collective-permute-start(bf16[1024,256]{1,0:T(8,128)(2,1)S(1)} %get-tuple-element.17), channel_id=1, source_target_pairs={{0,384},{16,400},{32,416},{48,432},{64,448},{80,464},{96,480},{112... | collective-permute-start | bytes 1572872 | tf_op jit(solution)/shard_map/ppermute | solution.py:9
  374.9 17.4 %collective-permute-done.6 = bf16[1024,256]{1,0:T(8,128)(2,1)S(1)} collective-permute-done((bf16[1024,256]{1,0:T(8,128)(2,1)S(1)}, bf16[1024,256]{1,0:T(8,128)(2,1)S(1)}, u32[]{:S(2)}, u32[]{:S(2)}) %collective-permute-start.6) | collective-permute-done | bytes 524320 | tf_op jit(solution)/shard_map/ppermute | solution.py:9
  392.5 28.6 %collective-permute-start.7 = (bf16[1024,256]{1,0:T(8,128)(2,1)S(1)}, bf16[1024,256]{1,0:T(8,128)(2,1)S(1)}, u32[]{:S(2)}, u32[]{:S(2)}) collective-permute-start(bf16[1024,256]{1,0:T(8,128)(2,1)S(1)} %convert_select_fusion.2), channel_id=1, source_target_pairs={{0,448},{16,464},{32,480},{48,496},{64,0},{80,16},{96,32},{112,48}... | collective-permute-start | bytes 1572872 | tf_op jit(solution)/shard_map/ppermute | solution.py:9
  421.1 20.1 %collective-permute-done.7 = bf16[1024,256]{1,0:T(8,128)(2,1)S(1)} collective-permute-done((bf16[1024,256]{1,0:T(8,128)(2,1)S(1)}, bf16[1024,256]{1,0:T(8,128)(2,1)S(1)}, u32[]{:S(2)}, u32[]{:S(2)}) %collective-permute-start.7) | collective-permute-done | bytes 524320 | tf_op jit(solution)/shard_map/ppermute | solution.py:9
  441.3 15.1 %collective-permute-start.8 = (bf16[1024,256]{1,0:T(8,128)(2,1)S(1)}, bf16[1024,256]{1,0:T(8,128)(2,1)S(1)}, u32[]{:S(2)}, u32[]{:S(2)}) collective-permute-start(bf16[1024,256]{1,0:T(8,128)(2,1)S(1)} %fusion.26), channel_id=1, source_target_pairs={{0,480},{16,496},{32,0},{48,16},{64,32},{80,48},{96,64},{112,80},{... | collective-permute-start | bytes 1572872 | tf_op jit(solution)/shard_map/ppermute | solution.py:9
  456.4 15.0 %collective-permute-done.8 = bf16[1024,256]{1,0:T(8,128)(2,1)S(1)} collective-permute-done((bf16[1024,256]{1,0:T(8,128)(2,1)S(1)}, bf16[1024,256]{1,0:T(8,128)(2,1)S(1)}, u32[]{:S(2)}, u32[]{:S(2)}) %collective-permute-start.8) | collective-permute-done | bytes 524320 | tf_op jit(solution)/shard_map/ppermute | solution.py:9
  471.6 2.1 collective-permute-start.9
  473.7 12.5 %collective-permute-done.9 = bf16[1024,256]{1,0:T(8,128)(2,1)S(1)} collective-permute-done((bf16[1024,256]{1,0:T(8,128)(2,1)S(1)}, bf16[1024,256]{1,0:T(8,128)(2,1)S(1)}, u32[]{:S(2)}, u32[]{:S(2)}) %collective-permute-start.9) | collective-permute-done | bytes 524320 | tf_op jit(solution)/shard_map/ppermute | solution.py:9
  487.4 99.8 %psum.15 = f32[256]{0:T(256)} all-reduce(f32[256]{0:T(256)S(1)} %get-tuple-element.8), channel_id=1, replica_groups=mesh['blk'=32,'rep'=16] {'blk','rep'}, use_global_device_ids=true, to_apply=%region_4.5 | all-reduce | flops 256 | bytes 2048 | tf_op jit(solution)/shard_map/psum | solution.py:99
  587.2 1.7 convolution_bitcast_fusion
  588.9 1.6 convolution_convert_fusion.2
  590.4 449.4 %all-reduce.2.cloned.1.call-done = f32[256,256]{0,1:T(8,128)} async-done(((f32[256,256]{0,1:T(8,128)}), f32[256,256]{0,1:T(8,128)}) %all-reduce.2.cloned.1.call-update) | async-done | bytes 262160 | tf_op jit(solution)/shard_map/psum | solution.py:99
  (41 shorter events, 10.2 us)
Async XLA Ops:
  7.2 0.9 copy-start
  7.2 67.2 %copy-start.6 = (s32[1,1,2,64]{3,2,1,0:T(2,128)S(1)}, s32[1,1,2,64]{3,2,1,0:T(2,128)}, u32[]{:S(2)}) copy-start(s32[1,1,2,64]{3,2,1,0:T(2,128)} %param.14) | copy-start | bytes 1540
  7.2 67.2 %copy-start.7 = (s32[1,1,2,64]{3,2,1,0:T(2,128)S(1)}, s32[1,1,2,64]{3,2,1,0:T(2,128)}, u32[]{:S(2)}) copy-start(s32[1,1,2,64]{3,2,1,0:T(2,128)} %param.13) | copy-start | bytes 1540
  7.2 287.4 %reduce-scatter.3.cloned.1.call-start = ((), (), s32[]{:S(2)}) async-start(), calls=%async_computation.2 | async-start | bytes 557056 | tf_op jit(solution)/shard_map/reduce_scatter | solution.py:66
  31.8 23.7 %collective-permute-start = (bf16[1024,256]{1,0:T(8,128)(2,1)S(1)}, bf16[1024,256]{1,0:T(8,128)(2,1)S(1)}, u32[]{:S(2)}, u32[]{:S(2)}) collective-permute-start(bf16[1024,256]{1,0:T(8,128)(2,1)S(1)} %all_gather.6), channel_id=1, source_target_pairs={{0,16},{16,32},{32,48},{48,64},{64,80},{80,96},{96,112},{112,128},... | collective-permute-start | bytes 1572872 | tf_op jit(solution)/shard_map/ppermute | solution.py:9
  34.2 68.4 %copy-start.4 = (s32[1,1,2]{2,1,0:T(1,128)S(1)}, s32[1,1,2]{2,1,0:T(1,128)}, u32[]{:S(2)}) copy-start(s32[1,1,2]{2,1,0:T(1,128)} %param.15) | copy-start | bytes 28
  55.6 16.7 %collective-permute-start.1 = (bf16[1024,256]{1,0:T(8,128)(2,1)S(1)}, bf16[1024,256]{1,0:T(8,128)(2,1)S(1)}, u32[]{:S(2)}, u32[]{:S(2)}) collective-permute-start(bf16[1024,256]{1,0:T(8,128)(2,1)S(1)} %broadcast_select_fusion), channel_id=1, source_target_pairs={{0,32},{16,48},{32,64},{48,80},{64,96},{80,112},{96,128},{112,144}... | collective-permute-start | bytes 1572872 | tf_op jit(solution)/shard_map/ppermute | solution.py:9
  72.4 27.0 %collective-permute-start.2 = (bf16[1024,256]{1,0:T(8,128)(2,1)S(1)}, bf16[1024,256]{1,0:T(8,128)(2,1)S(1)}, u32[]{:S(2)}, u32[]{:S(2)}) collective-permute-start(bf16[1024,256]{1,0:T(8,128)(2,1)S(1)} %broadcast_select_fusion.1), channel_id=1, source_target_pairs={{0,64},{16,80},{32,96},{48,112},{64,128},{80,144},{96,160},{112,17... | collective-permute-start | bytes 1572872 | tf_op jit(solution)/shard_map/ppermute | solution.py:9
  99.5 48.0 %collective-permute-start.3 = (bf16[1024,256]{1,0:T(8,128)(2,1)S(1)}, bf16[1024,256]{1,0:T(8,128)(2,1)S(1)}, u32[]{:S(2)}, u32[]{:S(2)}) collective-permute-start(bf16[1024,256]{1,0:T(8,128)(2,1)S(1)} %broadcast_select_fusion.2), channel_id=1, source_target_pairs={{0,128},{16,144},{32,160},{48,176},{64,192},{80,208},{96,224},{112... | collective-permute-start | bytes 1572872 | tf_op jit(solution)/shard_map/ppermute | solution.py:9
  147.5 37.2 %collective-permute-start.4 = (bf16[1024,256]{1,0:T(8,128)(2,1)S(1)}, bf16[1024,256]{1,0:T(8,128)(2,1)S(1)}, u32[]{:S(2)}, u32[]{:S(2)}) collective-permute-start(bf16[1024,256]{1,0:T(8,128)(2,1)S(1)} %broadcast_select_fusion.3), channel_id=1, source_target_pairs={{0,256},{16,272},{32,288},{48,304},{64,320},{80,336},{96,352},{112... | collective-permute-start | bytes 1572872 | tf_op jit(solution)/shard_map/ppermute | solution.py:9
  156.4 29.1 %copy-start.1 = (bf16[64,16384]{1,0:T(8,128)(2,1)}, bf16[64,16384]{1,0:T(8,128)(2,1)S(1)}, u32[]{:S(2)}) copy-start(bf16[64,16384]{1,0:T(8,128)(2,1)S(1)} %convolution_convert_fusion) | copy-start | bytes 6291460
  185.5 109.1 %copy-start.3 = (bf16[64,256]{1,0:T(8,128)(2,1)S(1)}, bf16[64,256]{1,0:T(8,128)(2,1)}, u32[]{:S(2)}) copy-start(bf16[64,256]{1,0:T(8,128)(2,1)} %param.11) | copy-start | bytes 98308
  185.5 109.1 %copy-start.5 = (f32[256]{0:T(256)S(1)}, f32[256]{0:T(256)}, u32[]{:S(2)}) copy-start(f32[256]{0:T(256)} %param.10) | copy-start | bytes 3076
  187.0 400.1 %reduce-scatter.5.cloned.1.call-start = ((), (), s32[]{:S(2)}) async-start(), calls=%async_computation.3 | async-start | bytes 557056 | tf_op jit(solution)/shard_map/reduce_scatter | solution.py:88
  318.9 38.4 %collective-permute-start.5 = (bf16[1024,256]{1,0:T(8,128)(2,1)S(1)}, bf16[1024,256]{1,0:T(8,128)(2,1)S(1)}, u32[]{:S(2)}, u32[]{:S(2)}) collective-permute-start(bf16[1024,256]{1,0:T(8,128)(2,1)S(1)} %fusion.19), channel_id=1, source_target_pairs={{0,256},{16,272},{32,288},{48,304},{64,320},{80,336},{96,352},{112... | collective-permute-start | bytes 1572872 | tf_op jit(solution)/shard_map/ppermute | solution.py:9
  358.1 34.2 %collective-permute-start.6 = (bf16[1024,256]{1,0:T(8,128)(2,1)S(1)}, bf16[1024,256]{1,0:T(8,128)(2,1)S(1)}, u32[]{:S(2)}, u32[]{:S(2)}) collective-permute-start(bf16[1024,256]{1,0:T(8,128)(2,1)S(1)} %get-tuple-element.17), channel_id=1, source_target_pairs={{0,384},{16,400},{32,416},{48,432},{64,448},{80,464},{96,480},{112... | collective-permute-start | bytes 1572872 | tf_op jit(solution)/shard_map/ppermute | solution.py:9
  392.5 48.7 %collective-permute-start.7 = (bf16[1024,256]{1,0:T(8,128)(2,1)S(1)}, bf16[1024,256]{1,0:T(8,128)(2,1)S(1)}, u32[]{:S(2)}, u32[]{:S(2)}) collective-permute-start(bf16[1024,256]{1,0:T(8,128)(2,1)S(1)} %convert_select_fusion.2), channel_id=1, source_target_pairs={{0,448},{16,464},{32,480},{48,496},{64,0},{80,16},{96,32},{112,48}... | collective-permute-start | bytes 1572872 | tf_op jit(solution)/shard_map/ppermute | solution.py:9
  441.3 30.1 %collective-permute-start.8 = (bf16[1024,256]{1,0:T(8,128)(2,1)S(1)}, bf16[1024,256]{1,0:T(8,128)(2,1)S(1)}, u32[]{:S(2)}, u32[]{:S(2)}) collective-permute-start(bf16[1024,256]{1,0:T(8,128)(2,1)S(1)} %fusion.26), channel_id=1, source_target_pairs={{0,480},{16,496},{32,0},{48,16},{64,32},{80,48},{96,64},{112,80},{... | collective-permute-start | bytes 1572872 | tf_op jit(solution)/shard_map/ppermute | solution.py:9
  471.6 115.6 %copy-start.2 = (bf16[64,256]{1,0:T(8,128)(2,1)S(1)}, bf16[64,256]{1,0:T(8,128)(2,1)}, u32[]{:S(2)}) copy-start(bf16[64,256]{1,0:T(8,128)(2,1)} %param.8) | copy-start | bytes 98308
  471.6 14.6 %collective-permute-start.9 = (bf16[1024,256]{1,0:T(8,128)(2,1)S(1)}, bf16[1024,256]{1,0:T(8,128)(2,1)S(1)}, u32[]{:S(2)}, u32[]{:S(2)}) collective-permute-start(bf16[1024,256]{1,0:T(8,128)(2,1)S(1)} %fusion.27), channel_id=1, source_target_pairs={{0,496},{16,0},{32,16},{48,32},{64,48},{80,64},{96,80},{112,96},{1... | collective-permute-start | bytes 1572872 | tf_op jit(solution)/shard_map/ppermute | solution.py:9
  487.3 552.5 %all-reduce.2.cloned.1.call-start = ((), (), s32[]{:S(2)}) async-start(), calls=%async_computation.4 | async-start | bytes 524288 | tf_op jit(solution)/shard_map/psum | solution.py:99
Sparse Core Ops, SparseCore 0:
  187.2 107.3 reduce-scatter.2
  487.4 81.3 reduce-scatter.4
  589.0 450.8 all-reduce.1

commit v2 on v1

--- a/solution.py
+++ b/solution.py
@@ -94,10 +94,11 @@
     weight_terms = lax.dot_general(
         feats, grad_hw, (((0,), (0,)), ((), ())), preferred_element_type=jnp.float32
     )
-    weight_rows = weight.shape[0] // replicas
-    bias_terms = jnp.sum(grad_rows.astype(jnp.float32), axis=0)
-    weight_total, grad_bias = lax.psum((weight_terms, bias_terms), ("blk", "rep"))
-    grad_weight = lax.dynamic_slice_in_dim(weight_total, rep_index * weight_rows, weight_rows, 0)
+    weight_part = lax.psum_scatter(weight_terms, "rep", scatter_dimension=0, tiled=True)
+    bias_part = jnp.sum(grad_block.astype(jnp.float32), axis=0)
+    totals = lax.psum(jnp.concatenate([weight_part, bias_part[None, :]], axis=0), "blk")
+    grad_weight = totals[:-1]
+    grad_bias = totals[-1]
     return (out, grad_feats, grad_weight, grad_bias)
 
 

time: 1050 us -> 793 us (0.76)
  waiting for transfers between devices: 778 us -> 498 us
  blocking collectives: 143 us -> 166 us
    psum x1 -> x0, waiting for transfers between devices: 449 us -> none  [body(): lax.psum((weight_terms, bias_terms), ('blk', 'rep'))]
    reduce_scatter x0 -> x1, waiting for transfers between devices: none -> 88.4 us  [body(): lax.psum_scatter(weight_terms, 'rep', scatter_dimension=0, tiled=True)]
    reduce_scatter x1, waiting for transfers between devices: 0.01 us -> 84 us  [body(): lax.psum_scatter(partial_grad.astype(jnp.bfloat16), 'rep', scatter_dimens...]
    psum x1, blocking collectives: 99.8 us -> 122 us  [body(): lax.psum(jnp.concatenate([weight_part, bias_part[None, :]], axis=0), 'blk')]
  transfers between devices with their start and end apart: 13 -> 13, of which waited for: 12 -> 13; matrix products, arithmetic and copies ran while one was open for 1% -> 1% of each run, Pallas kernels for 0% -> 0%
where the time goes in v2:
time: 793 us; the launch traced here: 792 us
  waiting for transfers between devices  498 us (63%)
  blocking collectives  166 us (21%)
  starting transfers between devices  90 us (11%)
  between operations  14.1 us (2%)
  matrix products  12.2 us (2%)
    ppermute x10, waiting for transfers between devices, passed_along(): lax.ppermute(x, axis, [(i, (i + by) % devices) for i in range(devices)])  218 us
    psum x1, blocking collectives, body(): lax.psum(jnp.concatenate([weight_part, bias_part[None, :]], axis=0), 'blk')  122 us
    reduce_scatter x1, waiting for transfers between devices, body(): lax.psum_scatter(aggregate.astype(jnp.bfloat16), 'rep', scatter_dimension...  108 us
    ppermute x10, starting transfers between devices, passed_along(): lax.ppermute(x, axis, [(i, (i + by) % devices) for i in range(devices)])  89.9 us
    reduce_scatter x1, waiting for transfers between devices, body(): lax.psum_scatter(weight_terms, 'rep', scatter_dimension=0, tiled=True)  88.4 us
    reduce_scatter x1, waiting for transfers between devices, body(): lax.psum_scatter(partial_grad.astype(jnp.bfloat16), 'rep', scatter_dimens...  84 us
    all_gather x1, blocking collectives, body(): feature_block = lax.all_gather(hw_slice, 'rep', axis=0, tiled=True)  22.8 us
    all_gather x1, blocking collectives, body(): grad_block = lax.all_gather(grad_rows, 'rep', axis=0, tiled=True)  20.5 us
  transfers between devices with their start and end apart: 13, of which 13 were waited for; matrix products, arithmetic and copies ran while one was open for 1% of the time, Pallas kernels for 0%

profile of v2, /device:TPU:6, one launch (start us, length us, event | category | flops | bytes accessed | tf_op | source)
XLA Modules:
  0.0 791.5 jit_solution(4068678257483347519)
XLA Ops:
  9.0 22.8 %all_gather.6 = bf16[1024,256]{1,0:T(8,128)(2,1)S(1)} all-gather(bf16[64,256]{1,0:T(8,128)(2,1)S(1)} %convolution_convert_fusion.3), channel_id=1, replica_groups=mesh['blk'=32,'rep'=16] {'rep'}, dimensions={0}, use_global_device_ids=true | all-gather | bytes 557056 | tf_op jit(solution)/shard_map/all_gather | solution.py:48
  31.8 2.4 collective-permute-start
  34.2 21.3 %collective-permute-done = bf16[1024,256]{1,0:T(8,128)(2,1)S(1)} collective-permute-done((bf16[1024,256]{1,0:T(8,128)(2,1)S(1)}, bf16[1024,256]{1,0:T(8,128)(2,1)S(1)}, u32[]{:S(2)}, u32[]{:S(2)}) %collective-permute-start) | collective-permute-done | bytes 524320 | tf_op jit(solution)/shard_map/ppermute | solution.py:9
  55.6 1.9 collective-permute-start.1
  57.6 14.7 %collective-permute-done.1 = bf16[1024,256]{1,0:T(8,128)(2,1)S(1)} collective-permute-done((bf16[1024,256]{1,0:T(8,128)(2,1)S(1)}, bf16[1024,256]{1,0:T(8,128)(2,1)S(1)}, u32[]{:S(2)}, u32[]{:S(2)}) %collective-permute-start.1) | collective-permute-done | bytes 524320 | tf_op jit(solution)/shard_map/ppermute | solution.py:9
  72.4 1.9 collective-permute-start.2
  74.4 25.0 %collective-permute-done.2 = bf16[1024,256]{1,0:T(8,128)(2,1)S(1)} collective-permute-done((bf16[1024,256]{1,0:T(8,128)(2,1)S(1)}, bf16[1024,256]{1,0:T(8,128)(2,1)S(1)}, u32[]{:S(2)}, u32[]{:S(2)}) %collective-permute-start.2) | collective-permute-done | bytes 524320 | tf_op jit(solution)/shard_map/ppermute | solution.py:9
  99.5 3.1 collective-permute-start.3
  103.9 2.7 fusion.36
  106.6 40.9 %collective-permute-done.3 = bf16[1024,256]{1,0:T(8,128)(2,1)S(1)} collective-permute-done((bf16[1024,256]{1,0:T(8,128)(2,1)S(1)}, bf16[1024,256]{1,0:T(8,128)(2,1)S(1)}, u32[]{:S(2)}, u32[]{:S(2)}) %collective-permute-start.3) | collective-permute-done | bytes 524320 | tf_op jit(solution)/shard_map/ppermute | solution.py:9
  147.5 4.8 collective-permute-start.4
  152.4 1.7 convolution_convert_fusion.1
  154.7 1.7 convolution_convert_fusion
  156.4 28.3 %collective-permute-done.4 = bf16[1024,256]{1,0:T(8,128)(2,1)S(1)} collective-permute-done((bf16[1024,256]{1,0:T(8,128)(2,1)S(1)}, bf16[1024,256]{1,0:T(8,128)(2,1)S(1)}, u32[]{:S(2)}, u32[]{:S(2)}) %collective-permute-start.4) | collective-permute-done | bytes 524320 | tf_op jit(solution)/shard_map/ppermute | solution.py:9
  185.5 1.5 fusion.22
  187.1 107.5 %reduce-scatter.6.cloned.1.call-done = bf16[64,256]{1,0:T(8,128)(2,1)} async-done(((bf16[1024,256]{1,0:T(8,128)(2,1)}), bf16[64,256]{1,0:T(8,128)(2,1)}) %reduce-scatter.6.cloned.1.call-update) | async-done | bytes 32784 | tf_op jit(solution)/shard_map/reduce_scatter | solution.py:66
  296.0 20.5 %all_gather.7 = bf16[1024,256]{1,0:T(8,128)(2,1)S(1)} all-gather(bf16[64,256]{1,0:T(8,128)(2,1)S(1)} %get-tuple-element.14), channel_id=1, replica_groups=mesh['blk'=32,'rep'=16] {'rep'}, dimensions={0}, use_global_device_ids=true | all-gather | bytes 557056 | tf_op jit(solution)/shard_map/all_gather | solution.py:70
  316.5 2.4 fusion.19
  318.9 12.8 %collective-permute-start.5 = (bf16[1024,256]{1,0:T(8,128)(2,1)S(1)}, bf16[1024,256]{1,0:T(8,128)(2,1)S(1)}, u32[]{:S(2)}, u32[]{:S(2)}) collective-permute-start(bf16[1024,256]{1,0:T(8,128)(2,1)S(1)} %fusion.19), channel_id=1, source_target_pairs={{0,256},{16,272},{32,288},{48,304},{64,320},{80,336},{96,352},{112... | collective-permute-start | bytes 1572872 | tf_op jit(solution)/shard_map/ppermute | solution.py:9
  331.7 25.5 %collective-permute-done.5 = bf16[1024,256]{1,0:T(8,128)(2,1)S(1)} collective-permute-done((bf16[1024,256]{1,0:T(8,128)(2,1)S(1)}, bf16[1024,256]{1,0:T(8,128)(2,1)S(1)}, u32[]{:S(2)}, u32[]{:S(2)}) %collective-permute-start.5) | collective-permute-done | bytes 524320 | tf_op jit(solution)/shard_map/ppermute | solution.py:9
  357.9 16.7 %collective-permute-start.6 = (bf16[1024,256]{1,0:T(8,128)(2,1)S(1)}, bf16[1024,256]{1,0:T(8,128)(2,1)S(1)}, u32[]{:S(2)}, u32[]{:S(2)}) collective-permute-start(bf16[1024,256]{1,0:T(8,128)(2,1)S(1)} %get-tuple-element.20), channel_id=1, source_target_pairs={{0,384},{16,400},{32,416},{48,432},{64,448},{80,464},{96,480},{112... | collective-permute-start | bytes 1572872 | tf_op jit(solution)/shard_map/ppermute | solution.py:9
  374.7 17.4 %collective-permute-done.6 = bf16[1024,256]{1,0:T(8,128)(2,1)S(1)} collective-permute-done((bf16[1024,256]{1,0:T(8,128)(2,1)S(1)}, bf16[1024,256]{1,0:T(8,128)(2,1)S(1)}, u32[]{:S(2)}, u32[]{:S(2)}) %collective-permute-start.6) | collective-permute-done | bytes 524320 | tf_op jit(solution)/shard_map/ppermute | solution.py:9
  392.3 28.6 %collective-permute-start.7 = (bf16[1024,256]{1,0:T(8,128)(2,1)S(1)}, bf16[1024,256]{1,0:T(8,128)(2,1)S(1)}, u32[]{:S(2)}, u32[]{:S(2)}) collective-permute-start(bf16[1024,256]{1,0:T(8,128)(2,1)S(1)} %convert_select_fusion.2), channel_id=1, source_target_pairs={{0,448},{16,464},{32,480},{48,496},{64,0},{80,16},{96,32},{112,48}... | collective-permute-start | bytes 1572872 | tf_op jit(solution)/shard_map/ppermute | solution.py:9
  420.9 19.6 %collective-permute-done.7 = bf16[1024,256]{1,0:T(8,128)(2,1)S(1)} collective-permute-done((bf16[1024,256]{1,0:T(8,128)(2,1)S(1)}, bf16[1024,256]{1,0:T(8,128)(2,1)S(1)}, u32[]{:S(2)}, u32[]{:S(2)}) %collective-permute-start.7) | collective-permute-done | bytes 524320 | tf_op jit(solution)/shard_map/ppermute | solution.py:9
  440.7 15.7 %collective-permute-start.8 = (bf16[1024,256]{1,0:T(8,128)(2,1)S(1)}, bf16[1024,256]{1,0:T(8,128)(2,1)S(1)}, u32[]{:S(2)}, u32[]{:S(2)}) collective-permute-start(bf16[1024,256]{1,0:T(8,128)(2,1)S(1)} %fusion.26), channel_id=1, source_target_pairs={{0,480},{16,496},{32,0},{48,16},{64,32},{80,48},{96,64},{112,80},{... | collective-permute-start | bytes 1572872 | tf_op jit(solution)/shard_map/ppermute | solution.py:9
  456.4 11.9 %collective-permute-done.8 = bf16[1024,256]{1,0:T(8,128)(2,1)S(1)} collective-permute-done((bf16[1024,256]{1,0:T(8,128)(2,1)S(1)}, bf16[1024,256]{1,0:T(8,128)(2,1)S(1)}, u32[]{:S(2)}, u32[]{:S(2)}) %collective-permute-start.8) | collective-permute-done | bytes 524320 | tf_op jit(solution)/shard_map/ppermute | solution.py:9
  468.5 1.9 collective-permute-start.9
  470.4 13.3 %collective-permute-done.9 = bf16[1024,256]{1,0:T(8,128)(2,1)S(1)} collective-permute-done((bf16[1024,256]{1,0:T(8,128)(2,1)S(1)}, bf16[1024,256]{1,0:T(8,128)(2,1)S(1)}, u32[]{:S(2)}, u32[]{:S(2)}) %collective-permute-start.9) | collective-permute-done | bytes 524320 | tf_op jit(solution)/shard_map/ppermute | solution.py:9
  484.8 84.0 %reduce-scatter.8.cloned.1.call-done = bf16[64,256]{1,0:T(8,128)(2,1)} async-done(((bf16[1024,256]{1,0:T(8,128)(2,1)}), bf16[64,256]{1,0:T(8,128)(2,1)}) %reduce-scatter.8.cloned.1.call-update) | async-done | bytes 32784 | tf_op jit(solution)/shard_map/reduce_scatter | solution.py:88
  570.8 1.6 convolution_convert_fusion.2
  572.4 88.4 %reduce-scatter.10.cloned.1.call-done = f32[16,256]{1,0:T(8,128)} async-done(((f32[256,256]{1,0:T(8,128)}), f32[16,256]{1,0:T(8,128)}) %reduce-scatter.10.cloned.1.call-update) | async-done | bytes 16400 | tf_op jit(solution)/shard_map/reduce_scatter | solution.py:97
  661.4 122.4 %psum.7 = f32[17,256]{1,0:T(8,128)S(1)} all-reduce(f32[17,256]{1,0:T(8,128)S(1)} %pad_maximum_fusion), channel_id=1, replica_groups=mesh['blk'=32,'rep'=16] {'blk'}, use_global_device_ids=true, to_apply=%region_4.5 | all-reduce | flops 4352 | bytes 34816 | tf_op jit(solution)/shard_map/psum | solution.py:99
  (44 shorter events, 12.3 us)
Async XLA Ops:
  7.2 0.9 copy-start
  7.2 67.2 %copy-start.6 = (s32[1,1,2,64]{3,2,1,0:T(2,128)S(1)}, s32[1,1,2,64]{3,2,1,0:T(2,128)}, u32[]{:S(2)}) copy-start(s32[1,1,2,64]{3,2,1,0:T(2,128)} %param.14) | copy-start | bytes 1540
  7.2 67.2 %copy-start.7 = (s32[1,1,2,64]{3,2,1,0:T(2,128)S(1)}, s32[1,1,2,64]{3,2,1,0:T(2,128)}, u32[]{:S(2)}) copy-start(s32[1,1,2,64]{3,2,1,0:T(2,128)} %param.13) | copy-start | bytes 1540
  7.2 287.4 %reduce-scatter.6.cloned.1.call-start = ((), (), s32[]{:S(2)}) async-start(), calls=%async_computation.3 | async-start | bytes 557056 | tf_op jit(solution)/shard_map/reduce_scatter | solution.py:66
  31.8 23.7 %collective-permute-start = (bf16[1024,256]{1,0:T(8,128)(2,1)S(1)}, bf16[1024,256]{1,0:T(8,128)(2,1)S(1)}, u32[]{:S(2)}, u32[]{:S(2)}) collective-permute-start(bf16[1024,256]{1,0:T(8,128)(2,1)S(1)} %all_gather.6), channel_id=1, source_target_pairs={{0,16},{16,32},{32,48},{48,64},{64,80},{80,96},{96,112},{112,128},... | collective-permute-start | bytes 1572872 | tf_op jit(solution)/shard_map/ppermute | solution.py:9
  34.2 68.4 %copy-start.4 = (s32[1,1,2]{2,1,0:T(1,128)S(1)}, s32[1,1,2]{2,1,0:T(1,128)}, u32[]{:S(2)}) copy-start(s32[1,1,2]{2,1,0:T(1,128)} %param.15) | copy-start | bytes 28
  55.6 16.7 %collective-permute-start.1 = (bf16[1024,256]{1,0:T(8,128)(2,1)S(1)}, bf16[1024,256]{1,0:T(8,128)(2,1)S(1)}, u32[]{:S(2)}, u32[]{:S(2)}) collective-permute-start(bf16[1024,256]{1,0:T(8,128)(2,1)S(1)} %broadcast_select_fusion), channel_id=1, source_target_pairs={{0,32},{16,48},{32,64},{48,80},{64,96},{80,112},{96,128},{112,144}... | collective-permute-start | bytes 1572872 | tf_op jit(solution)/shard_map/ppermute | solution.py:9
  72.4 27.0 %collective-permute-start.2 = (bf16[1024,256]{1,0:T(8,128)(2,1)S(1)}, bf16[1024,256]{1,0:T(8,128)(2,1)S(1)}, u32[]{:S(2)}, u32[]{:S(2)}) collective-permute-start(bf16[1024,256]{1,0:T(8,128)(2,1)S(1)} %broadcast_select_fusion.1), channel_id=1, source_target_pairs={{0,64},{16,80},{32,96},{48,112},{64,128},{80,144},{96,160},{112,17... | collective-permute-start | bytes 1572872 | tf_op jit(solution)/shard_map/ppermute | solution.py:9
  99.5 48.0 %collective-permute-start.3 = (bf16[1024,256]{1,0:T(8,128)(2,1)S(1)}, bf16[1024,256]{1,0:T(8,128)(2,1)S(1)}, u32[]{:S(2)}, u32[]{:S(2)}) collective-permute-start(bf16[1024,256]{1,0:T(8,128)(2,1)S(1)} %broadcast_select_fusion.2), channel_id=1, source_target_pairs={{0,128},{16,144},{32,160},{48,176},{64,192},{80,208},{96,224},{112... | collective-permute-start | bytes 1572872 | tf_op jit(solution)/shard_map/ppermute | solution.py:9
  147.5 37.2 %collective-permute-start.4 = (bf16[1024,256]{1,0:T(8,128)(2,1)S(1)}, bf16[1024,256]{1,0:T(8,128)(2,1)S(1)}, u32[]{:S(2)}, u32[]{:S(2)}) collective-permute-start(bf16[1024,256]{1,0:T(8,128)(2,1)S(1)} %broadcast_select_fusion.3), channel_id=1, source_target_pairs={{0,256},{16,272},{32,288},{48,304},{64,320},{80,336},{96,352},{112... | collective-permute-start | bytes 1572872 | tf_op jit(solution)/shard_map/ppermute | solution.py:9
  156.4 29.1 %copy-start.1 = (bf16[64,16384]{1,0:T(8,128)(2,1)}, bf16[64,16384]{1,0:T(8,128)(2,1)S(1)}, u32[]{:S(2)}) copy-start(bf16[64,16384]{1,0:T(8,128)(2,1)S(1)} %convolution_convert_fusion) | copy-start | bytes 6291460
  185.5 109.1 %copy-start.3 = (bf16[64,256]{1,0:T(8,128)(2,1)S(1)}, bf16[64,256]{1,0:T(8,128)(2,1)}, u32[]{:S(2)}) copy-start(bf16[64,256]{1,0:T(8,128)(2,1)} %param.11) | copy-start | bytes 98308
  185.5 109.1 %copy-start.5 = (f32[256]{0:T(256)S(1)}, f32[256]{0:T(256)}, u32[]{:S(2)}) copy-start(f32[256]{0:T(256)} %param.10) | copy-start | bytes 3076
  187.0 381.8 %reduce-scatter.8.cloned.1.call-start = ((), (), s32[]{:S(2)}) async-start(), calls=%async_computation.4 | async-start | bytes 557056 | tf_op jit(solution)/shard_map/reduce_scatter | solution.py:88
  318.9 38.3 %collective-permute-start.5 = (bf16[1024,256]{1,0:T(8,128)(2,1)S(1)}, bf16[1024,256]{1,0:T(8,128)(2,1)S(1)}, u32[]{:S(2)}, u32[]{:S(2)}) collective-permute-start(bf16[1024,256]{1,0:T(8,128)(2,1)S(1)} %fusion.19), channel_id=1, source_target_pairs={{0,256},{16,272},{32,288},{48,304},{64,320},{80,336},{96,352},{112... | collective-permute-start | bytes 1572872 | tf_op jit(solution)/shard_map/ppermute | solution.py:9
  357.9 34.2 %collective-permute-start.6 = (bf16[1024,256]{1,0:T(8,128)(2,1)S(1)}, bf16[1024,256]{1,0:T(8,128)(2,1)S(1)}, u32[]{:S(2)}, u32[]{:S(2)}) collective-permute-start(bf16[1024,256]{1,0:T(8,128)(2,1)S(1)} %get-tuple-element.20), channel_id=1, source_target_pairs={{0,384},{16,400},{32,416},{48,432},{64,448},{80,464},{96,480},{112... | collective-permute-start | bytes 1572872 | tf_op jit(solution)/shard_map/ppermute | solution.py:9
  392.3 48.2 %collective-permute-start.7 = (bf16[1024,256]{1,0:T(8,128)(2,1)S(1)}, bf16[1024,256]{1,0:T(8,128)(2,1)S(1)}, u32[]{:S(2)}, u32[]{:S(2)}) collective-permute-start(bf16[1024,256]{1,0:T(8,128)(2,1)S(1)} %convert_select_fusion.2), channel_id=1, source_target_pairs={{0,448},{16,464},{32,480},{48,496},{64,0},{80,16},{96,32},{112,48}... | collective-permute-start | bytes 1572872 | tf_op jit(solution)/shard_map/ppermute | solution.py:9
  440.7 27.6 %collective-permute-start.8 = (bf16[1024,256]{1,0:T(8,128)(2,1)S(1)}, bf16[1024,256]{1,0:T(8,128)(2,1)S(1)}, u32[]{:S(2)}, u32[]{:S(2)}) collective-permute-start(bf16[1024,256]{1,0:T(8,128)(2,1)S(1)} %fusion.26), channel_id=1, source_target_pairs={{0,480},{16,496},{32,0},{48,16},{64,32},{80,48},{96,64},{112,80},{... | collective-permute-start | bytes 1572872 | tf_op jit(solution)/shard_map/ppermute | solution.py:9
  468.5 100.3 %copy-start.2 = (bf16[64,256]{1,0:T(8,128)(2,1)S(1)}, bf16[64,256]{1,0:T(8,128)(2,1)}, u32[]{:S(2)}) copy-start(bf16[64,256]{1,0:T(8,128)(2,1)} %param.8) | copy-start | bytes 98308
  468.5 15.2 %collective-permute-start.9 = (bf16[1024,256]{1,0:T(8,128)(2,1)S(1)}, bf16[1024,256]{1,0:T(8,128)(2,1)S(1)}, u32[]{:S(2)}, u32[]{:S(2)}) collective-permute-start(bf16[1024,256]{1,0:T(8,128)(2,1)S(1)} %fusion.27), channel_id=1, source_target_pairs={{0,496},{16,0},{32,16},{48,32},{64,48},{80,64},{96,80},{112,96},{1... | collective-permute-start | bytes 1572872 | tf_op jit(solution)/shard_map/ppermute | solution.py:9
  484.8 175.9 %reduce-scatter.10.cloned.1.call-start = ((), (), s32[]{:S(2)}) async-start(), calls=%async_computation.5 | async-start | bytes 278528 | tf_op jit(solution)/shard_map/reduce_scatter | solution.py:97
Sparse Core Ops, SparseCore 0:
  187.2 107.3 reduce-scatter.5
  484.9 83.8 reduce-scatter.7
  573.4 87.2 reduce-scatter.9

commit v3 on v2

v3 whole, which is shorter than its diff:
```python
import jax
import jax.numpy as jnp
from jax import lax
from jax.sharding import PartitionSpec as P


def dense_adjacency(tile_vals, tile_row, tile_col, live, tiles_per_part):
    entries, tile_size, _ = tile_vals.shape
    cells = tiles_per_part * tiles_per_part
    cell_of_entry = tile_row * tiles_per_part + tile_col
    alive = jnp.arange(entries) < live
    select = (cell_of_entry[None, :] == jnp.arange(cells)[:, None]) & alive[None, :]
    placed = jnp.dot(
        select.astype(tile_vals.dtype),
        tile_vals.reshape(entries, tile_size * tile_size),
        preferred_element_type=jnp.float32,
    ).astype(tile_vals.dtype)
    placed = placed.reshape(tiles_per_part, tiles_per_part, tile_size, tile_size)
    side = tiles_per_part * tile_size
    return placed.transpose(0, 2, 1, 3).reshape(side, side)


def rep_reduce_scatter(x, wire_dtype):
    replicas = lax.axis_size("rep")
    rep_index = lax.axis_index("rep")
    bit_count = (replicas - 1).bit_length()
    rows = x.shape[0] // replicas
    current = x.reshape((2,) * bit_count + (rows,) + x.shape[1:])
    remaining = list(reversed(range(bit_count)))
    order = [0] + list(range(2, bit_count)) + [1] if bit_count > 2 else list(range(bit_count))
    for bit in order:
        axis = remaining.index(bit)
        mine = (rep_index >> bit) & 1
        keep = lax.dynamic_index_in_dim(current, mine, axis, keepdims=False)
        send = lax.dynamic_index_in_dim(current, 1 - mine, axis, keepdims=False)
        partner = [(i, i ^ (1 << bit)) for i in range(replicas)]
        got = lax.ppermute(send.astype(wire_dtype), "rep", partner)
        current = keep + got.astype(jnp.float32)
        remaining.remove(bit)
    return current


def blk_all_reduce(x):
    blocks = lax.axis_size("blk")
    step = 1
    while step < blocks:
        x = x + lax.ppermute(x, "blk", [(i, i ^ step) for i in range(blocks)])
        step <<= 1
    return x


def source_pairs(blocks, replicas, slot, half, backward):
    pairs = []
    for b in range(blocks):
        for r in range(replicas):
            src_rep = r if half == 0 else replicas - 1 - r
            src = ((b - r - slot * replicas) % blocks) * replicas + src_rep
            dst = b * replicas + r
            pairs.append((dst, src) if backward else (src, dst))
    return pairs


def activation(pre_act, cotangent):
    logistic = jax.nn.sigmoid(pre_act)
    result = (pre_act * logistic).astype(jnp.bfloat16)
    grad_pre = (
        cotangent.astype(jnp.float32) * logistic * (1.0 + pre_act * (1.0 - logistic))
    ).astype(jnp.bfloat16)
    return (result, grad_pre)


def body(feats, weight, bias, grad_out, tile_values, tile_rows, tile_cols, tile_count):
    replicas = lax.axis_size("rep")
    blocks = lax.axis_size("blk")
    tile_size = tile_values.shape[-1]
    pair_slots = tile_values.shape[2]
    values_here = tile_values[0, 0]
    rows_here = tile_rows[0, 0]
    cols_here = tile_cols[0, 0]
    counts_here = tile_count[0, 0]
    hw_slice = jnp.dot(feats, weight, preferred_element_type=jnp.float32).astype(jnp.bfloat16)
    partition = lax.all_gather(hw_slice, "rep", axis=0, tiled=True)
    part_rows = partition.shape[0]
    half_rows = part_rows // 2
    tiles_per_part = part_rows // tile_size
    both_axes = ("blk", "rep")
    sources = []
    for slot in range(pair_slots):
        halves = [
            lax.ppermute(
                partition[half * half_rows:(half + 1) * half_rows],
                both_axes,
                source_pairs(blocks, replicas, slot, half, False),
            )
            for half in range(2)
        ]
        sources.append(jnp.concatenate(halves, axis=0))
    adjacency = [
        dense_adjacency(
            values_here[slot], rows_here[slot], cols_here[slot], counts_here[slot], tiles_per_part
        )
        for slot in range(pair_slots)
    ]
    aggregate = jnp.zeros(partition.shape, jnp.float32)
    for slot in range(pair_slots):
        aggregate = aggregate + jnp.dot(
            adjacency[slot], sources[slot], preferred_element_type=jnp.float32
        )
    aggregate_rows = rep_reduce_scatter(aggregate, jnp.bfloat16)
    out, grad_rows = activation(aggregate_rows + bias, grad_out)
    grad_block = lax.all_gather(grad_rows, "rep", axis=0, tiled=True)
    returned = [jnp.zeros((half_rows, partition.shape[1]), jnp.float32) for _ in range(2)]
    for slot in range(pair_slots):
        partial = lax.dot_general(
            adjacency[slot],
            grad_block,
            (((0,), (0,)), ((), ())),
            preferred_element_type=jnp.float32,
        ).astype(jnp.bfloat16)
        for half in range(2):
            got = lax.ppermute(
                partial[half * half_rows:(half + 1) * half_rows],
                both_axes,
                source_pairs(blocks, replicas, slot, half, True),
            )
            returned[half] = returned[half] + got.astype(jnp.float32)
    partial_grad = jnp.concatenate(returned, axis=0)
    grad_hw = rep_reduce_scatter(partial_grad, jnp.bfloat16).astype(jnp.bfloat16)
    grad_feats = lax.dot_general(
        grad_hw, weight, (((1,), (1,)), ((), ())), preferred_element_type=jnp.float32
    ).astype(jnp.bfloat16)
    weight_terms = lax.dot_general(
        feats, grad_hw, (((0,), (0,)), ((), ())), preferred_element_type=jnp.float32
    )
    weight_part = rep_reduce_scatter(weight_terms, jnp.float32)
    bias_part = jnp.sum(grad_block.astype(jnp.float32), axis=0)
    totals = blk_all_reduce(jnp.concatenate([weight_part, bias_part[None, :]], axis=0))
    grad_weight = totals[:-1]
    grad_bias = totals[-1]
    return (out, grad_feats, grad_weight, grad_bias)


def solution(mesh):
    in_specs = (
        P(("blk", "rep"), None),
        P(),
        P(),
        P(("blk", "rep"), None),
        P("blk", "rep", None, None, None, None),
        P("blk", "rep", None, None),
        P("blk", "rep", None, None),
        P("blk", "rep", None),
    )
    out_specs = (P(("blk", "rep"), None), P(("blk", "rep"), None), P("rep", None), P())
    return jax.shard_map(body, mesh=mesh, in_specs=in_specs, out_specs=out_specs, check_vma=False)
```

time: 793 us -> 350 us (0.44)
  waiting for transfers between devices: 498 us -> 147 us
  blocking collectives: 166 us -> 45.5 us
  starting transfers between devices: 90 us -> 128 us
  between operations: 14.1 us -> 1.21 us
    reduce_scatter x3 -> x0, waiting for transfers between devices: 280 us -> none  [the longest x1 108 us: body(): lax.psum_scatter(aggregate.astype(jnp.bfloat16), 'rep', scatter_dimension...]
    psum x1 -> x0, blocking collectives: 122 us -> none  [body(): lax.psum(jnp.concatenate([weight_part, bias_part[None, :]], axis=0), 'blk')]
    ppermute x10 -> x25, waiting for transfers between devices: 218 us -> 147 us  [the longest x4 59.5 us: body(): lax.ppermute(partial[half * half_rows:(half + 1) * half_rows], both_axes,...]
    ppermute x10 -> x25, starting transfers between devices: 89.9 us -> 128 us  [the longest x12 52.2 us: rep_reduce_scatter(): got = lax.ppermute(send.astype(wire_dtype), 'rep', partner)]
  transfers between devices with their start and end apart: 13 -> 25, of which waited for: 13 -> 21; matrix products, arithmetic and copies ran while one was open for 1% -> 4% of each run, Pallas kernels for 0% -> 0%
where the time goes in v3:
time: 350 us; the launch traced here: 346 us
  waiting for transfers between devices  147 us (42%)
  starting transfers between devices  128 us (37%)
  blocking collectives  45.5 us (13%)
  matrix products  10.8 us (3%)
  local copies, waits for them, and re-layouts  9.57 us (3%)
  other arithmetic  3.62 us (1%)
    ppermute x4, waiting for transfers between devices, body(): lax.ppermute(partial[half * half_rows:(half + 1) * half_rows], both_axes,...  59.5 us
    ppermute x12, starting transfers between devices, rep_reduce_scatter(): got = lax.ppermute(send.astype(wire_dtype), 'rep', partner)  52.2 us
    ppermute x12, waiting for transfers between devices, rep_reduce_scatter(): got = lax.ppermute(send.astype(wire_dtype), 'rep', partner)  37.1 us
    ppermute x4, waiting for transfers between devices, body(): lax.ppermute(partition[half * half_rows:(half + 1) * half_rows], both_axe...  32.4 us
    ppermute x4, starting transfers between devices, body(): lax.ppermute(partial[half * half_rows:(half + 1) * half_rows], both_axes,...  28.6 us
    ppermute x4, starting transfers between devices, body(): lax.ppermute(partition[half * half_rows:(half + 1) * half_rows], both_axe...  24.2 us
    ppermute x5, starting transfers between devices, blk_all_reduce(): x = x + lax.ppermute(x, 'blk', [(i, i ^ step) for i in range(blocks)])  23 us
    all_gather x1, blocking collectives, body(): partition = lax.all_gather(hw_slice, 'rep', axis=0, tiled=True)  22.8 us
  transfers between devices with their start and end apart: 25, of which 21 were waited for; matrix products, arithmetic and copies ran while one was open for 4% of the time, Pallas kernels for 0%

profile of v3, /device:TPU:6, one launch (start us, length us, event | category | flops | bytes accessed | tf_op | source)
XLA Modules:
  0.0 346.3 jit_solution(12261497730635303897)
XLA Ops:
  2.4 22.8 %all_gather.6 = bf16[1024,256]{1,0:T(8,128)(2,1)S(1)} all-gather(bf16[64,256]{1,0:T(8,128)(2,1)S(1)} %convolution_convert_fusion.3), channel_id=1, replica_groups=mesh['blk'=32,'rep'=16] {'rep'}, dimensions={0}, use_global_device_ids=true | all-gather | bytes 557056 | tf_op jit(solution)/shard_map/all_gather | solution.py:82
  25.3 11.3 %collective-permute-start.2 = (bf16[512,256]{1,0:T(8,128)(2,1)S(1)}, bf16[512,256]{1,0:T(8,128)(2,1)S(1)}, u32[]{:S(2)}, u32[]{:S(2)}) collective-permute-start(bf16[512,256]{1,0:T(8,128)(2,1)S(1)} %get-tuple-element.10), channel_id=1, source_target_pairs={{256,0},{241,1},{226,2},{211,3},{196,4},{181,5},{166,6},{151,7},{1... | collective-permute-start | bytes 786440 | tf_op jit(solution)/shard_map/ppermute | solution.py:90
  38.6 8.9 %collective-permute-start.3 = (bf16[512,256]{1,0:T(8,128)(2,1)S(1)}, bf16[512,256]{1,0:T(8,128)(2,1)}, u32[]{:S(2)}, u32[]{:S(2)}) collective-permute-start(bf16[512,256]{1,0:T(8,128)(2,1)S(1)} %get-tuple-element.11), channel_id=1, source_target_pairs={{271,0},{254,1},{237,2},{220,3},{203,4},{186,5},{169,6},{152,7},{1... | collective-permute-start | bytes 786440 | tf_op jit(solution)/shard_map/ppermute | solution.py:90
  52.2 4.0 %fusion.52 = (bf16[1,1,1,64,128,128]{5,4,3,2,1,0:T(8,128)(2,1)}, bf16[1,1,1,64,128,128]{5,4,3,2,1,0:T(8,128)(2,1)S(1)}) fusion(bf16[1,1,2,64,128,128]{5,4,3,2,1,0:T(8,128)(2,1)} %param.12), kind=kLoop, calls=%fused_computation.88 | loop fusion | bytes 8388608 | tf_op jit(solution)/shard_map/slice | solution.py:100
  56.2 3.3 convolution_convert_fusion.1
  61.2 6.0 %collective-permute-done.2 = bf16[512,256]{1,0:T(8,128)(2,1)S(1)} collective-permute-done((bf16[512,256]{1,0:T(8,128)(2,1)S(1)}, bf16[512,256]{1,0:T(8,128)(2,1)S(1)}, u32[]{:S(2)}, u32[]{:S(2)}) %collective-permute-start.2) | collective-permute-done | bytes 262176 | tf_op jit(solution)/shard_map/ppermute | solution.py:90
  67.2 26.4 %collective-permute-done.3 = bf16[512,256]{1,0:T(8,128)(2,1)} collective-permute-done((bf16[512,256]{1,0:T(8,128)(2,1)S(1)}, bf16[512,256]{1,0:T(8,128)(2,1)}, u32[]{:S(2)}, u32[]{:S(2)}) %collective-permute-start.3) | collective-permute-done | bytes 262176 | tf_op jit(solution)/shard_map/ppermute | solution.py:90
  103.6 5.5 %collective-permute-done.5 = bf16[2,2,64,256]{3,2,1,0:T(8,128)(2,1)S(1)} collective-permute-done((bf16[2,2,64,256]{3,2,1,0:T(8,128)(2,1)S(1)}, bf16[2,2,64,256]{3,2,1,0:T(8,128)(2,1)S(1)}, u32[]{:S(2)}, u32[]{:S(2)}) %collective-permute-start.5) | collective-permute-done | bytes 131104 | tf_op jit(solution)/shard_map/ppermute | solution.py:37
  109.2 15.2 %collective-permute-start.6 = (bf16[2,64,256]{2,1,0:T(8,128)(2,1)S(1)}, bf16[2,64,256]{2,1,0:T(8,128)(2,1)S(1)}, u32[]{:S(2)}, u32[]{:S(2)}) collective-permute-start(bf16[2,64,256]{2,1,0:T(8,128)(2,1)S(1)} %fusion.35), channel_id=1, source_target_pairs={{0,8},{1,9},{2,10},{3,11},{4,12},{5,13},{6,14},{7,15},{8,0},{9,1},... | collective-permute-start | bytes 196616 | tf_op jit(solution)/shard_map/ppermute | solution.py:37
  124.4 2.2 collective-permute-done.6
  126.7 8.7 %collective-permute-start.7 = (bf16[64,256]{1,0:T(8,128)(2,1)S(1)}, bf16[64,256]{1,0:T(8,128)(2,1)S(1)}, u32[]{:S(2)}, u32[]{:S(2)}) collective-permute-start(bf16[64,256]{1,0:T(8,128)(2,1)S(1)} %fusion.39), channel_id=1, source_target_pairs={{0,2},{1,3},{2,0},{3,1},{4,6},{5,7},{6,4},{7,5},{8,10},{9,11},{10,... | collective-permute-start | bytes 98312 | tf_op jit(solution)/shard_map/ppermute | solution.py:37
  138.0 22.6 %all_gather.7 = bf16[1024,256]{1,0:T(8,128)(2,1)S(1)} all-gather(bf16[64,256]{1,0:T(8,128)(2,1)S(1)} %get-tuple-element.12), channel_id=1, replica_groups=mesh['blk'=32,'rep'=16] {'rep'}, dimensions={0}, use_global_device_ids=true | all-gather | bytes 557056 | tf_op jit(solution)/shard_map/all_gather | solution.py:111
  165.0 11.6 %collective-permute-start.8 = (bf16[512,256]{1,0:T(8,128)(2,1)S(1)}, bf16[512,256]{1,0:T(8,128)(2,1)S(1)}, u32[]{:S(2)}, u32[]{:S(2)}) collective-permute-start(bf16[512,256]{1,0:T(8,128)(2,1)S(1)} %get-tuple-element.6), channel_id=1, source_target_pairs={{0,0},{1,497},{2,482},{3,467},{4,452},{5,437},{6,422},{7,407},{8,3... | collective-permute-start | bytes 786440 | tf_op jit(solution)/shard_map/ppermute | solution.py:121
  178.8 13.0 %collective-permute-start.10 = (bf16[512,256]{1,0:T(8,128)(2,1)S(1)}, bf16[512,256]{1,0:T(8,128)(2,1)S(1)}, u32[]{:S(2)}, u32[]{:S(2)}) collective-permute-start(bf16[512,256]{1,0:T(8,128)(2,1)S(1)} %get-tuple-element.7), channel_id=1, source_target_pairs={{0,15},{1,510},{2,493},{3,476},{4,459},{5,442},{6,425},{7,408},{8,... | collective-permute-start | bytes 786440 | tf_op jit(solution)/shard_map/ppermute | solution.py:121
  191.8 13.6 %collective-permute-done.8 = bf16[512,256]{1,0:T(8,128)(2,1)S(1)} collective-permute-done((bf16[512,256]{1,0:T(8,128)(2,1)S(1)}, bf16[512,256]{1,0:T(8,128)(2,1)S(1)}, u32[]{:S(2)}, u32[]{:S(2)}) %collective-permute-start.8) | collective-permute-done | bytes 262176 | tf_op jit(solution)/shard_map/ppermute | solution.py:121
  205.5 45.8 %collective-permute-done.11 = bf16[512,256]{1,0:T(8,128)(2,1)S(1)} collective-permute-done((bf16[512,256]{1,0:T(8,128)(2,1)S(1)}, bf16[512,256]{1,0:T(8,128)(2,1)S(1)}, u32[]{:S(2)}, u32[]{:S(2)}) %collective-permute-start.11) | collective-permute-done | bytes 262176 | tf_op jit(solution)/shard_map/ppermute | solution.py:121
  257.0 5.5 %collective-permute-done.13 = bf16[2,2,64,256]{3,2,1,0:T(8,128)(2,1)S(1)} collective-permute-done((bf16[2,2,64,256]{3,2,1,0:T(8,128)(2,1)S(1)}, bf16[2,2,64,256]{3,2,1,0:T(8,128)(2,1)S(1)}, u32[]{:S(2)}, u32[]{:S(2)}) %collective-permute-start.13) | collective-permute-done | bytes 131104 | tf_op jit(solution)/shard_map/ppermute | solution.py:37
  262.5 6.4 %collective-permute-start.14 = (bf16[2,64,256]{2,1,0:T(8,128)(2,1)S(1)}, bf16[2,64,256]{2,1,0:T(8,128)(2,1)S(1)}, u32[]{:S(2)}, u32[]{:S(2)}) collective-permute-start(bf16[2,64,256]{2,1,0:T(8,128)(2,1)S(1)} %fusion.36), channel_id=1, source_target_pairs={{0,8},{1,9},{2,10},{3,11},{4,12},{5,13},{6,14},{7,15},{8,0},{9,1},... | collective-permute-start | bytes 196616 | tf_op jit(solution)/shard_map/ppermute | solution.py:37
  268.9 2.2 collective-permute-done.14
  273.1 5.4 %collective-permute-done.15 = bf16[64,256]{1,0:T(8,128)(2,1)S(1)} collective-permute-done((bf16[64,256]{1,0:T(8,128)(2,1)S(1)}, bf16[64,256]{1,0:T(8,128)(2,1)S(1)}, u32[]{:S(2)}, u32[]{:S(2)}) %collective-permute-start.15) | collective-permute-done | bytes 32800 | tf_op jit(solution)/shard_map/ppermute | solution.py:37
  282.0 3.0 collective-permute-start.17
  285.1 3.1 collective-permute-done.17
  288.2 5.4 %collective-permute-start.18 = (f32[2,16,256]{2,1,0:T(8,128)S(1)}, f32[2,16,256]{2,1,0:T(8,128)S(1)}, u32[]{:S(2)}, u32[]{:S(2)}) collective-permute-start(f32[2,16,256]{2,1,0:T(8,128)S(1)} %dynamic-slice_bitcast_fusion.2), channel_id=1, source_target_pairs={{0,8},{1,9},{2,10},{3,11},{4,12},{5,13},{6,14},{7,15},{8,0},{9,1},... | collective-permute-start | bytes 98312 | tf_op jit(solution)/shard_map/ppermute | solution.py:37
  297.7 5.1 %collective-permute-done.19 = f32[16,256]{1,0:T(8,128)S(1)} collective-permute-done((f32[16,256]{1,0:T(8,128)S(1)}, f32[16,256]{1,0:T(8,128)S(1)}, u32[]{:S(2)}, u32[]{:S(2)}) %collective-permute-start.19) | collective-permute-done | bytes 16416 | tf_op jit(solution)/shard_map/ppermute | solution.py:37
  302.7 2.4 collective-permute-start.20
  305.1 3.3 collective-permute-done.20
  310.4 3.8 %collective-permute-done.21 = f32[17,256]{1,0:T(8,128)S(1)} collective-permute-done((f32[17,256]{1,0:T(8,128)S(1)}, f32[17,256]{1,0:T(8,128)S(1)}, u32[]{:S(2)}, u32[]{:S(2)}) %collective-permute-start.21) | collective-permute-done | bytes 17440 | tf_op jit(solution)/shard_map/ppermute | solution.py:47
  316.1 4.7 %collective-permute-done.22 = f32[17,256]{1,0:T(8,128)S(1)} collective-permute-done((f32[17,256]{1,0:T(8,128)S(1)}, f32[17,256]{1,0:T(8,128)S(1)}, u32[]{:S(2)}, u32[]{:S(2)}) %collective-permute-start.22) | collective-permute-done | bytes 17440 | tf_op jit(solution)/shard_map/ppermute | solution.py:47
  320.8 5.8 %collective-permute-start.23 = (f32[17,256]{1,0:T(8,128)S(1)}, f32[17,256]{1,0:T(8,128)S(1)}, u32[]{:S(2)}, u32[]{:S(2)}) collective-permute-start(f32[17,256]{1,0:T(8,128)S(1)} %add.179), channel_id=1, source_target_pairs={{0,128},{16,144},{32,160},{48,176},{64,192},{80,208},{96,224},{112... | collective-permute-start | bytes 52232 | tf_op jit(solution)/shard_map/ppermute | solution.py:47
  326.6 4.0 %collective-permute-done.23 = f32[17,256]{1,0:T(8,128)S(1)} collective-permute-done((f32[17,256]{1,0:T(8,128)S(1)}, f32[17,256]{1,0:T(8,128)S(1)}, u32[]{:S(2)}, u32[]{:S(2)}) %collective-permute-start.23) | collective-permute-done | bytes 17440 | tf_op jit(solution)/shard_map/ppermute | solution.py:47
  330.7 10.9 %collective-permute-start.24 = (f32[17,256]{1,0:T(8,128)S(1)}, f32[17,256]{1,0:T(8,128)S(1)}, u32[]{:S(2)}, u32[]{:S(2)}) collective-permute-start(f32[17,256]{1,0:T(8,128)S(1)} %add.180), channel_id=1, source_target_pairs={{0,256},{16,272},{32,288},{48,304},{64,320},{80,336},{96,352},{112... | collective-permute-start | bytes 52232 | tf_op jit(solution)/shard_map/ppermute | solution.py:47
  342.4 2.7 collective-permute-done.24
  (95 shorter events, 50.0 us)
Async XLA Ops:
  25.3 41.9 %collective-permute-start.2 = (bf16[512,256]{1,0:T(8,128)(2,1)S(1)}, bf16[512,256]{1,0:T(8,128)(2,1)S(1)}, u32[]{:S(2)}, u32[]{:S(2)}) collective-permute-start(bf16[512,256]{1,0:T(8,128)(2,1)S(1)} %get-tuple-element.10), channel_id=1, source_target_pairs={{256,0},{241,1},{226,2},{211,3},{196,4},{181,5},{166,6},{151,7},{1... | collective-permute-start | bytes 786440 | tf_op jit(solution)/shard_map/ppermute | solution.py:90
  36.7 58.7 %collective-permute-start = (bf16[512,256]{1,0:T(8,128)(2,1)S(1)}, bf16[512,256]{1,0:T(8,128)(2,1)S(1)}, u32[]{:S(2)}, u32[]{:S(2)}) collective-permute-start(bf16[512,256]{1,0:T(8,128)(2,1)S(1)} %get-tuple-element.10), channel_id=1, source_target_pairs={{0,0},{497,1},{482,2},{467,3},{452,4},{437,5},{422,6},{407,7},{392... | collective-permute-start | bytes 786440 | tf_op jit(solution)/shard_map/ppermute | solution.py:90
  38.6 55.1 %collective-permute-start.3 = (bf16[512,256]{1,0:T(8,128)(2,1)S(1)}, bf16[512,256]{1,0:T(8,128)(2,1)}, u32[]{:S(2)}, u32[]{:S(2)}) collective-permute-start(bf16[512,256]{1,0:T(8,128)(2,1)S(1)} %get-tuple-element.11), channel_id=1, source_target_pairs={{271,0},{254,1},{237,2},{220,3},{203,4},{186,5},{169,6},{152,7},{1... | collective-permute-start | bytes 786440 | tf_op jit(solution)/shard_map/ppermute | solution.py:90
  47.5 47.9 %collective-permute-start.1 = (bf16[512,256]{1,0:T(8,128)(2,1)S(1)}, bf16[512,256]{1,0:T(8,128)(2,1)S(1)}, u32[]{:S(2)}, u32[]{:S(2)}) collective-permute-start(bf16[512,256]{1,0:T(8,128)(2,1)S(1)} %get-tuple-element.11), channel_id=1, source_target_pairs={{15,0},{510,1},{493,2},{476,3},{459,4},{442,5},{425,6},{408,7},{39... | collective-permute-start | bytes 786440 | tf_op jit(solution)/shard_map/ppermute | solution.py:90
  52.2 4.1 %copy-start.9 = (s32[1,1,2,64]{3,2,1,0:T(2,128)S(1)}, s32[1,1,2,64]{3,2,1,0:T(2,128)}, u32[]{:S(2)}) copy-start(s32[1,1,2,64]{3,2,1,0:T(2,128)} %param.14) | copy-start | bytes 1540
  59.5 35.8 %copy-start.1 = (bf16[64,16384]{1,0:T(8,128)(2,1)}, bf16[64,16384]{1,0:T(8,128)(2,1)S(1)}, u32[]{:S(2)}) copy-start(bf16[64,16384]{1,0:T(8,128)(2,1)S(1)} %convolution_convert_fusion.1) | copy-start | bytes 6291460
  61.2 34.1 %copy-start.3 = (bf16[64,16384]{1,0:T(8,128)(2,1)}, bf16[64,16384]{1,0:T(8,128)(2,1)S(1)}, u32[]{:S(2)}) copy-start(bf16[64,16384]{1,0:T(8,128)(2,1)S(1)} %convolution_convert_fusion) | copy-start | bytes 6291460
  96.1 41.2 %copy-start.7 = (bf16[64,256]{1,0:T(8,128)(2,1)S(1)}, bf16[64,256]{1,0:T(8,128)(2,1)}, u32[]{:S(2)}) copy-start(bf16[64,256]{1,0:T(8,128)(2,1)} %param.11) | copy-start | bytes 98308
  96.1 41.2 %copy-start.8 = (f32[256]{0:T(256)S(1)}, f32[256]{0:T(256)}, u32[]{:S(2)}) copy-start(f32[256]{0:T(256)} %param.10) | copy-start | bytes 3076
  96.1 64.5 %copy-start.4 = (bf16[64,16384]{1,0:T(8,128)(2,1)S(1)}, bf16[64,16384]{1,0:T(8,128)(2,1)}, u32[]{:S(2)}) copy-start(bf16[64,16384]{1,0:T(8,128)(2,1)} %copy-done.3) | copy-start | bytes 6291460
  97.1 3.4 collective-permute-start.4
  101.7 7.4 %collective-permute-start.5 = (bf16[2,2,64,256]{3,2,1,0:T(8,128)(2,1)S(1)}, bf16[2,2,64,256]{3,2,1,0:T(8,128)(2,1)S(1)}, u32[]{:S(2)}, u32[]{:S(2)}) collective-permute-start(bf16[2,2,64,256]{3,2,1,0:T(8,128)(2,1)S(1)} %fusion.33), channel_id=1, source_target_pairs={{0,4},{1,5},{2,6},{3,7},{4,0},{5,1},{6,2},{7,3},{8,12},{9,13},{10,... | collective-permute-start | bytes 393224 | tf_op jit(solution)/shard_map/ppermute | solution.py:37
  109.2 17.5 %collective-permute-start.6 = (bf16[2,64,256]{2,1,0:T(8,128)(2,1)S(1)}, bf16[2,64,256]{2,1,0:T(8,128)(2,1)S(1)}, u32[]{:S(2)}, u32[]{:S(2)}) collective-permute-start(bf16[2,64,256]{2,1,0:T(8,128)(2,1)S(1)} %fusion.35), channel_id=1, source_target_pairs={{0,8},{1,9},{2,10},{3,11},{4,12},{5,13},{6,14},{7,15},{8,0},{9,1},... | collective-permute-start | bytes 196616 | tf_op jit(solution)/shard_map/ppermute | solution.py:37
  126.7 10.6 %collective-permute-start.7 = (bf16[64,256]{1,0:T(8,128)(2,1)S(1)}, bf16[64,256]{1,0:T(8,128)(2,1)S(1)}, u32[]{:S(2)}, u32[]{:S(2)}) collective-permute-start(bf16[64,256]{1,0:T(8,128)(2,1)S(1)} %fusion.39), channel_id=1, source_target_pairs={{0,2},{1,3},{2,0},{3,1},{4,6},{5,7},{6,4},{7,5},{8,10},{9,11},{10,... | collective-permute-start | bytes 98312 | tf_op jit(solution)/shard_map/ppermute | solution.py:37
  163.1 28.7 %collective-permute-start.9 = (bf16[512,256]{1,0:T(8,128)(2,1)S(1)}, bf16[512,256]{1,0:T(8,128)(2,1)S(1)}, u32[]{:S(2)}, u32[]{:S(2)}) collective-permute-start(bf16[512,256]{1,0:T(8,128)(2,1)S(1)} %get-tuple-element.8), channel_id=1, source_target_pairs={{0,256},{1,241},{2,226},{3,211},{4,196},{5,181},{6,166},{7,151},{8... | collective-permute-start | bytes 786440 | tf_op jit(solution)/shard_map/ppermute | solution.py:121
  165.0 40.4 %collective-permute-start.8 = (bf16[512,256]{1,0:T(8,128)(2,1)S(1)}, bf16[512,256]{1,0:T(8,128)(2,1)S(1)}, u32[]{:S(2)}, u32[]{:S(2)}) collective-permute-start(bf16[512,256]{1,0:T(8,128)(2,1)S(1)} %get-tuple-element.6), channel_id=1, source_target_pairs={{0,0},{1,497},{2,482},{3,467},{4,452},{5,437},{6,422},{7,407},{8,3... | collective-permute-start | bytes 786440 | tf_op jit(solution)/shard_map/ppermute | solution.py:121
  176.7 74.6 %collective-permute-start.11 = (bf16[512,256]{1,0:T(8,128)(2,1)S(1)}, bf16[512,256]{1,0:T(8,128)(2,1)S(1)}, u32[]{:S(2)}, u32[]{:S(2)}) collective-permute-start(bf16[512,256]{1,0:T(8,128)(2,1)S(1)} %get-tuple-element.9), channel_id=1, source_target_pairs={{0,271},{1,254},{2,237},{3,220},{4,203},{5,186},{6,169},{7,152},{8... | collective-permute-start | bytes 786440 | tf_op jit(solution)/shard_map/ppermute | solution.py:121
  178.8 72.5 %collective-permute-start.10 = (bf16[512,256]{1,0:T(8,128)(2,1)S(1)}, bf16[512,256]{1,0:T(8,128)(2,1)S(1)}, u32[]{:S(2)}, u32[]{:S(2)}) collective-permute-start(bf16[512,256]{1,0:T(8,128)(2,1)S(1)} %get-tuple-element.7), channel_id=1, source_target_pairs={{0,15},{1,510},{2,493},{3,476},{4,459},{5,442},{6,425},{7,408},{8,... | collective-permute-start | bytes 786440 | tf_op jit(solution)/shard_map/ppermute | solution.py:121
  251.4 27.1 %copy-start.6 = (bf16[64,256]{1,0:T(8,128)(2,1)S(1)}, bf16[64,256]{1,0:T(8,128)(2,1)}, u32[]{:S(2)}) copy-start(bf16[64,256]{1,0:T(8,128)(2,1)} %param.8) | copy-start | bytes 98308
  251.5 3.4 collective-permute-start.12
  255.0 7.4 %collective-permute-start.13 = (bf16[2,2,64,256]{3,2,1,0:T(8,128)(2,1)S(1)}, bf16[2,2,64,256]{3,2,1,0:T(8,128)(2,1)S(1)}, u32[]{:S(2)}, u32[]{:S(2)}) collective-permute-start(bf16[2,2,64,256]{3,2,1,0:T(8,128)(2,1)S(1)} %fusion.34), channel_id=1, source_target_pairs={{0,4},{1,5},{2,6},{3,7},{4,0},{5,1},{6,2},{7,3},{8,12},{9,13},{10,... | collective-permute-start | bytes 393224 | tf_op jit(solution)/shard_map/ppermute | solution.py:37
  262.5 8.6 %collective-permute-start.14 = (bf16[2,64,256]{2,1,0:T(8,128)(2,1)S(1)}, bf16[2,64,256]{2,1,0:T(8,128)(2,1)S(1)}, u32[]{:S(2)}, u32[]{:S(2)}) collective-permute-start(bf16[2,64,256]{2,1,0:T(8,128)(2,1)S(1)} %fusion.36), channel_id=1, source_target_pairs={{0,8},{1,9},{2,10},{3,11},{4,12},{5,13},{6,14},{7,15},{8,0},{9,1},... | collective-permute-start | bytes 196616 | tf_op jit(solution)/shard_map/ppermute | solution.py:37
  271.2 7.3 %collective-permute-start.15 = (bf16[64,256]{1,0:T(8,128)(2,1)S(1)}, bf16[64,256]{1,0:T(8,128)(2,1)S(1)}, u32[]{:S(2)}, u32[]{:S(2)}) collective-permute-start(bf16[64,256]{1,0:T(8,128)(2,1)S(1)} %fusion.40), channel_id=1, source_target_pairs={{0,2},{1,3},{2,0},{3,1},{4,6},{5,7},{6,4},{7,5},{8,10},{9,11},{10,... | collective-permute-start | bytes 98312 | tf_op jit(solution)/shard_map/ppermute | solution.py:37
  278.8 3.2 collective-permute-start.16
  282.0 6.2 %collective-permute-start.17 = (f32[2,2,16,256]{3,2,1,0:T(8,128)S(1)}, f32[2,2,16,256]{3,2,1,0:T(8,128)S(1)}, u32[]{:S(2)}, u32[]{:S(2)}) collective-permute-start(f32[2,2,16,256]{3,2,1,0:T(8,128)S(1)} %dynamic-slice_bitcast_fusion.1), channel_id=1, source_target_pairs={{0,4},{1,5},{2,6},{3,7},{4,0},{5,1},{6,2},{7,3},{8,12},{9,13},{10,... | collective-permute-start | bytes 196616 | tf_op jit(solution)/shard_map/ppermute | solution.py:37
  288.2 7.3 %collective-permute-start.18 = (f32[2,16,256]{2,1,0:T(8,128)S(1)}, f32[2,16,256]{2,1,0:T(8,128)S(1)}, u32[]{:S(2)}, u32[]{:S(2)}) collective-permute-start(f32[2,16,256]{2,1,0:T(8,128)S(1)} %dynamic-slice_bitcast_fusion.2), channel_id=1, source_target_pairs={{0,8},{1,9},{2,10},{3,11},{4,12},{5,13},{6,14},{7,15},{8,0},{9,1},... | collective-permute-start | bytes 98312 | tf_op jit(solution)/shard_map/ppermute | solution.py:37
  295.6 7.1 %collective-permute-start.19 = (f32[16,256]{1,0:T(8,128)S(1)}, f32[16,256]{1,0:T(8,128)S(1)}, u32[]{:S(2)}, u32[]{:S(2)}) collective-permute-start(f32[16,256]{1,0:T(8,128)S(1)} %dynamic-slice_bitcast_fusion.3), channel_id=1, source_target_pairs={{0,2},{1,3},{2,0},{3,1},{4,6},{5,7},{6,4},{7,5},{8,10},{9,11},{10,... | collective-permute-start | bytes 49160 | tf_op jit(solution)/shard_map/ppermute | solution.py:37
  302.7 5.7 %collective-permute-start.20 = (f32[17,256]{1,0:T(8,128)S(1)}, f32[17,256]{1,0:T(8,128)S(1)}, u32[]{:S(2)}, u32[]{:S(2)}) collective-permute-start(f32[17,256]{1,0:T(8,128)S(1)} %pad_maximum_fusion.1), channel_id=1, source_target_pairs={{0,16},{16,0},{32,48},{48,32},{64,80},{80,64},{96,112},{112,96},{1... | collective-permute-start | bytes 52232 | tf_op jit(solution)/shard_map/ppermute | solution.py:47
  308.4 5.7 %collective-permute-start.21 = (f32[17,256]{1,0:T(8,128)S(1)}, f32[17,256]{1,0:T(8,128)S(1)}, u32[]{:S(2)}, u32[]{:S(2)}) collective-permute-start(f32[17,256]{1,0:T(8,128)S(1)} %fusion.51), channel_id=1, source_target_pairs={{0,32},{16,48},{32,0},{48,16},{64,96},{80,112},{96,64},{112,80},{1... | collective-permute-start | bytes 52232 | tf_op jit(solution)/shard_map/ppermute | solution.py:47
  314.2 6.6 %collective-permute-start.22 = (f32[17,256]{1,0:T(8,128)S(1)}, f32[17,256]{1,0:T(8,128)S(1)}, u32[]{:S(2)}, u32[]{:S(2)}) collective-permute-start(f32[17,256]{1,0:T(8,128)S(1)} %add.178), channel_id=1, source_target_pairs={{0,64},{16,80},{32,96},{48,112},{64,0},{80,16},{96,32},{112,48},{1... | collective-permute-start | bytes 52232 | tf_op jit(solution)/shard_map/ppermute | solution.py:47
  320.8 9.9 %collective-permute-start.23 = (f32[17,256]{1,0:T(8,128)S(1)}, f32[17,256]{1,0:T(8,128)S(1)}, u32[]{:S(2)}, u32[]{:S(2)}) collective-permute-start(f32[17,256]{1,0:T(8,128)S(1)} %add.179), channel_id=1, source_target_pairs={{0,128},{16,144},{32,160},{48,176},{64,192},{80,208},{96,224},{112... | collective-permute-start | bytes 52232 | tf_op jit(solution)/shard_map/ppermute | solution.py:47
  330.7 14.4 %collective-permute-start.24 = (f32[17,256]{1,0:T(8,128)S(1)}, f32[17,256]{1,0:T(8,128)S(1)}, u32[]{:S(2)}, u32[]{:S(2)}) collective-permute-start(f32[17,256]{1,0:T(8,128)S(1)} %add.180), channel_id=1, source_target_pairs={{0,256},{16,272},{32,288},{48,304},{64,320},{80,336},{96,352},{112... | collective-permute-start | bytes 52232 | tf_op jit(solution)/shard_map/ppermute | solution.py:47
  (4 other events, 7.6 us)

commit v4 on v3

--- a/solution.py
+++ b/solution.py
@@ -78,8 +78,7 @@
     rows_here = tile_rows[0, 0]
     cols_here = tile_cols[0, 0]
     counts_here = tile_count[0, 0]
-    hw_slice = jnp.dot(feats, weight, preferred_element_type=jnp.float32).astype(jnp.bfloat16)
-    partition = lax.all_gather(hw_slice, "rep", axis=0, tiled=True)
+    partition = lax.all_gather(feats, "rep", axis=0, tiled=True)
     part_rows = partition.shape[0]
     half_rows = part_rows // 2
     tiles_per_part = part_rows // tile_size
@@ -101,14 +100,30 @@
         )
         for slot in range(pair_slots)
     ]
-    aggregate = jnp.zeros(partition.shape, jnp.float32)
+    aggregated_feats = jnp.zeros(partition.shape, jnp.float32)
     for slot in range(pair_slots):
-        aggregate = aggregate + jnp.dot(
+        aggregated_feats = aggregated_feats + jnp.dot(
             adjacency[slot], sources[slot], preferred_element_type=jnp.float32
         )
+    aggregate = jnp.dot(
+        aggregated_feats,
+        weight.astype(jnp.float32),
+        precision=lax.Precision.HIGHEST,
+        preferred_element_type=jnp.float32,
+    )
     aggregate_rows = rep_reduce_scatter(aggregate, jnp.bfloat16)
     out, grad_rows = activation(aggregate_rows + bias, grad_out)
     grad_block = lax.all_gather(grad_rows, "rep", axis=0, tiled=True)
+    weight_terms = lax.dot_general(
+        aggregated_feats,
+        grad_block.astype(jnp.float32),
+        (((0,), (0,)), ((), ())),
+        precision=lax.Precision.HIGHEST,
+        preferred_element_type=jnp.float32,
+    )
+    weight_part = rep_reduce_scatter(weight_terms, jnp.float32)
+    bias_part = jnp.sum(grad_block.astype(jnp.float32), axis=0)
+    totals = blk_all_reduce(jnp.concatenate([weight_part, bias_part[None, :]], axis=0))
     returned = [jnp.zeros((half_rows, partition.shape[1]), jnp.float32) for _ in range(2)]
     for slot in range(pair_slots):
         partial = lax.dot_general(
@@ -129,12 +144,6 @@
     grad_feats = lax.dot_general(
         grad_hw, weight, (((1,), (1,)), ((), ())), preferred_element_type=jnp.float32
     ).astype(jnp.bfloat16)
-    weight_terms = lax.dot_general(
-        feats, grad_hw, (((0,), (0,)), ((), ())), preferred_element_type=jnp.float32
-    )
-    weight_part = rep_reduce_scatter(weight_terms, jnp.float32)
-    bias_part = jnp.sum(grad_block.astype(jnp.float32), axis=0)
-    totals = blk_all_reduce(jnp.concatenate([weight_part, bias_part[None, :]], axis=0))
     grad_weight = totals[:-1]
     grad_bias = totals[-1]
     return (out, grad_feats, grad_weight, grad_bias)

time: 350 us -> 328 us (0.937)
  waiting for transfers between devices: 147 us -> 113 us
  starting transfers between devices: 128 us -> 140 us
    ppermute x12, waiting for transfers between devices: 37.1 us -> 15.7 us  [rep_reduce_scatter(): got = lax.ppermute(send.astype(wire_dtype), 'rep', partner)]
    ppermute x12, starting transfers between devices: 52.2 us -> 66.6 us  [rep_reduce_scatter(): got = lax.ppermute(send.astype(wire_dtype), 'rep', partner)]
    ppermute x5, waiting for transfers between devices: 18.5 us -> 6.97 us  [blk_all_reduce(): x = x + lax.ppermute(x, 'blk', [(i, i ^ step) for i in range(blocks)])]
    ppermute x4, starting transfers between devices: 28.6 us -> 19.5 us  [body(): lax.ppermute(partial[half * half_rows:(half + 1) * half_rows], both_axes,...]
    ppermute x5, starting transfers between devices: 23 us -> 30 us  [blk_all_reduce(): x = x + lax.ppermute(x, 'blk', [(i, i ^ step) for i in range(blocks)])]
  transfers between devices with their start and end apart: 25 -> 25, of which waited for: 21 -> 14; matrix products, arithmetic and copies ran while one was open for 4% -> 5% of each run, Pallas kernels for 0% -> 0%
where the time goes in v4:
time: 328 us; the launch traced here: 326 us
  starting transfers between devices  140 us (43%)
  waiting for transfers between devices  113 us (34%)
  blocking collectives  45.8 us (14%)
  matrix products  11.3 us (3%)
  local copies, waits for them, and re-layouts  9.74 us (3%)
  other arithmetic  5.3 us (2%)
    ppermute x12, starting transfers between devices, rep_reduce_scatter(): got = lax.ppermute(send.astype(wire_dtype), 'rep', partner)  66.6 us
    ppermute x4, waiting for transfers between devices, body(): lax.ppermute(partial[half * half_rows:(half + 1) * half_rows], both_axes,...  57.5 us
    ppermute x4, waiting for transfers between devices, body(): lax.ppermute(partition[half * half_rows:(half + 1) * half_rows], both_axe...  32.4 us
    ppermute x5, starting transfers between devices, blk_all_reduce(): x = x + lax.ppermute(x, 'blk', [(i, i ^ step) for i in range(blocks)])  30 us
    ppermute x4, starting transfers between devices, body(): lax.ppermute(partition[half * half_rows:(half + 1) * half_rows], both_axe...  24.2 us
    all_gather x1, blocking collectives, body(): partition = lax.all_gather(feats, 'rep', axis=0, tiled=True)  23.2 us
    all_gather x1, blocking collectives, body(): grad_block = lax.all_gather(grad_rows, 'rep', axis=0, tiled=True)  22.6 us
    ppermute x4, starting transfers between devices, body(): lax.ppermute(partial[half * half_rows:(half + 1) * half_rows], both_axes,...  19.5 us
  transfers between devices with their start and end apart: 25, of which 14 were waited for; matrix products, arithmetic and copies ran while one was open for 5% of the time, Pallas kernels for 0%

profile of v4, /device:TPU:6, one launch (start us, length us, event | category | flops | bytes accessed | tf_op | source)
XLA Modules:
  0.0 326.3 jit_solution(9031470624948047421)
XLA Ops:
  0.6 23.2 %all_gather.6 = bf16[1024,256]{1,0:T(8,128)(2,1)S(1)} all-gather(bf16[64,256]{1,0:T(8,128)(2,1)} %param.8), channel_id=1, replica_groups=mesh['blk'=32,'rep'=16] {'rep'}, dimensions={0}, use_global_device_ids=true | all-gather | bytes 557056 | tf_op jit(solution)/shard_map/all_gather | solution.py:81
  23.9 11.4 %collective-permute-start.2 = (bf16[512,256]{1,0:T(8,128)(2,1)S(1)}, bf16[512,256]{1,0:T(8,128)(2,1)S(1)}, u32[]{:S(2)}, u32[]{:S(2)}) collective-permute-start(bf16[512,256]{1,0:T(8,128)(2,1)S(1)} %get-tuple-element.10), channel_id=1, source_target_pairs={{256,0},{241,1},{226,2},{211,3},{196,4},{181,5},{166,6},{151,7},{1... | collective-permute-start | bytes 786440 | tf_op jit(solution)/shard_map/ppermute | solution.py:89
  35.3 1.9 collective-permute-start
  37.2 8.8 %collective-permute-start.3 = (bf16[512,256]{1,0:T(8,128)(2,1)S(1)}, bf16[512,256]{1,0:T(8,128)(2,1)}, u32[]{:S(2)}, u32[]{:S(2)}) collective-permute-start(bf16[512,256]{1,0:T(8,128)(2,1)S(1)} %get-tuple-element.11), channel_id=1, source_target_pairs={{271,0},{254,1},{237,2},{220,3},{203,4},{186,5},{169,6},{152,7},{1... | collective-permute-start | bytes 786440 | tf_op jit(solution)/shard_map/ppermute | solution.py:89
  46.0 2.0 collective-permute-start.1
  50.7 4.0 %fusion.54 = (bf16[1,1,1,64,128,128]{5,4,3,2,1,0:T(8,128)(2,1)}, bf16[1,1,1,64,128,128]{5,4,3,2,1,0:T(8,128)(2,1)S(1)}) fusion(bf16[1,1,2,64,128,128]{5,4,3,2,1,0:T(8,128)(2,1)} %param.12), kind=kLoop, calls=%fused_computation.88 | loop fusion | bytes 8388608 | tf_op jit(solution)/shard_map/slice | solution.py:99
  54.8 3.3 %convolution_convert_fusion.1 = bf16[64,16384]{1,0:T(8,128)(2,1)S(1)} fusion(bf16[8,8,128,128]{3,2,1,0:T(8,128)(2,1)} %bitcast.112, s32[64]{0:T(128)S(1)} %get-tuple-element.14, pred[64]{0:T(512)(128)(4,1)S(1)} %iota_compare_fusion.3), kind=kOutput, calls=%fused_computation.1 | convolution fusion | flops 135274496 | bytes 4194624 | tf_op jit(solution)/shard_map/dot_general | solution.py:13
  59.8 6.1 %collective-permute-done.2 = bf16[512,256]{1,0:T(8,128)(2,1)S(1)} collective-permute-done((bf16[512,256]{1,0:T(8,128)(2,1)S(1)}, bf16[512,256]{1,0:T(8,128)(2,1)S(1)}, u32[]{:S(2)}, u32[]{:S(2)}) %collective-permute-start.2) | collective-permute-done | bytes 262176 | tf_op jit(solution)/shard_map/ppermute | solution.py:89
  65.9 26.3 %collective-permute-done.3 = bf16[512,256]{1,0:T(8,128)(2,1)} collective-permute-done((bf16[512,256]{1,0:T(8,128)(2,1)S(1)}, bf16[512,256]{1,0:T(8,128)(2,1)}, u32[]{:S(2)}, u32[]{:S(2)}) %collective-permute-start.3) | collective-permute-done | bytes 262176 | tf_op jit(solution)/shard_map/ppermute | solution.py:89
  99.6 2.1 collective-permute-start.5
  101.7 5.6 %collective-permute-done.5 = bf16[2,2,64,256]{3,2,1,0:T(8,128)(2,1)} collective-permute-done((bf16[2,2,64,256]{3,2,1,0:T(8,128)(2,1)S(1)}, bf16[2,2,64,256]{3,2,1,0:T(8,128)(2,1)}, u32[]{:S(2)}, u32[]{:S(2)}) %collective-permute-start.5) | collective-permute-done | bytes 131104 | tf_op jit(solution)/shard_map/ppermute | solution.py:37
  109.0 15.6 %collective-permute-start.6 = (bf16[2,64,256]{2,1,0:T(8,128)(2,1)}, bf16[2,64,256]{2,1,0:T(8,128)(2,1)}, u32[]{:S(2)}, u32[]{:S(2)}) collective-permute-start(bf16[2,64,256]{2,1,0:T(8,128)(2,1)} %fusion.35), channel_id=1, source_target_pairs={{0,8},{1,9},{2,10},{3,11},{4,12},{5,13},{6,14},{7,15},{8,0},{9,1},... | collective-permute-start | bytes 196616 | tf_op jit(solution)/shard_map/ppermute | solution.py:37
  124.6 2.5 collective-permute-done.6
  128.6 8.4 %collective-permute-start.7 = (bf16[64,256]{1,0:T(8,128)(2,1)S(1)}, bf16[64,256]{1,0:T(8,128)(2,1)S(1)}, u32[]{:S(2)}, u32[]{:S(2)}) collective-permute-start(bf16[64,256]{1,0:T(8,128)(2,1)S(1)} %fusion.39), channel_id=1, source_target_pairs={{0,2},{1,3},{2,0},{3,1},{4,6},{5,7},{6,4},{7,5},{8,10},{9,11},{10,... | collective-permute-start | bytes 98312 | tf_op jit(solution)/shard_map/ppermute | solution.py:37
  140.4 22.6 %all_gather.7 = bf16[1024,256]{1,0:T(8,128)(2,1)S(1)} all-gather(bf16[64,256]{1,0:T(8,128)(2,1)S(1)} %get-tuple-element.12), channel_id=1, replica_groups=mesh['blk'=32,'rep'=16] {'rep'}, dimensions={0}, use_global_device_ids=true | all-gather | bytes 557056 | tf_op jit(solution)/shard_map/all_gather | solution.py:116
  166.5 2.3 collective-permute-start.16
  169.8 2.3 collective-permute-start.17
  174.2 11.5 %collective-permute-start.11 = (bf16[512,256]{1,0:T(8,128)(2,1)S(1)}, bf16[512,256]{1,0:T(8,128)(2,1)S(1)}, u32[]{:S(2)}, u32[]{:S(2)}) collective-permute-start(bf16[512,256]{1,0:T(8,128)(2,1)S(1)} %get-tuple-element.9), channel_id=1, source_target_pairs={{0,271},{1,254},{2,237},{3,220},{4,203},{5,186},{6,169},{7,152},{8... | collective-permute-start | bytes 786440 | tf_op jit(solution)/shard_map/ppermute | solution.py:136
  185.7 2.7 collective-permute-start.8
  188.4 3.4 %collective-permute-start.10 = (bf16[512,256]{1,0:T(8,128)(2,1)S(1)}, bf16[512,256]{1,0:T(8,128)(2,1)S(1)}, u32[]{:S(2)}, u32[]{:S(2)}) collective-permute-start(bf16[512,256]{1,0:T(8,128)(2,1)S(1)} %get-tuple-element.7), channel_id=1, source_target_pairs={{0,15},{1,510},{2,493},{3,476},{4,459},{5,442},{6,425},{7,408},{8,... | collective-permute-start | bytes 786440 | tf_op jit(solution)/shard_map/ppermute | solution.py:136
  191.9 10.8 %collective-permute-start.18 = (f32[2,16,256]{2,1,0:T(8,128)S(1)}, f32[2,16,256]{2,1,0:T(8,128)S(1)}, u32[]{:S(2)}, u32[]{:S(2)}) collective-permute-start(f32[2,16,256]{2,1,0:T(8,128)S(1)} %dynamic-slice_bitcast_fusion.2), channel_id=1, source_target_pairs={{0,8},{1,9},{2,10},{3,11},{4,12},{5,13},{6,14},{7,15},{8,0},{9,1},... | collective-permute-start | bytes 98312 | tf_op jit(solution)/shard_map/ppermute | solution.py:37
  202.7 29.5 %collective-permute-done.8 = bf16[512,256]{1,0:T(8,128)(2,1)S(1)} collective-permute-done((bf16[512,256]{1,0:T(8,128)(2,1)S(1)}, bf16[512,256]{1,0:T(8,128)(2,1)S(1)}, u32[]{:S(2)}, u32[]{:S(2)}) %collective-permute-start.8) | collective-permute-done | bytes 262176 | tf_op jit(solution)/shard_map/ppermute | solution.py:136
  232.2 28.0 %collective-permute-done.11 = bf16[512,256]{1,0:T(8,128)(2,1)S(1)} collective-permute-done((bf16[512,256]{1,0:T(8,128)(2,1)S(1)}, bf16[512,256]{1,0:T(8,128)(2,1)S(1)}, u32[]{:S(2)}, u32[]{:S(2)}) %collective-permute-start.11) | collective-permute-done | bytes 262176 | tf_op jit(solution)/shard_map/ppermute | solution.py:136
  266.4 3.2 collective-permute-done.19
  269.5 2.6 collective-permute-start.20
  272.3 12.4 %collective-permute-start.14 = (bf16[2,64,256]{2,1,0:T(8,128)(2,1)S(1)}, bf16[2,64,256]{2,1,0:T(8,128)(2,1)S(1)}, u32[]{:S(2)}, u32[]{:S(2)}) collective-permute-start(bf16[2,64,256]{2,1,0:T(8,128)(2,1)S(1)} %fusion.36), channel_id=1, source_target_pairs={{0,8},{1,9},{2,10},{3,11},{4,12},{5,13},{6,14},{7,15},{8,0},{9,1},... | collective-permute-start | bytes 196616 | tf_op jit(solution)/shard_map/ppermute | solution.py:37
  284.7 6.2 %collective-permute-start.21 = (f32[17,256]{1,0:T(8,128)S(1)}, f32[17,256]{1,0:T(8,128)S(1)}, u32[]{:S(2)}, u32[]{:S(2)}) collective-permute-start(f32[17,256]{1,0:T(8,128)S(1)} %fusion.53), channel_id=1, source_target_pairs={{0,32},{16,48},{32,0},{48,16},{64,96},{80,112},{96,64},{112,80},{1... | collective-permute-start | bytes 52232 | tf_op jit(solution)/shard_map/ppermute | solution.py:47
  292.7 3.4 %collective-permute-start.22 = (f32[17,256]{1,0:T(8,128)S(1)}, f32[17,256]{1,0:T(8,128)S(1)}, u32[]{:S(2)}, u32[]{:S(2)}) collective-permute-start(f32[17,256]{1,0:T(8,128)S(1)} %add.178), channel_id=1, source_target_pairs={{0,64},{16,80},{32,96},{48,112},{64,0},{80,16},{96,32},{112,48},{1... | collective-permute-start | bytes 52232 | tf_op jit(solution)/shard_map/ppermute | solution.py:47
  296.2 3.2 collective-permute-done.22
  299.3 4.2 %collective-permute-start.23 = (f32[17,256]{1,0:T(8,128)S(1)}, f32[17,256]{1,0:T(8,128)S(1)}, u32[]{:S(2)}, u32[]{:S(2)}) collective-permute-start(f32[17,256]{1,0:T(8,128)S(1)} %add.179), channel_id=1, source_target_pairs={{0,128},{16,144},{32,160},{48,176},{64,192},{80,208},{96,224},{112... | collective-permute-start | bytes 52232 | tf_op jit(solution)/shard_map/ppermute | solution.py:47
  303.6 5.1 %collective-permute-start.15 = (bf16[64,256]{1,0:T(8,128)(2,1)S(1)}, bf16[64,256]{1,0:T(8,128)(2,1)S(1)}, u32[]{:S(2)}, u32[]{:S(2)}) collective-permute-start(bf16[64,256]{1,0:T(8,128)(2,1)S(1)} %fusion.40), channel_id=1, source_target_pairs={{0,2},{1,3},{2,0},{3,1},{4,6},{5,7},{6,4},{7,5},{8,10},{9,11},{10,... | collective-permute-start | bytes 98312 | tf_op jit(solution)/shard_map/ppermute | solution.py:37
  309.0 13.6 %collective-permute-start.24 = (f32[17,256]{1,0:T(8,128)S(1)}, f32[17,256]{1,0:T(8,128)S(1)}, u32[]{:S(2)}, u32[]{:S(2)}) collective-permute-start(f32[17,256]{1,0:T(8,128)S(1)} %add.180), channel_id=1, source_target_pairs={{0,256},{16,272},{32,288},{48,304},{64,320},{80,336},{96,352},{112... | collective-permute-start | bytes 52232 | tf_op jit(solution)/shard_map/ppermute | solution.py:47
  (92 shorter events, 36.9 us)
Async XLA Ops:
  0.6 94.0 %copy-start = (bf16[256,256]{1,0:T(8,128)(2,1)S(1)}, bf16[256,256]{1,0:T(8,128)(2,1)}, u32[]{:S(2)}) copy-start(bf16[256,256]{1,0:T(8,128)(2,1)} %param.9) | copy-start | bytes 393220
  23.9 42.0 %collective-permute-start.2 = (bf16[512,256]{1,0:T(8,128)(2,1)S(1)}, bf16[512,256]{1,0:T(8,128)(2,1)S(1)}, u32[]{:S(2)}, u32[]{:S(2)}) collective-permute-start(bf16[512,256]{1,0:T(8,128)(2,1)S(1)} %get-tuple-element.10), channel_id=1, source_target_pairs={{256,0},{241,1},{226,2},{211,3},{196,4},{181,5},{166,6},{151,7},{1... | collective-permute-start | bytes 786440 | tf_op jit(solution)/shard_map/ppermute | solution.py:89
  35.3 58.6 %collective-permute-start = (bf16[512,256]{1,0:T(8,128)(2,1)S(1)}, bf16[512,256]{1,0:T(8,128)(2,1)S(1)}, u32[]{:S(2)}, u32[]{:S(2)}) collective-permute-start(bf16[512,256]{1,0:T(8,128)(2,1)S(1)} %get-tuple-element.10), channel_id=1, source_target_pairs={{0,0},{497,1},{482,2},{467,3},{452,4},{437,5},{422,6},{407,7},{392... | collective-permute-start | bytes 786440 | tf_op jit(solution)/shard_map/ppermute | solution.py:89
  37.2 55.0 %collective-permute-start.3 = (bf16[512,256]{1,0:T(8,128)(2,1)S(1)}, bf16[512,256]{1,0:T(8,128)(2,1)}, u32[]{:S(2)}, u32[]{:S(2)}) collective-permute-start(bf16[512,256]{1,0:T(8,128)(2,1)S(1)} %get-tuple-element.11), channel_id=1, source_target_pairs={{271,0},{254,1},{237,2},{220,3},{203,4},{186,5},{169,6},{152,7},{1... | collective-permute-start | bytes 786440 | tf_op jit(solution)/shard_map/ppermute | solution.py:89
  46.0 47.9 %collective-permute-start.1 = (bf16[512,256]{1,0:T(8,128)(2,1)S(1)}, bf16[512,256]{1,0:T(8,128)(2,1)S(1)}, u32[]{:S(2)}, u32[]{:S(2)}) collective-permute-start(bf16[512,256]{1,0:T(8,128)(2,1)S(1)} %get-tuple-element.11), channel_id=1, source_target_pairs={{15,0},{510,1},{493,2},{476,3},{459,4},{442,5},{425,6},{408,7},{39... | collective-permute-start | bytes 786440 | tf_op jit(solution)/shard_map/ppermute | solution.py:89
  50.7 4.1 %copy-start.8 = (s32[1,1,2,64]{3,2,1,0:T(2,128)S(1)}, s32[1,1,2,64]{3,2,1,0:T(2,128)}, u32[]{:S(2)}) copy-start(s32[1,1,2,64]{3,2,1,0:T(2,128)} %param.14) | copy-start | bytes 1540
  50.7 4.1 %copy-start.9 = (s32[1,1,2,64]{3,2,1,0:T(2,128)S(1)}, s32[1,1,2,64]{3,2,1,0:T(2,128)}, u32[]{:S(2)}) copy-start(s32[1,1,2,64]{3,2,1,0:T(2,128)} %param.13) | copy-start | bytes 1540
  58.1 35.8 %copy-start.1 = (bf16[64,16384]{1,0:T(8,128)(2,1)}, bf16[64,16384]{1,0:T(8,128)(2,1)S(1)}, u32[]{:S(2)}) copy-start(bf16[64,16384]{1,0:T(8,128)(2,1)S(1)} %convolution_convert_fusion.1) | copy-start | bytes 6291460
  59.8 34.1 %copy-start.3 = (bf16[64,16384]{1,0:T(8,128)(2,1)}, bf16[64,16384]{1,0:T(8,128)(2,1)S(1)}, u32[]{:S(2)}) copy-start(bf16[64,16384]{1,0:T(8,128)(2,1)S(1)} %convolution_convert_fusion) | copy-start | bytes 6291460
  95.3 43.6 %copy-start.7 = (f32[256]{0:T(256)S(1)}, f32[256]{0:T(256)}, u32[]{:S(2)}) copy-start(f32[256]{0:T(256)} %param.10) | copy-start | bytes 3076
  95.3 3.4 %collective-permute-start.4 = (bf16[2,2,2,64,256]{4,3,2,0,1:T(8,128)(2,1)S(1)}, bf16[2,2,2,64,256]{4,3,2,0,1:T(8,128)(2,1)S(1)}, u32[]{:S(2)}, u32[]{:S(2)}) collective-permute-start(bf16[2,2,2,64,256]{4,3,2,0,1:T(8,128)(2,1)S(1)} %fusion.32), channel_id=1, source_target_pairs={{0,1},{1,0},{2,3},{3,2},{4,5},{5,4},{6,7},{7,6},{8,9},{9,8},{10,11... | collective-permute-start | bytes 786440 | tf_op jit(solution)/shard_map/ppermute | solution.py:37
  99.6 63.4 %copy-start.4 = (bf16[64,16384]{1,0:T(8,128)(2,1)S(1)}, bf16[64,16384]{1,0:T(8,128)(2,1)}, u32[]{:S(2)}) copy-start(bf16[64,16384]{1,0:T(8,128)(2,1)} %copy-done.3) | copy-start | bytes 6291460
  99.6 7.7 %collective-permute-start.5 = (bf16[2,2,64,256]{3,2,1,0:T(8,128)(2,1)S(1)}, bf16[2,2,64,256]{3,2,1,0:T(8,128)(2,1)}, u32[]{:S(2)}, u32[]{:S(2)}) collective-permute-start(bf16[2,2,64,256]{3,2,1,0:T(8,128)(2,1)S(1)} %fusion.33), channel_id=1, source_target_pairs={{0,4},{1,5},{2,6},{3,7},{4,0},{5,1},{6,2},{7,3},{8,12},{9,13},{10,... | collective-permute-start | bytes 393224 | tf_op jit(solution)/shard_map/ppermute | solution.py:37
  109.0 18.1 %collective-permute-start.6 = (bf16[2,64,256]{2,1,0:T(8,128)(2,1)}, bf16[2,64,256]{2,1,0:T(8,128)(2,1)}, u32[]{:S(2)}, u32[]{:S(2)}) collective-permute-start(bf16[2,64,256]{2,1,0:T(8,128)(2,1)} %fusion.35), channel_id=1, source_target_pairs={{0,8},{1,9},{2,10},{3,11},{4,12},{5,13},{6,14},{7,15},{8,0},{9,1},... | collective-permute-start | bytes 196616 | tf_op jit(solution)/shard_map/ppermute | solution.py:37
  128.6 10.3 %collective-permute-start.7 = (bf16[64,256]{1,0:T(8,128)(2,1)S(1)}, bf16[64,256]{1,0:T(8,128)(2,1)S(1)}, u32[]{:S(2)}, u32[]{:S(2)}) collective-permute-start(bf16[64,256]{1,0:T(8,128)(2,1)S(1)} %fusion.39), channel_id=1, source_target_pairs={{0,2},{1,3},{2,0},{3,1},{4,6},{5,7},{6,4},{7,5},{8,10},{9,11},{10,... | collective-permute-start | bytes 98312 | tf_op jit(solution)/shard_map/ppermute | solution.py:37
  166.5 3.2 collective-permute-start.16
  169.8 22.0 %collective-permute-start.17 = (f32[2,2,16,256]{3,2,1,0:T(8,128)S(1)}, f32[2,2,16,256]{3,2,1,0:T(8,128)S(1)}, u32[]{:S(2)}, u32[]{:S(2)}) collective-permute-start(f32[2,2,16,256]{3,2,1,0:T(8,128)S(1)} %dynamic-slice_bitcast_fusion.1), channel_id=1, source_target_pairs={{0,4},{1,5},{2,6},{3,7},{4,0},{5,1},{6,2},{7,3},{8,12},{9,13},{10,... | collective-permute-start | bytes 196616 | tf_op jit(solution)/shard_map/ppermute | solution.py:37
  172.3 30.4 %collective-permute-start.9 = (bf16[512,256]{1,0:T(8,128)(2,1)S(1)}, bf16[512,256]{1,0:T(8,128)(2,1)S(1)}, u32[]{:S(2)}, u32[]{:S(2)}) collective-permute-start(bf16[512,256]{1,0:T(8,128)(2,1)S(1)} %get-tuple-element.8), channel_id=1, source_target_pairs={{0,256},{1,241},{2,226},{3,211},{4,196},{5,181},{6,166},{7,151},{8... | collective-permute-start | bytes 786440 | tf_op jit(solution)/shard_map/ppermute | solution.py:136
  174.2 86.0 %collective-permute-start.11 = (bf16[512,256]{1,0:T(8,128)(2,1)S(1)}, bf16[512,256]{1,0:T(8,128)(2,1)S(1)}, u32[]{:S(2)}, u32[]{:S(2)}) collective-permute-start(bf16[512,256]{1,0:T(8,128)(2,1)S(1)} %get-tuple-element.9), channel_id=1, source_target_pairs={{0,271},{1,254},{2,237},{3,220},{4,203},{5,186},{6,169},{7,152},{8... | collective-permute-start | bytes 786440 | tf_op jit(solution)/shard_map/ppermute | solution.py:136
  185.7 46.4 %collective-permute-start.8 = (bf16[512,256]{1,0:T(8,128)(2,1)S(1)}, bf16[512,256]{1,0:T(8,128)(2,1)S(1)}, u32[]{:S(2)}, u32[]{:S(2)}) collective-permute-start(bf16[512,256]{1,0:T(8,128)(2,1)S(1)} %get-tuple-element.6), channel_id=1, source_target_pairs={{0,0},{1,497},{2,482},{3,467},{4,452},{5,437},{6,422},{7,407},{8,3... | collective-permute-start | bytes 786440 | tf_op jit(solution)/shard_map/ppermute | solution.py:136
  188.4 71.8 %collective-permute-start.10 = (bf16[512,256]{1,0:T(8,128)(2,1)S(1)}, bf16[512,256]{1,0:T(8,128)(2,1)S(1)}, u32[]{:S(2)}, u32[]{:S(2)}) collective-permute-start(bf16[512,256]{1,0:T(8,128)(2,1)S(1)} %get-tuple-element.7), channel_id=1, source_target_pairs={{0,15},{1,510},{2,493},{3,476},{4,459},{5,442},{6,425},{7,408},{8,... | collective-permute-start | bytes 786440 | tf_op jit(solution)/shard_map/ppermute | solution.py:136
  191.9 70.5 %collective-permute-start.18 = (f32[2,16,256]{2,1,0:T(8,128)S(1)}, f32[2,16,256]{2,1,0:T(8,128)S(1)}, u32[]{:S(2)}, u32[]{:S(2)}) collective-permute-start(f32[2,16,256]{2,1,0:T(8,128)S(1)} %dynamic-slice_bitcast_fusion.2), channel_id=1, source_target_pairs={{0,8},{1,9},{2,10},{3,11},{4,12},{5,13},{6,14},{7,15},{8,0},{9,1},... | collective-permute-start | bytes 98312 | tf_op jit(solution)/shard_map/ppermute | solution.py:37
  260.4 3.9 %collective-permute-start.12 = (bf16[2,2,2,64,256]{4,3,2,1,0:T(8,128)(2,1)S(1)}, bf16[2,2,2,64,256]{4,3,2,1,0:T(8,128)(2,1)S(1)}, u32[]{:S(2)}, u32[]{:S(2)}) collective-permute-start(bf16[2,2,2,64,256]{4,3,2,1,0:T(8,128)(2,1)S(1)} %fusion.31), channel_id=1, source_target_pairs={{0,1},{1,0},{2,3},{3,2},{4,5},{5,4},{6,7},{7,6},{8,9},{9,8},{10,11... | collective-permute-start | bytes 786440 | tf_op jit(solution)/shard_map/ppermute | solution.py:37
  262.4 7.1 %collective-permute-start.19 = (f32[16,256]{1,0:T(8,128)S(1)}, f32[16,256]{1,0:T(8,128)S(1)}, u32[]{:S(2)}, u32[]{:S(2)}) collective-permute-start(f32[16,256]{1,0:T(8,128)S(1)} %dynamic-slice_bitcast_fusion.3), channel_id=1, source_target_pairs={{0,2},{1,3},{2,0},{3,1},{4,6},{5,7},{6,4},{7,5},{8,10},{9,11},{10,... | collective-permute-start | bytes 49160 | tf_op jit(solution)/shard_map/ppermute | solution.py:37
  264.4 7.8 %collective-permute-start.13 = (bf16[2,2,64,256]{3,2,1,0:T(8,128)(2,1)S(1)}, bf16[2,2,64,256]{3,2,1,0:T(8,128)(2,1)S(1)}, u32[]{:S(2)}, u32[]{:S(2)}) collective-permute-start(bf16[2,2,64,256]{3,2,1,0:T(8,128)(2,1)S(1)} %fusion.34), channel_id=1, source_target_pairs={{0,4},{1,5},{2,6},{3,7},{4,0},{5,1},{6,2},{7,3},{8,12},{9,13},{10,... | collective-permute-start | bytes 393224 | tf_op jit(solution)/shard_map/ppermute | solution.py:37
  269.5 15.1 %collective-permute-start.20 = (f32[17,256]{1,0:T(8,128)S(1)}, f32[17,256]{1,0:T(8,128)S(1)}, u32[]{:S(2)}, u32[]{:S(2)}) collective-permute-start(f32[17,256]{1,0:T(8,128)S(1)} %pad_maximum_fusion.1), channel_id=1, source_target_pairs={{0,16},{16,0},{32,48},{48,32},{64,80},{80,64},{96,112},{112,96},{1... | collective-permute-start | bytes 52232 | tf_op jit(solution)/shard_map/ppermute | solution.py:47
  272.3 31.2 %collective-permute-start.14 = (bf16[2,64,256]{2,1,0:T(8,128)(2,1)S(1)}, bf16[2,64,256]{2,1,0:T(8,128)(2,1)S(1)}, u32[]{:S(2)}, u32[]{:S(2)}) collective-permute-start(bf16[2,64,256]{2,1,0:T(8,128)(2,1)S(1)} %fusion.36), channel_id=1, source_target_pairs={{0,8},{1,9},{2,10},{3,11},{4,12},{5,13},{6,14},{7,15},{8,0},{9,1},... | collective-permute-start | bytes 196616 | tf_op jit(solution)/shard_map/ppermute | solution.py:37
  284.7 8.0 %collective-permute-start.21 = (f32[17,256]{1,0:T(8,128)S(1)}, f32[17,256]{1,0:T(8,128)S(1)}, u32[]{:S(2)}, u32[]{:S(2)}) collective-permute-start(f32[17,256]{1,0:T(8,128)S(1)} %fusion.53), channel_id=1, source_target_pairs={{0,32},{16,48},{32,0},{48,16},{64,96},{80,112},{96,64},{112,80},{1... | collective-permute-start | bytes 52232 | tf_op jit(solution)/shard_map/ppermute | solution.py:47
  292.7 6.6 %collective-permute-start.22 = (f32[17,256]{1,0:T(8,128)S(1)}, f32[17,256]{1,0:T(8,128)S(1)}, u32[]{:S(2)}, u32[]{:S(2)}) collective-permute-start(f32[17,256]{1,0:T(8,128)S(1)} %add.178), channel_id=1, source_target_pairs={{0,64},{16,80},{32,96},{48,112},{64,0},{80,16},{96,32},{112,48},{1... | collective-permute-start | bytes 52232 | tf_op jit(solution)/shard_map/ppermute | solution.py:47
  299.3 9.6 %collective-permute-start.23 = (f32[17,256]{1,0:T(8,128)S(1)}, f32[17,256]{1,0:T(8,128)S(1)}, u32[]{:S(2)}, u32[]{:S(2)}) collective-permute-start(f32[17,256]{1,0:T(8,128)S(1)} %add.179), channel_id=1, source_target_pairs={{0,128},{16,144},{32,160},{48,176},{64,192},{80,208},{96,224},{112... | collective-permute-start | bytes 52232 | tf_op jit(solution)/shard_map/ppermute | solution.py:47
  303.6 21.9 %collective-permute-start.15 = (bf16[64,256]{1,0:T(8,128)(2,1)S(1)}, bf16[64,256]{1,0:T(8,128)(2,1)S(1)}, u32[]{:S(2)}, u32[]{:S(2)}) collective-permute-start(bf16[64,256]{1,0:T(8,128)(2,1)S(1)} %fusion.40), channel_id=1, source_target_pairs={{0,2},{1,3},{2,0},{3,1},{4,6},{5,7},{6,4},{7,5},{8,10},{9,11},{10,... | collective-permute-start | bytes 98312 | tf_op jit(solution)/shard_map/ppermute | solution.py:37
  309.0 15.4 %collective-permute-start.24 = (f32[17,256]{1,0:T(8,128)S(1)}, f32[17,256]{1,0:T(8,128)S(1)}, u32[]{:S(2)}, u32[]{:S(2)}) collective-permute-start(f32[17,256]{1,0:T(8,128)S(1)} %add.180), channel_id=1, source_target_pairs={{0,256},{16,272},{32,288},{48,304},{64,320},{80,336},{96,352},{112... | collective-permute-start | bytes 52232 | tf_op jit(solution)/shard_map/ppermute | solution.py:47
  (3 other events, 3.0 us)

commit v5 on v4

--- a/solution.py
+++ b/solution.py
@@ -124,7 +124,7 @@
     weight_part = rep_reduce_scatter(weight_terms, jnp.float32)
     bias_part = jnp.sum(grad_block.astype(jnp.float32), axis=0)
     totals = blk_all_reduce(jnp.concatenate([weight_part, bias_part[None, :]], axis=0))
-    returned = [jnp.zeros((half_rows, partition.shape[1]), jnp.float32) for _ in range(2)]
+    arrived = []
     for slot in range(pair_slots):
         partial = lax.dot_general(
             adjacency[slot],
@@ -133,12 +133,17 @@
             preferred_element_type=jnp.float32,
         ).astype(jnp.bfloat16)
         for half in range(2):
-            got = lax.ppermute(
-                partial[half * half_rows:(half + 1) * half_rows],
-                both_axes,
-                source_pairs(blocks, replicas, slot, half, True),
+            arrived.append(
+                lax.ppermute(
+                    partial[half * half_rows:(half + 1) * half_rows],
+                    both_axes,
+                    source_pairs(blocks, replicas, slot, half, True),
+                )
             )
-            returned[half] = returned[half] + got.astype(jnp.float32)
+    arrived, totals = lax.optimization_barrier((arrived, totals))
+    returned = [jnp.zeros((half_rows, partition.shape[1]), jnp.float32) for _ in range(2)]
+    for index, got in enumerate(arrived):
+        returned[index % 2] = returned[index % 2] + got.astype(jnp.float32)
     partial_grad = jnp.concatenate(returned, axis=0)
     grad_hw = rep_reduce_scatter(partial_grad, jnp.bfloat16).astype(jnp.bfloat16)
     grad_feats = lax.dot_general(

time: 328 us -> 351 us (1.070); the launches traced: 326 us -> 345 us
  waiting for transfers between devices: 113 us -> 156 us
  starting transfers between devices: 140 us -> 117 us
    ppermute x5, waiting for transfers between devices: 6.97 us -> 84.7 us  [blk_all_reduce(): x = x + lax.ppermute(x, 'blk', [(i, i ^ step) for i in range(blocks)])]
    ppermute x4, waiting for transfers between devices: 57.5 us -> 0.01 us  [body(): lax.ppermute(partial[half * half_rows:(half + 1) * half_rows], both_axes,...]
    ppermute x12, waiting for transfers between devices: 15.7 us -> 38.5 us  [rep_reduce_scatter(): got = lax.ppermute(send.astype(wire_dtype), 'rep', partner)]
    ppermute x12, starting transfers between devices: 66.6 us -> 48 us  [rep_reduce_scatter(): got = lax.ppermute(send.astype(wire_dtype), 'rep', partner)]
    ppermute x5, starting transfers between devices: 30 us -> 16.8 us  [blk_all_reduce(): x = x + lax.ppermute(x, 'blk', [(i, i ^ step) for i in range(blocks)])]
    ppermute x4, starting transfers between devices: 19.5 us -> 28.2 us  [body(): lax.ppermute(partial[half * half_rows:(half + 1) * half_rows], both_axes,...]
  transfers between devices with their start and end apart: 25 -> 25, of which waited for: 14 -> 18; matrix products, arithmetic and copies ran while one was open for 5% -> 5% of each run, Pallas kernels for 0% -> 0%
where the time goes in v5:
time: 351 us; the launch traced here: 345 us
  waiting for transfers between devices  156 us (44%)
  starting transfers between devices  117 us (33%)
  blocking collectives  45.8 us (13%)
  matrix products  11.4 us (3%)
  local copies, waits for them, and re-layouts  8.95 us (3%)
  other arithmetic  5.29 us (2%)
    ppermute x5, waiting for transfers between devices, blk_all_reduce(): x = x + lax.ppermute(x, 'blk', [(i, i ^ step) for i in range(blocks)])  84.7 us
    ppermute x12, starting transfers between devices, rep_reduce_scatter(): got = lax.ppermute(send.astype(wire_dtype), 'rep', partner)  48 us
    ppermute x12, waiting for transfers between devices, rep_reduce_scatter(): got = lax.ppermute(send.astype(wire_dtype), 'rep', partner)  38.5 us
    ppermute x4, waiting for transfers between devices, body(): lax.ppermute(partition[half * half_rows:(half + 1) * half_rows], both_axe...  32.4 us
    ppermute x4, starting transfers between devices, body(): lax.ppermute(partial[half * half_rows:(half + 1) * half_rows], both_axes,...  28.2 us
    ppermute x4, starting transfers between devices, body(): lax.ppermute(partition[half * half_rows:(half + 1) * half_rows], both_axe...  24.2 us
    all_gather x1, blocking collectives, body(): partition = lax.all_gather(feats, 'rep', axis=0, tiled=True)  23.2 us
    all_gather x1, blocking collectives, body(): grad_block = lax.all_gather(grad_rows, 'rep', axis=0, tiled=True)  22.6 us
  transfers between devices with their start and end apart: 25, of which 18 were waited for; matrix products, arithmetic and copies ran while one was open for 5% of the time, Pallas kernels for 0%

profile of v5, /device:TPU:6, one launch (start us, length us, event | category | flops | bytes accessed | tf_op | source)
XLA Modules:
  0.0 345.4 jit_solution(8976168975441101022)
XLA Ops:
  0.6 23.2 %all_gather.6 = bf16[1024,256]{1,0:T(8,128)(2,1)S(1)} all-gather(bf16[64,256]{1,0:T(8,128)(2,1)} %param.8), channel_id=1, replica_groups=mesh['blk'=32,'rep'=16] {'rep'}, dimensions={0}, use_global_device_ids=true | all-gather | bytes 557056 | tf_op jit(solution)/shard_map/all_gather | solution.py:81
  23.9 11.4 %collective-permute-start.2 = (bf16[512,256]{1,0:T(8,128)(2,1)S(1)}, bf16[512,256]{1,0:T(8,128)(2,1)S(1)}, u32[]{:S(2)}, u32[]{:S(2)}) collective-permute-start(bf16[512,256]{1,0:T(8,128)(2,1)S(1)} %get-tuple-element.20), channel_id=1, source_target_pairs={{256,0},{241,1},{226,2},{211,3},{196,4},{181,5},{166,6},{151,7},{1... | collective-permute-start | bytes 786440 | tf_op jit(solution)/shard_map/ppermute | solution.py:89
  37.2 8.8 %collective-permute-start.3 = (bf16[512,256]{1,0:T(8,128)(2,1)S(1)}, bf16[512,256]{1,0:T(8,128)(2,1)}, u32[]{:S(2)}, u32[]{:S(2)}) collective-permute-start(bf16[512,256]{1,0:T(8,128)(2,1)S(1)} %get-tuple-element.21), channel_id=1, source_target_pairs={{271,0},{254,1},{237,2},{220,3},{203,4},{186,5},{169,6},{152,7},{1... | collective-permute-start | bytes 786440 | tf_op jit(solution)/shard_map/ppermute | solution.py:89
  50.7 4.0 %fusion.54 = (bf16[1,1,1,64,128,128]{5,4,3,2,1,0:T(8,128)(2,1)}, bf16[1,1,1,64,128,128]{5,4,3,2,1,0:T(8,128)(2,1)S(1)}) fusion(bf16[1,1,2,64,128,128]{5,4,3,2,1,0:T(8,128)(2,1)} %param.12), kind=kLoop, calls=%fused_computation.88 | loop fusion | bytes 8388608 | tf_op jit(solution)/shard_map/slice | solution.py:99
  54.8 3.3 convolution_convert_fusion.1
  59.8 6.1 %collective-permute-done.2 = bf16[512,256]{1,0:T(8,128)(2,1)S(1)} collective-permute-done((bf16[512,256]{1,0:T(8,128)(2,1)S(1)}, bf16[512,256]{1,0:T(8,128)(2,1)S(1)}, u32[]{:S(2)}, u32[]{:S(2)}) %collective-permute-start.2) | collective-permute-done | bytes 262176 | tf_op jit(solution)/shard_map/ppermute | solution.py:89
  65.9 26.3 %collective-permute-done.3 = bf16[512,256]{1,0:T(8,128)(2,1)} collective-permute-done((bf16[512,256]{1,0:T(8,128)(2,1)S(1)}, bf16[512,256]{1,0:T(8,128)(2,1)}, u32[]{:S(2)}, u32[]{:S(2)}) %collective-permute-start.3) | collective-permute-done | bytes 262176 | tf_op jit(solution)/shard_map/ppermute | solution.py:89
  99.7 2.1 collective-permute-start.5
  101.7 5.6 %collective-permute-done.5 = bf16[2,2,64,256]{3,2,1,0:T(8,128)(2,1)} collective-permute-done((bf16[2,2,64,256]{3,2,1,0:T(8,128)(2,1)S(1)}, bf16[2,2,64,256]{3,2,1,0:T(8,128)(2,1)}, u32[]{:S(2)}, u32[]{:S(2)}) %collective-permute-start.5) | collective-permute-done | bytes 131104 | tf_op jit(solution)/shard_map/ppermute | solution.py:37
  109.0 15.6 %collective-permute-start.6 = (bf16[2,64,256]{2,1,0:T(8,128)(2,1)}, bf16[2,64,256]{2,1,0:T(8,128)(2,1)}, u32[]{:S(2)}, u32[]{:S(2)}) collective-permute-start(bf16[2,64,256]{2,1,0:T(8,128)(2,1)} %fusion.35), channel_id=1, source_target_pairs={{0,8},{1,9},{2,10},{3,11},{4,12},{5,13},{6,14},{7,15},{8,0},{9,1},... | collective-permute-start | bytes 196616 | tf_op jit(solution)/shard_map/ppermute | solution.py:37
  124.6 2.5 collective-permute-done.6
  128.6 8.4 %collective-permute-start.7 = (bf16[64,256]{1,0:T(8,128)(2,1)S(1)}, bf16[64,256]{1,0:T(8,128)(2,1)S(1)}, u32[]{:S(2)}, u32[]{:S(2)}) collective-permute-start(bf16[64,256]{1,0:T(8,128)(2,1)S(1)} %fusion.39), channel_id=1, source_target_pairs={{0,2},{1,3},{2,0},{3,1},{4,6},{5,7},{6,4},{7,5},{8,10},{9,11},{10,... | collective-permute-start | bytes 98312 | tf_op jit(solution)/shard_map/ppermute | solution.py:37
  140.4 22.6 %all_gather.7 = bf16[1024,256]{1,0:T(8,128)(2,1)S(1)} all-gather(bf16[64,256]{1,0:T(8,128)(2,1)S(1)} %get-tuple-element.22), channel_id=1, replica_groups=mesh['blk'=32,'rep'=16] {'rep'}, dimensions={0}, use_global_device_ids=true | all-gather | bytes 557056 | tf_op jit(solution)/shard_map/all_gather | solution.py:116
  164.1 2.4 collective-permute-start.12
  167.5 2.3 collective-permute-start.13
  170.6 3.2 collective-permute-done.13
  173.8 5.5 %collective-permute-start.14 = (f32[2,16,256]{2,1,0:T(8,128)S(1)}, f32[2,16,256]{2,1,0:T(8,128)S(1)}, u32[]{:S(2)}, u32[]{:S(2)}) collective-permute-start(f32[2,16,256]{2,1,0:T(8,128)S(1)} %dynamic-slice_bitcast_fusion.2), channel_id=1, source_target_pairs={{0,8},{1,9},{2,10},{3,11},{4,12},{5,13},{6,14},{7,15},{8,0},{9,1},... | collective-permute-start | bytes 98312 | tf_op jit(solution)/shard_map/ppermute | solution.py:37
  181.3 2.1 collective-permute-start.15
  183.6 4.8 %collective-permute-done.15 = f32[16,256]{1,0:T(8,128)S(1)} collective-permute-done((f32[16,256]{1,0:T(8,128)S(1)}, f32[16,256]{1,0:T(8,128)S(1)}, u32[]{:S(2)}, u32[]{:S(2)}) %collective-permute-start.15) | collective-permute-done | bytes 16416 | tf_op jit(solution)/shard_map/ppermute | solution.py:37
  192.4 3.1 collective-permute-start.10
  195.5 19.2 %collective-permute-start.9 = (bf16[512,256]{1,0:T(8,128)(2,1)S(1)}, bf16[512,256]{1,0:T(8,128)(2,1)S(1)}, u32[]{:S(2)}, u32[]{:S(2)}) collective-permute-start(bf16[512,256]{1,0:T(8,128)(2,1)S(1)} %get-tuple-element.18), channel_id=1, source_target_pairs={{0,15},{1,510},{2,493},{3,476},{4,459},{5,442},{6,425},{7,408},{8,... | collective-permute-start | bytes 786440 | tf_op jit(solution)/shard_map/ppermute | solution.py:137
  214.7 4.0 %collective-permute-start.8 = (bf16[512,256]{1,0:T(8,128)(2,1)S(1)}, bf16[512,256]{1,0:T(8,128)(2,1)S(1)}, u32[]{:S(2)}, u32[]{:S(2)}) collective-permute-start(bf16[512,256]{1,0:T(8,128)(2,1)S(1)} %get-tuple-element.19), channel_id=1, source_target_pairs={{0,0},{1,497},{2,482},{3,467},{4,452},{5,437},{6,422},{7,407},{8,3... | collective-permute-start | bytes 786440 | tf_op jit(solution)/shard_map/ppermute | solution.py:137
  218.7 3.8 %collective-permute-start.17 = (f32[17,256]{1,0:T(8,128)S(1)}, f32[17,256]{1,0:T(8,128)S(1)}, u32[]{:S(2)}, u32[]{:S(2)}) collective-permute-start(f32[17,256]{1,0:T(8,128)S(1)} %fusion.53), channel_id=1, source_target_pairs={{0,32},{16,48},{32,0},{48,16},{64,96},{80,112},{96,64},{112,80},{1... | collective-permute-start | bytes 52232 | tf_op jit(solution)/shard_map/ppermute | solution.py:47
  222.6 65.0 %collective-permute-done.17 = f32[17,256]{1,0:T(8,128)S(1)} collective-permute-done((f32[17,256]{1,0:T(8,128)S(1)}, f32[17,256]{1,0:T(8,128)S(1)}, u32[]{:S(2)}, u32[]{:S(2)}) %collective-permute-start.17) | collective-permute-done | bytes 17440 | tf_op jit(solution)/shard_map/ppermute | solution.py:47
  287.6 2.2 collective-permute-start.18
  289.9 4.4 %collective-permute-done.18 = f32[17,256]{1,0:T(8,128)S(1)} collective-permute-done((f32[17,256]{1,0:T(8,128)S(1)}, f32[17,256]{1,0:T(8,128)S(1)}, u32[]{:S(2)}, u32[]{:S(2)}) %collective-permute-start.18) | collective-permute-done | bytes 17440 | tf_op jit(solution)/shard_map/ppermute | solution.py:47
  296.1 7.7 %collective-permute-done.19 = f32[17,256]{1,0:T(8,128)S(1)} collective-permute-done((f32[17,256]{1,0:T(8,128)S(1)}, f32[17,256]{1,0:T(8,128)S(1)}, u32[]{:S(2)}, u32[]{:S(2)}) %collective-permute-start.19) | collective-permute-done | bytes 17440 | tf_op jit(solution)/shard_map/ppermute | solution.py:47
  303.9 6.8 %collective-permute-start.20 = (f32[17,256]{1,0:T(8,128)S(1)}, f32[17,256]{1,0:T(8,128)S(1)}, u32[]{:S(2)}, u32[]{:S(2)}) collective-permute-start(f32[17,256]{1,0:T(8,128)S(1)} %add.174), channel_id=1, source_target_pairs={{0,256},{16,272},{32,288},{48,304},{64,320},{80,336},{96,352},{112... | collective-permute-start | bytes 52232 | tf_op jit(solution)/shard_map/ppermute | solution.py:47
  310.7 7.6 %collective-permute-done.20 = f32[17,256]{1,0:T(8,128)S(1)} collective-permute-done((f32[17,256]{1,0:T(8,128)S(1)}, f32[17,256]{1,0:T(8,128)S(1)}, u32[]{:S(2)}, u32[]{:S(2)}) %collective-permute-start.20) | collective-permute-done | bytes 17440 | tf_op jit(solution)/shard_map/ppermute | solution.py:47
  324.1 5.5 %collective-permute-done.22 = bf16[2,2,64,256]{3,2,1,0:T(8,128)(2,1)S(1)} collective-permute-done((bf16[2,2,64,256]{3,2,1,0:T(8,128)(2,1)S(1)}, bf16[2,2,64,256]{3,2,1,0:T(8,128)(2,1)S(1)}, u32[]{:S(2)}, u32[]{:S(2)}) %collective-permute-start.22) | collective-permute-done | bytes 131104 | tf_op jit(solution)/shard_map/ppermute | solution.py:37
  331.5 5.7 %collective-permute-done.23 = bf16[2,64,256]{2,1,0:T(8,128)(2,1)S(1)} collective-permute-done((bf16[2,64,256]{2,1,0:T(8,128)(2,1)S(1)}, bf16[2,64,256]{2,1,0:T(8,128)(2,1)S(1)}, u32[]{:S(2)}, u32[]{:S(2)}) %collective-permute-start.23) | collective-permute-done | bytes 65568 | tf_op jit(solution)/shard_map/ppermute | solution.py:37
  340.4 4.2 %collective-permute-done.24 = bf16[64,256]{1,0:T(8,128)(2,1)S(1)} collective-permute-done((bf16[64,256]{1,0:T(8,128)(2,1)S(1)}, bf16[64,256]{1,0:T(8,128)(2,1)S(1)}, u32[]{:S(2)}, u32[]{:S(2)}) %collective-permute-start.24) | collective-permute-done | bytes 32800 | tf_op jit(solution)/shard_map/ppermute | solution.py:37
  (91 shorter events, 44.6 us)
Async XLA Ops:
  0.6 94.0 %copy-start = (bf16[256,256]{1,0:T(8,128)(2,1)S(1)}, bf16[256,256]{1,0:T(8,128)(2,1)}, u32[]{:S(2)}) copy-start(bf16[256,256]{1,0:T(8,128)(2,1)} %param.9) | copy-start | bytes 393220
  23.9 42.0 %collective-permute-start.2 = (bf16[512,256]{1,0:T(8,128)(2,1)S(1)}, bf16[512,256]{1,0:T(8,128)(2,1)S(1)}, u32[]{:S(2)}, u32[]{:S(2)}) collective-permute-start(bf16[512,256]{1,0:T(8,128)(2,1)S(1)} %get-tuple-element.20), channel_id=1, source_target_pairs={{256,0},{241,1},{226,2},{211,3},{196,4},{181,5},{166,6},{151,7},{1... | collective-permute-start | bytes 786440 | tf_op jit(solution)/shard_map/ppermute | solution.py:89
  35.3 58.6 %collective-permute-start = (bf16[512,256]{1,0:T(8,128)(2,1)S(1)}, bf16[512,256]{1,0:T(8,128)(2,1)S(1)}, u32[]{:S(2)}, u32[]{:S(2)}) collective-permute-start(bf16[512,256]{1,0:T(8,128)(2,1)S(1)} %get-tuple-element.20), channel_id=1, source_target_pairs={{0,0},{497,1},{482,2},{467,3},{452,4},{437,5},{422,6},{407,7},{392... | collective-permute-start | bytes 786440 | tf_op jit(solution)/shard_map/ppermute | solution.py:89
  37.2 55.0 %collective-permute-start.3 = (bf16[512,256]{1,0:T(8,128)(2,1)S(1)}, bf16[512,256]{1,0:T(8,128)(2,1)}, u32[]{:S(2)}, u32[]{:S(2)}) collective-permute-start(bf16[512,256]{1,0:T(8,128)(2,1)S(1)} %get-tuple-element.21), channel_id=1, source_target_pairs={{271,0},{254,1},{237,2},{220,3},{203,4},{186,5},{169,6},{152,7},{1... | collective-permute-start | bytes 786440 | tf_op jit(solution)/shard_map/ppermute | solution.py:89
  46.0 47.9 %collective-permute-start.1 = (bf16[512,256]{1,0:T(8,128)(2,1)S(1)}, bf16[512,256]{1,0:T(8,128)(2,1)S(1)}, u32[]{:S(2)}, u32[]{:S(2)}) collective-permute-start(bf16[512,256]{1,0:T(8,128)(2,1)S(1)} %get-tuple-element.21), channel_id=1, source_target_pairs={{15,0},{510,1},{493,2},{476,3},{459,4},{442,5},{425,6},{408,7},{39... | collective-permute-start | bytes 786440 | tf_op jit(solution)/shard_map/ppermute | solution.py:89
  50.7 4.1 %copy-start.8 = (s32[1,1,2,64]{3,2,1,0:T(2,128)S(1)}, s32[1,1,2,64]{3,2,1,0:T(2,128)}, u32[]{:S(2)}) copy-start(s32[1,1,2,64]{3,2,1,0:T(2,128)} %param.14) | copy-start | bytes 1540
  58.1 35.9 %copy-start.1 = (bf16[64,16384]{1,0:T(8,128)(2,1)}, bf16[64,16384]{1,0:T(8,128)(2,1)S(1)}, u32[]{:S(2)}) copy-start(bf16[64,16384]{1,0:T(8,128)(2,1)S(1)} %convolution_convert_fusion.1) | copy-start | bytes 6291460
  59.8 34.1 %copy-start.3 = (bf16[64,16384]{1,0:T(8,128)(2,1)}, bf16[64,16384]{1,0:T(8,128)(2,1)S(1)}, u32[]{:S(2)}) copy-start(bf16[64,16384]{1,0:T(8,128)(2,1)S(1)} %convolution_convert_fusion) | copy-start | bytes 6291460
  95.3 43.6 %copy-start.7 = (f32[256]{0:T(256)S(1)}, f32[256]{0:T(256)}, u32[]{:S(2)}) copy-start(f32[256]{0:T(256)} %param.10) | copy-start | bytes 3076
  95.3 3.4 collective-permute-start.4
  99.6 66.9 %copy-start.4 = (bf16[64,16384]{1,0:T(8,128)(2,1)S(1)}, bf16[64,16384]{1,0:T(8,128)(2,1)}, u32[]{:S(2)}) copy-start(bf16[64,16384]{1,0:T(8,128)(2,1)} %copy-done.3) | copy-start | bytes 6291460
  99.7 7.7 %collective-permute-start.5 = (bf16[2,2,64,256]{3,2,1,0:T(8,128)(2,1)S(1)}, bf16[2,2,64,256]{3,2,1,0:T(8,128)(2,1)}, u32[]{:S(2)}, u32[]{:S(2)}) collective-permute-start(bf16[2,2,64,256]{3,2,1,0:T(8,128)(2,1)S(1)} %fusion.33), channel_id=1, source_target_pairs={{0,4},{1,5},{2,6},{3,7},{4,0},{5,1},{6,2},{7,3},{8,12},{9,13},{10,... | collective-permute-start | bytes 393224 | tf_op jit(solution)/shard_map/ppermute | solution.py:37
  109.0 18.1 %collective-permute-start.6 = (bf16[2,64,256]{2,1,0:T(8,128)(2,1)}, bf16[2,64,256]{2,1,0:T(8,128)(2,1)}, u32[]{:S(2)}, u32[]{:S(2)}) collective-permute-start(bf16[2,64,256]{2,1,0:T(8,128)(2,1)} %fusion.35), channel_id=1, source_target_pairs={{0,8},{1,9},{2,10},{3,11},{4,12},{5,13},{6,14},{7,15},{8,0},{9,1},... | collective-permute-start | bytes 196616 | tf_op jit(solution)/shard_map/ppermute | solution.py:37
  128.6 10.3 %collective-permute-start.7 = (bf16[64,256]{1,0:T(8,128)(2,1)S(1)}, bf16[64,256]{1,0:T(8,128)(2,1)S(1)}, u32[]{:S(2)}, u32[]{:S(2)}) collective-permute-start(bf16[64,256]{1,0:T(8,128)(2,1)S(1)} %fusion.39), channel_id=1, source_target_pairs={{0,2},{1,3},{2,0},{3,1},{4,6},{5,7},{6,4},{7,5},{8,10},{9,11},{10,... | collective-permute-start | bytes 98312 | tf_op jit(solution)/shard_map/ppermute | solution.py:37
  164.1 5.7 %copy-start.2 = (bf16[64,16384]{1,0:T(8,128)(2,1)S(1)}, bf16[64,16384]{1,0:T(8,128)(2,1)}, u32[]{:S(2)}) copy-start(bf16[64,16384]{1,0:T(8,128)(2,1)} %copy-done.1) | copy-start | bytes 6291460
  164.1 3.4 collective-permute-start.12
  167.5 6.2 %collective-permute-start.13 = (f32[2,2,16,256]{3,2,1,0:T(8,128)S(1)}, f32[2,2,16,256]{3,2,1,0:T(8,128)S(1)}, u32[]{:S(2)}, u32[]{:S(2)}) collective-permute-start(f32[2,2,16,256]{3,2,1,0:T(8,128)S(1)} %dynamic-slice_bitcast_fusion.1), channel_id=1, source_target_pairs={{0,4},{1,5},{2,6},{3,7},{4,0},{5,1},{6,2},{7,3},{8,12},{9,13},{10,... | collective-permute-start | bytes 196616 | tf_op jit(solution)/shard_map/ppermute | solution.py:37
  173.8 7.4 %collective-permute-start.14 = (f32[2,16,256]{2,1,0:T(8,128)S(1)}, f32[2,16,256]{2,1,0:T(8,128)S(1)}, u32[]{:S(2)}, u32[]{:S(2)}) collective-permute-start(f32[2,16,256]{2,1,0:T(8,128)S(1)} %dynamic-slice_bitcast_fusion.2), channel_id=1, source_target_pairs={{0,8},{1,9},{2,10},{3,11},{4,12},{5,13},{6,14},{7,15},{8,0},{9,1},... | collective-permute-start | bytes 98312 | tf_op jit(solution)/shard_map/ppermute | solution.py:37
  181.3 7.1 %collective-permute-start.15 = (f32[16,256]{1,0:T(8,128)S(1)}, f32[16,256]{1,0:T(8,128)S(1)}, u32[]{:S(2)}, u32[]{:S(2)}) collective-permute-start(f32[16,256]{1,0:T(8,128)S(1)} %dynamic-slice_bitcast_fusion.3), channel_id=1, source_target_pairs={{0,2},{1,3},{2,0},{3,1},{4,6},{5,7},{6,4},{7,5},{8,10},{9,11},{10,... | collective-permute-start | bytes 49160 | tf_op jit(solution)/shard_map/ppermute | solution.py:37
  188.4 30.3 %collective-permute-start.16 = (f32[17,256]{1,0:T(8,128)S(1)}, f32[17,256]{1,0:T(8,128)S(1)}, u32[]{:S(2)}, u32[]{:S(2)}) collective-permute-start(f32[17,256]{1,0:T(8,128)S(1)} %pad_maximum_fusion.1), channel_id=1, source_target_pairs={{0,16},{16,0},{32,48},{48,32},{64,80},{80,64},{96,112},{112,96},{1... | collective-permute-start | bytes 52232 | tf_op jit(solution)/shard_map/ppermute | solution.py:47
  190.5 127.8 %collective-permute-start.11 = (bf16[512,256]{1,0:T(8,128)(2,1)S(1)}, bf16[512,256]{1,0:T(8,128)(2,1)S(1)}, u32[]{:S(2)}, u32[]{:S(2)}) collective-permute-start(bf16[512,256]{1,0:T(8,128)(2,1)S(1)} %get-tuple-element.16), channel_id=1, source_target_pairs={{0,271},{1,254},{2,237},{3,220},{4,203},{5,186},{6,169},{7,152},{8... | collective-permute-start | bytes 786440 | tf_op jit(solution)/shard_map/ppermute | solution.py:137
  192.4 125.9 %collective-permute-start.10 = (bf16[512,256]{1,0:T(8,128)(2,1)S(1)}, bf16[512,256]{1,0:T(8,128)(2,1)S(1)}, u32[]{:S(2)}, u32[]{:S(2)}) collective-permute-start(bf16[512,256]{1,0:T(8,128)(2,1)S(1)} %get-tuple-element.17), channel_id=1, source_target_pairs={{0,256},{1,241},{2,226},{3,211},{4,196},{5,181},{6,166},{7,151},{8... | collective-permute-start | bytes 786440 | tf_op jit(solution)/shard_map/ppermute | solution.py:137
  195.5 122.8 %collective-permute-start.9 = (bf16[512,256]{1,0:T(8,128)(2,1)S(1)}, bf16[512,256]{1,0:T(8,128)(2,1)S(1)}, u32[]{:S(2)}, u32[]{:S(2)}) collective-permute-start(bf16[512,256]{1,0:T(8,128)(2,1)S(1)} %get-tuple-element.18), channel_id=1, source_target_pairs={{0,15},{1,510},{2,493},{3,476},{4,459},{5,442},{6,425},{7,408},{8,... | collective-permute-start | bytes 786440 | tf_op jit(solution)/shard_map/ppermute | solution.py:137
  214.7 103.6 %collective-permute-start.8 = (bf16[512,256]{1,0:T(8,128)(2,1)S(1)}, bf16[512,256]{1,0:T(8,128)(2,1)S(1)}, u32[]{:S(2)}, u32[]{:S(2)}) collective-permute-start(bf16[512,256]{1,0:T(8,128)(2,1)S(1)} %get-tuple-element.19), channel_id=1, source_target_pairs={{0,0},{1,497},{2,482},{3,467},{4,452},{5,437},{6,422},{7,407},{8,3... | collective-permute-start | bytes 786440 | tf_op jit(solution)/shard_map/ppermute | solution.py:137
  218.7 68.9 %collective-permute-start.17 = (f32[17,256]{1,0:T(8,128)S(1)}, f32[17,256]{1,0:T(8,128)S(1)}, u32[]{:S(2)}, u32[]{:S(2)}) collective-permute-start(f32[17,256]{1,0:T(8,128)S(1)} %fusion.53), channel_id=1, source_target_pairs={{0,32},{16,48},{32,0},{48,16},{64,96},{80,112},{96,64},{112,80},{1... | collective-permute-start | bytes 52232 | tf_op jit(solution)/shard_map/ppermute | solution.py:47
  287.6 6.6 %collective-permute-start.18 = (f32[17,256]{1,0:T(8,128)S(1)}, f32[17,256]{1,0:T(8,128)S(1)}, u32[]{:S(2)}, u32[]{:S(2)}) collective-permute-start(f32[17,256]{1,0:T(8,128)S(1)} %add.172), channel_id=1, source_target_pairs={{0,64},{16,80},{32,96},{48,112},{64,0},{80,16},{96,32},{112,48},{1... | collective-permute-start | bytes 52232 | tf_op jit(solution)/shard_map/ppermute | solution.py:47
  294.2 9.7 %collective-permute-start.19 = (f32[17,256]{1,0:T(8,128)S(1)}, f32[17,256]{1,0:T(8,128)S(1)}, u32[]{:S(2)}, u32[]{:S(2)}) collective-permute-start(f32[17,256]{1,0:T(8,128)S(1)} %add.173), channel_id=1, source_target_pairs={{0,128},{16,144},{32,160},{48,176},{64,192},{80,208},{96,224},{112... | collective-permute-start | bytes 52232 | tf_op jit(solution)/shard_map/ppermute | solution.py:47
  303.9 14.4 %collective-permute-start.20 = (f32[17,256]{1,0:T(8,128)S(1)}, f32[17,256]{1,0:T(8,128)S(1)}, u32[]{:S(2)}, u32[]{:S(2)}) collective-permute-start(f32[17,256]{1,0:T(8,128)S(1)} %add.174), channel_id=1, source_target_pairs={{0,256},{16,272},{32,288},{48,304},{64,320},{80,336},{96,352},{112... | collective-permute-start | bytes 52232 | tf_op jit(solution)/shard_map/ppermute | solution.py:47
  318.6 3.4 collective-permute-start.21
  322.1 7.4 %collective-permute-start.22 = (bf16[2,2,64,256]{3,2,1,0:T(8,128)(2,1)S(1)}, bf16[2,2,64,256]{3,2,1,0:T(8,128)(2,1)S(1)}, u32[]{:S(2)}, u32[]{:S(2)}) collective-permute-start(bf16[2,2,64,256]{3,2,1,0:T(8,128)(2,1)S(1)} %fusion.34), channel_id=1, source_target_pairs={{0,4},{1,5},{2,6},{3,7},{4,0},{5,1},{6,2},{7,3},{8,12},{9,13},{10,... | collective-permute-start | bytes 393224 | tf_op jit(solution)/shard_map/ppermute | solution.py:37
  329.6 7.7 %collective-permute-start.23 = (bf16[2,64,256]{2,1,0:T(8,128)(2,1)S(1)}, bf16[2,64,256]{2,1,0:T(8,128)(2,1)S(1)}, u32[]{:S(2)}, u32[]{:S(2)}) collective-permute-start(bf16[2,64,256]{2,1,0:T(8,128)(2,1)S(1)} %fusion.36), channel_id=1, source_target_pairs={{0,8},{1,9},{2,10},{3,11},{4,12},{5,13},{6,14},{7,15},{8,0},{9,1},... | collective-permute-start | bytes 196616 | tf_op jit(solution)/shard_map/ppermute | solution.py:37
  337.3 7.3 %collective-permute-start.24 = (bf16[64,256]{1,0:T(8,128)(2,1)S(1)}, bf16[64,256]{1,0:T(8,128)(2,1)S(1)}, u32[]{:S(2)}, u32[]{:S(2)}) collective-permute-start(bf16[64,256]{1,0:T(8,128)(2,1)S(1)} %fusion.40), channel_id=1, source_target_pairs={{0,2},{1,3},{2,0},{3,1},{4,6},{5,7},{6,4},{7,5},{8,10},{9,11},{10,... | collective-permute-start | bytes 98312 | tf_op jit(solution)/shard_map/ppermute | solution.py:37
  (3 other events, 5.5 us)

commit v6 on v4

--- a/solution.py
+++ b/solution.py
@@ -20,14 +20,12 @@
     return placed.transpose(0, 2, 1, 3).reshape(side, side)
 
 
-def rep_reduce_scatter(x, wire_dtype):
+def rep_reduce_scatter(x, wire_dtype, order):
     replicas = lax.axis_size("rep")
     rep_index = lax.axis_index("rep")
-    bit_count = (replicas - 1).bit_length()
-    rows = x.shape[0] // replicas
-    current = x.reshape((2,) * bit_count + (rows,) + x.shape[1:])
-    remaining = list(reversed(range(bit_count)))
-    order = [0] + list(range(2, bit_count)) + [1] if bit_count > 2 else list(range(bit_count))
+    rows = x.shape[0] >> len(order)
+    current = x.reshape((2,) * len(order) + (rows,) + x.shape[1:])
+    remaining = sorted(order, reverse=True)
     for bit in order:
         axis = remaining.index(bit)
         mine = (rep_index >> bit) & 1
@@ -40,6 +38,22 @@
     return current
 
 
+def rep_all_gather(x, order):
+    replicas = lax.axis_size("rep")
+    rep_index = lax.axis_index("rep")
+    current = x
+    held = []
+    for bit in order:
+        partner = [(i, i ^ (1 << bit)) for i in range(replicas)]
+        got = lax.ppermute(current, "rep", partner)
+        upper = ((rep_index >> bit) & 1) == 1
+        low = jnp.where(upper, got, current)
+        high = jnp.where(upper, current, got)
+        held = sorted(held + [bit], reverse=True)
+        current = jnp.stack([low, high], axis=held.index(bit))
+    return current.reshape((-1,) + x.shape[1:])
+
+
 def blk_all_reduce(x):
     blocks = lax.axis_size("blk")
     step = 1
@@ -49,13 +63,20 @@
     return x
 
 
-def source_pairs(blocks, replicas, slot, half, backward):
+def route_target(source_rep, route, replicas):
+    half = replicas // 2
+    if route == 0:
+        return source_rep if source_rep < half else replicas + half - 1 - source_rep
+    return replicas - 1 - source_rep if source_rep < half else source_rep - half
+
+
+def route_pairs(blocks, replicas, slot, route, backward):
     pairs = []
     for b in range(blocks):
-        for r in range(replicas):
-            src_rep = r if half == 0 else replicas - 1 - r
-            src = ((b - r - slot * replicas) % blocks) * replicas + src_rep
-            dst = b * replicas + r
+        for s in range(replicas):
+            d = route_target(s, route, replicas)
+            src = b * replicas + s
+            dst = ((b + d + slot * replicas) % blocks) * replicas + d
             pairs.append((dst, src) if backward else (src, dst))
     return pairs
 
@@ -78,29 +99,34 @@
     rows_here = tile_rows[0, 0]
     cols_here = tile_cols[0, 0]
     counts_here = tile_count[0, 0]
-    partition = lax.all_gather(feats, "rep", axis=0, tiled=True)
-    part_rows = partition.shape[0]
-    half_rows = part_rows // 2
+    replica_bits = (replicas - 1).bit_length()
+    gather_bits = [1] + list(range(2, replica_bits - 1)) + [0]
+    held_half = rep_all_gather(feats, gather_bits)
+    half_rows = held_half.shape[0]
+    part_rows = 2 * half_rows
     tiles_per_part = part_rows // tile_size
     both_axes = ("blk", "rep")
+    upper_rep = lax.axis_index("rep") >= replicas // 2
     sources = []
     for slot in range(pair_slots):
-        halves = [
-            lax.ppermute(
-                partition[half * half_rows:(half + 1) * half_rows],
-                both_axes,
-                source_pairs(blocks, replicas, slot, half, False),
+        by_route = [
+            lax.ppermute(held_half, both_axes, route_pairs(blocks, replicas, slot, route, False))
+            for route in range(2)
+        ]
+        sources.append(
+            jnp.where(
+                upper_rep,
+                jnp.concatenate([by_route[1], by_route[0]], axis=0),
+                jnp.concatenate([by_route[0], by_route[1]], axis=0),
             )
-            for half in range(2)
-        ]
-        sources.append(jnp.concatenate(halves, axis=0))
+        )
     adjacency = [
         dense_adjacency(
             values_here[slot], rows_here[slot], cols_here[slot], counts_here[slot], tiles_per_part
         )
         for slot in range(pair_slots)
     ]
-    aggregated_feats = jnp.zeros(partition.shape, jnp.float32)
+    aggregated_feats = jnp.zeros((part_rows, feats.shape[1]), jnp.float32)
     for slot in range(pair_slots):
         aggregated_feats = aggregated_feats + jnp.dot(
             adjacency[slot], sources[slot], preferred_element_type=jnp.float32
@@ -111,7 +137,8 @@
         precision=lax.Precision.HIGHEST,
         preferred_element_type=jnp.float32,
     )
-    aggregate_rows = rep_reduce_scatter(aggregate, jnp.bfloat16)
+    full_bits = [0] + list(range(2, replica_bits)) + [1]
+    aggregate_rows = rep_reduce_scatter(aggregate, jnp.bfloat16, full_bits)
     out, grad_rows = activation(aggregate_rows + bias, grad_out)
     grad_block = lax.all_gather(grad_rows, "rep", axis=0, tiled=True)
     weight_terms = lax.dot_general(
@@ -121,10 +148,10 @@
         precision=lax.Precision.HIGHEST,
         preferred_element_type=jnp.float32,
     )
-    weight_part = rep_reduce_scatter(weight_terms, jnp.float32)
+    weight_part = rep_reduce_scatter(weight_terms, jnp.float32, full_bits)
     bias_part = jnp.sum(grad_block.astype(jnp.float32), axis=0)
     totals = blk_all_reduce(jnp.concatenate([weight_part, bias_part[None, :]], axis=0))
-    returned = [jnp.zeros((half_rows, partition.shape[1]), jnp.float32) for _ in range(2)]
+    returned = jnp.zeros((half_rows, feats.shape[1]), jnp.float32)
     for slot in range(pair_slots):
         partial = lax.dot_general(
             adjacency[slot],
@@ -132,15 +159,18 @@
             (((0,), (0,)), ((), ())),
             preferred_element_type=jnp.float32,
         ).astype(jnp.bfloat16)
-        for half in range(2):
+        first, second = partial[:half_rows], partial[half_rows:]
+        for route in range(2):
+            own_half = jnp.where(upper_rep, second, first)
+            other_half = jnp.where(upper_rep, first, second)
             got = lax.ppermute(
-                partial[half * half_rows:(half + 1) * half_rows],
+                own_half if route == 0 else other_half,
                 both_axes,
-                source_pairs(blocks, replicas, slot, half, True),
+                route_pairs(blocks, replicas, slot, route, True),
             )
-            returned[half] = returned[half] + got.astype(jnp.float32)
-    partial_grad = jnp.concatenate(returned, axis=0)
-    grad_hw = rep_reduce_scatter(partial_grad, jnp.bfloat16).astype(jnp.bfloat16)
+            returned = returned + got.astype(jnp.float32)
+    half_bits = [0] + list(range(2, replica_bits - 1)) + [1]
+    grad_hw = rep_reduce_scatter(returned, jnp.bfloat16, half_bits).astype(jnp.bfloat16)
     grad_feats = lax.dot_general(
         grad_hw, weight, (((1,), (1,)), ((), ())), preferred_element_type=jnp.float32
     ).astype(jnp.bfloat16)

time: 328 us -> 333 us (1.015)
  blocking collectives: 45.8 us -> 22.6 us
  waiting for transfers between devices: 113 us -> 129 us
  starting transfers between devices: 140 us -> 153 us
    all_gather x1 -> x0, blocking collectives: 23.2 us -> none  [body(): partition = lax.all_gather(feats, 'rep', axis=0, tiled=True)]
    ppermute x8 -> x11, starting transfers between devices: 43.7 us -> 62.9 us  [the longest x4 29.4 us: body(): lax.ppermute(held_half, both_axes, route_pairs(blocks, replicas, slot, ro...]
    ppermute x8 -> x11, waiting for transfers between devices: 89.9 us -> 97.9 us  [the longest x4 50.4 us: body(): lax.ppermute(own_half if route == 0 else other_half, both_axes, route_pai...]
    ppermute x12 -> x11, starting transfers between devices: 66.6 us -> 61.6 us  [rep_reduce_scatter(): got = lax.ppermute(send.astype(wire_dtype), 'rep', partner)]
    ppermute x5, waiting for transfers between devices: 6.97 us -> 11.3 us  [blk_all_reduce(): x = x + lax.ppermute(x, 'blk', [(i, i ^ step) for i in range(blocks)])]
    ppermute x12 -> x11, waiting for transfers between devices: 15.7 us -> 19.8 us  [rep_reduce_scatter(): got = lax.ppermute(send.astype(wire_dtype), 'rep', partner)]
  transfers between devices with their start and end apart: 25 -> 27, of which waited for: 14 -> 17; matrix products, arithmetic and copies ran while one was open for 5% -> 4% of each run, Pallas kernels for 0% -> 0%
where the time goes in v6:
time: 333 us; the launch traced here: 332 us
  starting transfers between devices  153 us (46%)
  waiting for transfers between devices  129 us (39%)
  blocking collectives  22.6 us (7%)
  matrix products  11.8 us (4%)
  local copies, waits for them, and re-layouts  8.85 us (3%)
  other arithmetic  5.37 us (2%)
    ppermute x11, starting transfers between devices, rep_reduce_scatter(): got = lax.ppermute(send.astype(wire_dtype), 'rep', partner)  61.6 us
    ppermute x4, waiting for transfers between devices, body(): lax.ppermute(own_half if route == 0 else other_half, both_axes, route_pai...  50.4 us
    ppermute x4, waiting for transfers between devices, body(): lax.ppermute(held_half, both_axes, route_pairs(blocks, replicas, slot, ro...  44.8 us
    ppermute x4, starting transfers between devices, body(): lax.ppermute(held_half, both_axes, route_pairs(blocks, replicas, slot, ro...  29.4 us
    ppermute x5, starting transfers between devices, blk_all_reduce(): x = x + lax.ppermute(x, 'blk', [(i, i ^ step) for i in range(blocks)])  28.1 us
    ppermute x4, starting transfers between devices, body(): lax.ppermute(own_half if route == 0 else other_half, both_axes, route_pai...  23.6 us
    all_gather x1, blocking collectives, body(): grad_block = lax.all_gather(grad_rows, 'rep', axis=0, tiled=True)  22.6 us
    ppermute x11, waiting for transfers between devices, rep_reduce_scatter(): got = lax.ppermute(send.astype(wire_dtype), 'rep', partner)  19.8 us
  transfers between devices with their start and end apart: 27, of which 17 were waited for; matrix products, arithmetic and copies ran while one was open for 4% of the time, Pallas kernels for 0%

profile of v6, /device:TPU:6, one launch (start us, length us, event | category | flops | bytes accessed | tf_op | source)
XLA Modules:
  0.0 331.5 jit_solution(5768632684692050017)
XLA Ops:
  0.7 5.2 %collective-permute-start = (bf16[64,256]{1,0:T(8,128)(2,1)}, bf16[64,256]{1,0:T(8,128)(2,1)S(1)}, u32[]{:S(2)}, u32[]{:S(2)}) collective-permute-start(bf16[64,256]{1,0:T(8,128)(2,1)} %param.8), channel_id=1, source_target_pairs={{0,2},{1,3},{2,0},{3,1},{4,6},{5,7},{6,4},{7,5},{8,10},{9,11},{10,... | collective-permute-start | bytes 98312 | tf_op jit(solution)/shard_map/ppermute | solution.py:48
  5.9 4.0 %fusion.59 = (bf16[1,1,1,64,128,128]{5,4,3,2,1,0:T(8,128)(2,1)}, bf16[1,1,1,64,128,128]{5,4,3,2,1,0:T(8,128)(2,1)S(1)}) fusion(bf16[1,1,2,64,128,128]{5,4,3,2,1,0:T(8,128)(2,1)} %param.12), kind=kLoop, calls=%fused_computation.104 | loop fusion | bytes 8388608 | tf_op jit(solution)/shard_map/slice | solution.py:125
  10.6 2.7 collective-permute-start.1
  14.0 2.8 collective-permute-done.1
  18.7 4.6 %convolution_convert_fusion.1 = bf16[64,16384]{1,0:T(8,128)(2,1)} fusion(bf16[8,8,128,128]{3,2,1,0:T(8,128)(2,1)} %bitcast.123, s32[64]{0:T(128)S(1)} %get-tuple-element.18, pred[64]{0:T(512)(128)(4,1)S(1)} %iota_compare_fusion.3), kind=kOutput, calls=%fused_computation.1 | convolution fusion | flops 135274496 | bytes 4194624 | tf_op jit(solution)/shard_map/dot_general | solution.py:13
  24.1 13.2 %collective-permute-start.6 = (bf16[512,256]{1,0:T(8,128)(2,1)S(1)}, bf16[512,256]{1,0:T(8,128)(2,1)S(1)}, u32[]{:S(2)}, u32[]{:S(2)}) collective-permute-start(bf16[512,256]{1,0:T(8,128)(2,1)S(1)} %bitcast.134), channel_id=1, source_target_pairs={{0,256},{1,273},{2,290},{3,307},{4,324},{5,341},{6,358},{7,375},{8... | collective-permute-start | bytes 786440 | tf_op jit(solution)/shard_map/ppermute | solution.py:113
  37.2 4.4 %collective-permute-start.5 = (bf16[512,256]{1,0:T(8,128)(2,1)S(1)}, bf16[512,256]{1,0:T(8,128)(2,1)S(1)}, u32[]{:S(2)}, u32[]{:S(2)}) collective-permute-start(bf16[512,256]{1,0:T(8,128)(2,1)S(1)} %bitcast.135), channel_id=1, source_target_pairs={{0,511},{1,494},{2,477},{3,460},{4,443},{5,426},{6,409},{7,392},{8... | collective-permute-start | bytes 786440 | tf_op jit(solution)/shard_map/ppermute | solution.py:113
  43.4 9.9 %collective-permute-start.4 = (bf16[512,256]{1,0:T(8,128)(2,1)S(1)}, bf16[512,256]{1,0:T(8,128)(2,1)S(1)}, u32[]{:S(2)}, u32[]{:S(2)}) collective-permute-start(bf16[512,256]{1,0:T(8,128)(2,1)S(1)} %bitcast.136), channel_id=1, source_target_pairs={{0,0},{1,17},{2,34},{3,51},{4,68},{5,85},{6,102},{7,119},{8,255},{... | collective-permute-start | bytes 786440 | tf_op jit(solution)/shard_map/ppermute | solution.py:113
  55.2 22.9 %collective-permute-done.6 = bf16[512,256]{1,0:T(8,128)(2,1)S(1)} collective-permute-done((bf16[512,256]{1,0:T(8,128)(2,1)S(1)}, bf16[512,256]{1,0:T(8,128)(2,1)S(1)}, u32[]{:S(2)}, u32[]{:S(2)}) %collective-permute-start.6) | collective-permute-done | bytes 262176 | tf_op jit(solution)/shard_map/ppermute | solution.py:113
  78.2 12.3 %collective-permute-done.5 = bf16[512,256]{1,0:T(8,128)(2,1)S(1)} collective-permute-done((bf16[512,256]{1,0:T(8,128)(2,1)S(1)}, bf16[512,256]{1,0:T(8,128)(2,1)S(1)}, u32[]{:S(2)}, u32[]{:S(2)}) %collective-permute-start.5) | collective-permute-done | bytes 262176 | tf_op jit(solution)/shard_map/ppermute | solution.py:113
  91.2 9.6 %collective-permute-done.3 = bf16[512,256]{1,0:T(8,128)(2,1)S(1)} collective-permute-done((bf16[512,256]{1,0:T(8,128)(2,1)S(1)}, bf16[512,256]{1,0:T(8,128)(2,1)S(1)}, u32[]{:S(2)}, u32[]{:S(2)}) %collective-permute-start.3) | collective-permute-done | bytes 262176 | tf_op jit(solution)/shard_map/ppermute | solution.py:113
  102.2 3.2 collective-permute-start.7
  109.5 5.8 %collective-permute-done.8 = bf16[2,2,64,256]{3,2,1,0:T(8,128)(2,1)} collective-permute-done((bf16[2,2,64,256]{3,2,1,0:T(8,128)(2,1)S(1)}, bf16[2,2,64,256]{3,2,1,0:T(8,128)(2,1)}, u32[]{:S(2)}, u32[]{:S(2)}) %collective-permute-start.8) | collective-permute-done | bytes 131104 | tf_op jit(solution)/shard_map/ppermute | solution.py:35
  118.9 6.0 %collective-permute-done.9 = bf16[2,64,256]{2,1,0:T(8,128)(2,1)} collective-permute-done((bf16[2,64,256]{2,1,0:T(8,128)(2,1)}, bf16[2,64,256]{2,1,0:T(8,128)(2,1)}, u32[]{:S(2)}, u32[]{:S(2)}) %collective-permute-start.9) | collective-permute-done | bytes 65568 | tf_op jit(solution)/shard_map/ppermute | solution.py:35
  126.5 11.8 %collective-permute-start.10 = (bf16[64,256]{1,0:T(8,128)(2,1)S(1)}, bf16[64,256]{1,0:T(8,128)(2,1)S(1)}, u32[]{:S(2)}, u32[]{:S(2)}) collective-permute-start(bf16[64,256]{1,0:T(8,128)(2,1)S(1)} %fusion.44), channel_id=1, source_target_pairs={{0,2},{1,3},{2,0},{3,1},{4,6},{5,7},{6,4},{7,5},{8,10},{9,11},{10,... | collective-permute-start | bytes 98312 | tf_op jit(solution)/shard_map/ppermute | solution.py:35
  141.7 22.6 %all_gather.3 = bf16[1024,256]{1,0:T(8,128)(2,1)S(1)} all-gather(bf16[64,256]{1,0:T(8,128)(2,1)S(1)} %get-tuple-element.12), channel_id=1, replica_groups=mesh['blk'=32,'rep'=16] {'rep'}, dimensions={0}, use_global_device_ids=true | all-gather | bytes 557056 | tf_op jit(solution)/shard_map/all_gather | solution.py:143
  167.8 2.3 collective-permute-start.18
  171.1 2.3 collective-permute-start.19
  173.4 3.9 %collective-permute-done.19 = f32[2,2,16,256]{3,2,1,0:T(8,128)S(1)} collective-permute-done((f32[2,2,16,256]{3,2,1,0:T(8,128)S(1)}, f32[2,2,16,256]{3,2,1,0:T(8,128)S(1)}, u32[]{:S(2)}, u32[]{:S(2)}) %collective-permute-start.19) | collective-permute-done | bytes 65568 | tf_op jit(solution)/shard_map/ppermute | solution.py:35
  177.4 5.6 %collective-permute-start.20 = (f32[2,16,256]{2,1,0:T(8,128)S(1)}, f32[2,16,256]{2,1,0:T(8,128)S(1)}, u32[]{:S(2)}, u32[]{:S(2)}) collective-permute-start(f32[2,16,256]{2,1,0:T(8,128)S(1)} %dynamic-slice_bitcast_fusion.2), channel_id=1, source_target_pairs={{0,8},{1,9},{2,10},{3,11},{4,12},{5,13},{6,14},{7,15},{8,0},{9,1},... | collective-permute-start | bytes 98312 | tf_op jit(solution)/shard_map/ppermute | solution.py:35
  187.0 14.3 %collective-permute-start.13 = (bf16[512,256]{1,0:T(8,128)(2,1)S(1)}, bf16[512,256]{1,0:T(8,128)(2,1)S(1)}, u32[]{:S(2)}, u32[]{:S(2)}) collective-permute-start(bf16[512,256]{1,0:T(8,128)(2,1)S(1)} %get-tuple-element.8), channel_id=1, source_target_pairs={{256,0},{273,1},{290,2},{307,3},{324,4},{341,5},{358,6},{375,7},{5... | collective-permute-start | bytes 786440 | tf_op jit(solution)/shard_map/ppermute | solution.py:166
  201.3 5.5 %collective-permute-start.14 = (bf16[512,256]{1,0:T(8,128)(2,1)S(1)}, bf16[512,256]{1,0:T(8,128)(2,1)S(1)}, u32[]{:S(2)}, u32[]{:S(2)}) collective-permute-start(bf16[512,256]{1,0:T(8,128)(2,1)S(1)} %get-tuple-element.9), channel_id=1, source_target_pairs={{511,0},{494,1},{477,2},{460,3},{443,4},{426,5},{409,6},{392,7},{2... | collective-permute-start | bytes 786440 | tf_op jit(solution)/shard_map/ppermute | solution.py:166
  208.8 25.0 %collective-permute-done.11 = bf16[512,256]{1,0:T(8,128)(2,1)S(1)} collective-permute-done((bf16[512,256]{1,0:T(8,128)(2,1)S(1)}, bf16[512,256]{1,0:T(8,128)(2,1)S(1)}, u32[]{:S(2)}, u32[]{:S(2)}) %collective-permute-start.11) | collective-permute-done | bytes 262176 | tf_op jit(solution)/shard_map/ppermute | solution.py:166
  233.8 3.0 collective-permute-done.12
  236.9 22.3 %collective-permute-done.14 = bf16[512,256]{1,0:T(8,128)(2,1)S(1)} collective-permute-done((bf16[512,256]{1,0:T(8,128)(2,1)S(1)}, bf16[512,256]{1,0:T(8,128)(2,1)S(1)}, u32[]{:S(2)}, u32[]{:S(2)}) %collective-permute-start.14) | collective-permute-done | bytes 262176 | tf_op jit(solution)/shard_map/ppermute | solution.py:166
  259.3 14.1 %collective-permute-start.15 = (bf16[2,2,64,256]{3,2,1,0:T(8,128)(2,1)S(1)}, bf16[2,2,64,256]{3,2,1,0:T(8,128)(2,1)S(1)}, u32[]{:S(2)}, u32[]{:S(2)}) collective-permute-start(bf16[2,2,64,256]{3,2,1,0:T(8,128)(2,1)S(1)} %fusion.39), channel_id=1, source_target_pairs={{0,1},{1,0},{2,3},{3,2},{4,5},{5,4},{6,7},{7,6},{8,9},{9,8},{10,11... | collective-permute-start | bytes 393224 | tf_op jit(solution)/shard_map/ppermute | solution.py:35
  273.4 2.7 collective-permute-start.22
  281.1 3.8 %collective-permute-done.23 = f32[17,256]{1,0:T(8,128)S(1)} collective-permute-done((f32[17,256]{1,0:T(8,128)S(1)}, f32[17,256]{1,0:T(8,128)S(1)}, u32[]{:S(2)}, u32[]{:S(2)}) %collective-permute-start.23) | collective-permute-done | bytes 17440 | tf_op jit(solution)/shard_map/ppermute | solution.py:61
  286.8 4.7 %collective-permute-done.24 = f32[17,256]{1,0:T(8,128)S(1)} collective-permute-done((f32[17,256]{1,0:T(8,128)S(1)}, f32[17,256]{1,0:T(8,128)S(1)}, u32[]{:S(2)}, u32[]{:S(2)}) %collective-permute-start.24) | collective-permute-done | bytes 17440 | tf_op jit(solution)/shard_map/ppermute | solution.py:61
  291.5 4.7 %collective-permute-start.25 = (f32[17,256]{1,0:T(8,128)S(1)}, f32[17,256]{1,0:T(8,128)S(1)}, u32[]{:S(2)}, u32[]{:S(2)}) collective-permute-start(f32[17,256]{1,0:T(8,128)S(1)} %add.178), channel_id=1, source_target_pairs={{0,128},{16,144},{32,160},{48,176},{64,192},{80,208},{96,224},{112... | collective-permute-start | bytes 52232 | tf_op jit(solution)/shard_map/ppermute | solution.py:61
  296.3 14.6 %collective-permute-start.17 = (bf16[64,256]{1,0:T(8,128)(2,1)S(1)}, bf16[64,256]{1,0:T(8,128)(2,1)S(1)}, u32[]{:S(2)}, u32[]{:S(2)}) collective-permute-start(bf16[64,256]{1,0:T(8,128)(2,1)S(1)} %fusion.45), channel_id=1, source_target_pairs={{0,2},{1,3},{2,0},{3,1},{4,6},{5,7},{6,4},{7,5},{8,10},{9,11},{10,... | collective-permute-start | bytes 98312 | tf_op jit(solution)/shard_map/ppermute | solution.py:35
  310.8 16.9 %collective-permute-start.26 = (f32[17,256]{1,0:T(8,128)S(1)}, f32[17,256]{1,0:T(8,128)S(1)}, u32[]{:S(2)}, u32[]{:S(2)}) collective-permute-start(f32[17,256]{1,0:T(8,128)S(1)} %add.179), channel_id=1, source_target_pairs={{0,256},{16,272},{32,288},{48,304},{64,320},{80,336},{96,352},{112... | collective-permute-start | bytes 52232 | tf_op jit(solution)/shard_map/ppermute | solution.py:61
  (100 shorter events, 43.5 us)
Async XLA Ops:
  0.6 100.9 %copy-start = (bf16[256,256]{1,0:T(8,128)(2,1)S(1)}, bf16[256,256]{1,0:T(8,128)(2,1)}, u32[]{:S(2)}) copy-start(bf16[256,256]{1,0:T(8,128)(2,1)} %param.9) | copy-start | bytes 393220
  0.7 9.9 %collective-permute-start = (bf16[64,256]{1,0:T(8,128)(2,1)}, bf16[64,256]{1,0:T(8,128)(2,1)S(1)}, u32[]{:S(2)}, u32[]{:S(2)}) collective-permute-start(bf16[64,256]{1,0:T(8,128)(2,1)} %param.8), channel_id=1, source_target_pairs={{0,2},{1,3},{2,0},{3,1},{4,6},{5,7},{6,4},{7,5},{8,10},{9,11},{10,... | collective-permute-start | bytes 98312 | tf_op jit(solution)/shard_map/ppermute | solution.py:48
  10.6 6.2 %collective-permute-start.1 = (bf16[2,64,256]{2,1,0:T(8,128)(2,1)S(1)}, bf16[2,64,256]{2,1,0:T(8,128)(2,1)S(1)}, u32[]{:S(2)}, u32[]{:S(2)}) collective-permute-start(bf16[2,64,256]{2,1,0:T(8,128)(2,1)S(1)} %pad_maximum_fusion.2), channel_id=1, source_target_pairs={{0,4},{1,5},{2,6},{3,7},{4,0},{5,1},{6,2},{7,3},{8,12},{9,13},{10,... | collective-permute-start | bytes 196616 | tf_op jit(solution)/shard_map/ppermute | solution.py:48
  16.8 7.2 %collective-permute-start.2 = (bf16[2,2,64,256]{3,2,1,0:T(8,128)(2,1)S(1)}, bf16[2,2,64,256]{3,2,1,0:T(8,128)(2,1)S(1)}, u32[]{:S(2)}, u32[]{:S(2)}) collective-permute-start(bf16[2,2,64,256]{3,2,1,0:T(8,128)(2,1)S(1)} %pad_maximum_fusion.1), channel_id=1, source_target_pairs={{0,1},{1,0},{2,3},{3,2},{4,5},{5,4},{6,7},{7,6},{8,9},{9,8},{10,11... | collective-permute-start | bytes 393224 | tf_op jit(solution)/shard_map/ppermute | solution.py:48
  24.1 54.1 %collective-permute-start.6 = (bf16[512,256]{1,0:T(8,128)(2,1)S(1)}, bf16[512,256]{1,0:T(8,128)(2,1)S(1)}, u32[]{:S(2)}, u32[]{:S(2)}) collective-permute-start(bf16[512,256]{1,0:T(8,128)(2,1)S(1)} %bitcast.134), channel_id=1, source_target_pairs={{0,256},{1,273},{2,290},{3,307},{4,324},{5,341},{6,358},{7,375},{8... | collective-permute-start | bytes 786440 | tf_op jit(solution)/shard_map/ppermute | solution.py:113
  37.2 53.2 %collective-permute-start.5 = (bf16[512,256]{1,0:T(8,128)(2,1)S(1)}, bf16[512,256]{1,0:T(8,128)(2,1)S(1)}, u32[]{:S(2)}, u32[]{:S(2)}) collective-permute-start(bf16[512,256]{1,0:T(8,128)(2,1)S(1)} %bitcast.135), channel_id=1, source_target_pairs={{0,511},{1,494},{2,477},{3,460},{4,443},{5,426},{6,409},{7,392},{8... | collective-permute-start | bytes 786440 | tf_op jit(solution)/shard_map/ppermute | solution.py:113
  43.4 47.8 %copy-start.3 = (bf16[64,16384]{1,0:T(8,128)(2,1)}, bf16[64,16384]{1,0:T(8,128)(2,1)S(1)}, u32[]{:S(2)}) copy-start(bf16[64,16384]{1,0:T(8,128)(2,1)S(1)} %convolution_convert_fusion) | copy-start | bytes 6291460
  43.4 47.8 %collective-permute-start.4 = (bf16[512,256]{1,0:T(8,128)(2,1)S(1)}, bf16[512,256]{1,0:T(8,128)(2,1)S(1)}, u32[]{:S(2)}, u32[]{:S(2)}) collective-permute-start(bf16[512,256]{1,0:T(8,128)(2,1)S(1)} %bitcast.136), channel_id=1, source_target_pairs={{0,0},{1,17},{2,34},{3,51},{4,68},{5,85},{6,102},{7,119},{8,255},{... | collective-permute-start | bytes 786440 | tf_op jit(solution)/shard_map/ppermute | solution.py:113
  53.3 47.5 %collective-permute-start.3 = (bf16[512,256]{1,0:T(8,128)(2,1)S(1)}, bf16[512,256]{1,0:T(8,128)(2,1)S(1)}, u32[]{:S(2)}, u32[]{:S(2)}) collective-permute-start(bf16[512,256]{1,0:T(8,128)(2,1)S(1)} %bitcast.137), channel_id=1, source_target_pairs={{0,255},{1,238},{2,221},{3,204},{4,187},{5,170},{6,153},{7,136},{8... | collective-permute-start | bytes 786440 | tf_op jit(solution)/shard_map/ppermute | solution.py:113
  90.4 10.4 %copy-start.1 = (bf16[64,16384]{1,0:T(8,128)(2,1)S(1)}, bf16[64,16384]{1,0:T(8,128)(2,1)}, u32[]{:S(2)}) copy-start(bf16[64,16384]{1,0:T(8,128)(2,1)} %convolution_convert_fusion.1) | copy-start | bytes 6291460
  102.2 38.0 %copy-start.9 = (f32[256]{0:T(256)S(1)}, f32[256]{0:T(256)}, u32[]{:S(2)}) copy-start(f32[256]{0:T(256)} %param.10) | copy-start | bytes 3076
  102.2 4.3 %collective-permute-start.7 = (bf16[2,2,2,64,256]{4,3,2,0,1:T(8,128)(2,1)S(1)}, bf16[2,2,2,64,256]{4,3,2,0,1:T(8,128)(2,1)S(1)}, u32[]{:S(2)}, u32[]{:S(2)}) collective-permute-start(bf16[2,2,2,64,256]{4,3,2,0,1:T(8,128)(2,1)S(1)} %fusion.37), channel_id=1, source_target_pairs={{0,1},{1,0},{2,3},{3,2},{4,5},{5,4},{6,7},{7,6},{8,9},{9,8},{10,11... | collective-permute-start | bytes 786440 | tf_op jit(solution)/shard_map/ppermute | solution.py:35
  107.4 57.0 %copy-start.4 = (bf16[64,16384]{1,0:T(8,128)(2,1)S(1)}, bf16[64,16384]{1,0:T(8,128)(2,1)}, u32[]{:S(2)}) copy-start(bf16[64,16384]{1,0:T(8,128)(2,1)} %copy-done.3) | copy-start | bytes 6291460
  107.4 7.9 %collective-permute-start.8 = (bf16[2,2,64,256]{3,2,1,0:T(8,128)(2,1)S(1)}, bf16[2,2,64,256]{3,2,1,0:T(8,128)(2,1)}, u32[]{:S(2)}, u32[]{:S(2)}) collective-permute-start(bf16[2,2,64,256]{3,2,1,0:T(8,128)(2,1)S(1)} %fusion.38), channel_id=1, source_target_pairs={{0,4},{1,5},{2,6},{3,7},{4,0},{5,1},{6,2},{7,3},{8,12},{9,13},{10,... | collective-permute-start | bytes 393224 | tf_op jit(solution)/shard_map/ppermute | solution.py:35
  117.0 8.0 %collective-permute-start.9 = (bf16[2,64,256]{2,1,0:T(8,128)(2,1)}, bf16[2,64,256]{2,1,0:T(8,128)(2,1)}, u32[]{:S(2)}, u32[]{:S(2)}) collective-permute-start(bf16[2,64,256]{2,1,0:T(8,128)(2,1)} %fusion.40), channel_id=1, source_target_pairs={{0,8},{1,9},{2,10},{3,11},{4,12},{5,13},{6,14},{7,15},{8,0},{9,1},... | collective-permute-start | bytes 196616 | tf_op jit(solution)/shard_map/ppermute | solution.py:35
  126.5 13.7 %collective-permute-start.10 = (bf16[64,256]{1,0:T(8,128)(2,1)S(1)}, bf16[64,256]{1,0:T(8,128)(2,1)S(1)}, u32[]{:S(2)}, u32[]{:S(2)}) collective-permute-start(bf16[64,256]{1,0:T(8,128)(2,1)S(1)} %fusion.44), channel_id=1, source_target_pairs={{0,2},{1,3},{2,0},{3,1},{4,6},{5,7},{6,4},{7,5},{8,10},{9,11},{10,... | collective-permute-start | bytes 98312 | tf_op jit(solution)/shard_map/ppermute | solution.py:35
  167.8 3.2 collective-permute-start.18
  171.1 6.2 %collective-permute-start.19 = (f32[2,2,16,256]{3,2,1,0:T(8,128)S(1)}, f32[2,2,16,256]{3,2,1,0:T(8,128)S(1)}, u32[]{:S(2)}, u32[]{:S(2)}) collective-permute-start(f32[2,2,16,256]{3,2,1,0:T(8,128)S(1)} %dynamic-slice_bitcast_fusion.1), channel_id=1, source_target_pairs={{0,4},{1,5},{2,6},{3,7},{4,0},{5,1},{6,2},{7,3},{8,12},{9,13},{10,... | collective-permute-start | bytes 196616 | tf_op jit(solution)/shard_map/ppermute | solution.py:35
  177.4 29.4 %collective-permute-start.20 = (f32[2,16,256]{2,1,0:T(8,128)S(1)}, f32[2,16,256]{2,1,0:T(8,128)S(1)}, u32[]{:S(2)}, u32[]{:S(2)}) collective-permute-start(f32[2,16,256]{2,1,0:T(8,128)S(1)} %dynamic-slice_bitcast_fusion.2), channel_id=1, source_target_pairs={{0,8},{1,9},{2,10},{3,11},{4,12},{5,13},{6,14},{7,15},{8,0},{9,1},... | collective-permute-start | bytes 98312 | tf_op jit(solution)/shard_map/ppermute | solution.py:35
  183.2 50.6 %collective-permute-start.11 = (bf16[512,256]{1,0:T(8,128)(2,1)S(1)}, bf16[512,256]{1,0:T(8,128)(2,1)S(1)}, u32[]{:S(2)}, u32[]{:S(2)}) collective-permute-start(bf16[512,256]{1,0:T(8,128)(2,1)S(1)} %get-tuple-element.6), channel_id=1, source_target_pairs={{0,0},{17,1},{34,2},{51,3},{68,4},{85,5},{102,6},{119,7},{255,8},{... | collective-permute-start | bytes 786440 | tf_op jit(solution)/shard_map/ppermute | solution.py:166
  185.1 51.8 %collective-permute-start.12 = (bf16[512,256]{1,0:T(8,128)(2,1)S(1)}, bf16[512,256]{1,0:T(8,128)(2,1)S(1)}, u32[]{:S(2)}, u32[]{:S(2)}) collective-permute-start(bf16[512,256]{1,0:T(8,128)(2,1)S(1)} %get-tuple-element.7), channel_id=1, source_target_pairs={{255,0},{238,1},{221,2},{204,3},{187,4},{170,5},{153,6},{136,7},{0... | collective-permute-start | bytes 786440 | tf_op jit(solution)/shard_map/ppermute | solution.py:166
  187.0 49.8 %collective-permute-start.13 = (bf16[512,256]{1,0:T(8,128)(2,1)S(1)}, bf16[512,256]{1,0:T(8,128)(2,1)S(1)}, u32[]{:S(2)}, u32[]{:S(2)}) collective-permute-start(bf16[512,256]{1,0:T(8,128)(2,1)S(1)} %get-tuple-element.8), channel_id=1, source_target_pairs={{256,0},{273,1},{290,2},{307,3},{324,4},{341,5},{358,6},{375,7},{5... | collective-permute-start | bytes 786440 | tf_op jit(solution)/shard_map/ppermute | solution.py:166
  201.3 57.8 %collective-permute-start.14 = (bf16[512,256]{1,0:T(8,128)(2,1)S(1)}, bf16[512,256]{1,0:T(8,128)(2,1)S(1)}, u32[]{:S(2)}, u32[]{:S(2)}) collective-permute-start(bf16[512,256]{1,0:T(8,128)(2,1)S(1)} %get-tuple-element.9), channel_id=1, source_target_pairs={{511,0},{494,1},{477,2},{460,3},{443,4},{426,5},{409,6},{392,7},{2... | collective-permute-start | bytes 786440 | tf_op jit(solution)/shard_map/ppermute | solution.py:166
  206.8 66.5 %collective-permute-start.21 = (f32[16,256]{1,0:T(8,128)S(1)}, f32[16,256]{1,0:T(8,128)S(1)}, u32[]{:S(2)}, u32[]{:S(2)}) collective-permute-start(f32[16,256]{1,0:T(8,128)S(1)} %dynamic-slice_bitcast_fusion.3), channel_id=1, source_target_pairs={{0,2},{1,3},{2,0},{3,1},{4,6},{5,7},{6,4},{7,5},{8,10},{9,11},{10,... | collective-permute-start | bytes 49160 | tf_op jit(solution)/shard_map/ppermute | solution.py:35
  259.3 16.8 %collective-permute-start.15 = (bf16[2,2,64,256]{3,2,1,0:T(8,128)(2,1)S(1)}, bf16[2,2,64,256]{3,2,1,0:T(8,128)(2,1)S(1)}, u32[]{:S(2)}, u32[]{:S(2)}) collective-permute-start(bf16[2,2,64,256]{3,2,1,0:T(8,128)(2,1)S(1)} %fusion.39), channel_id=1, source_target_pairs={{0,1},{1,0},{2,3},{3,2},{4,5},{5,4},{6,7},{7,6},{8,9},{9,8},{10,11... | collective-permute-start | bytes 393224 | tf_op jit(solution)/shard_map/ppermute | solution.py:35
  273.4 5.7 %collective-permute-start.22 = (f32[17,256]{1,0:T(8,128)S(1)}, f32[17,256]{1,0:T(8,128)S(1)}, u32[]{:S(2)}, u32[]{:S(2)}) collective-permute-start(f32[17,256]{1,0:T(8,128)S(1)} %pad_maximum_fusion.3), channel_id=1, source_target_pairs={{0,16},{16,0},{32,48},{48,32},{64,80},{80,64},{96,112},{112,96},{1... | collective-permute-start | bytes 52232 | tf_op jit(solution)/shard_map/ppermute | solution.py:61
  276.2 20.0 %collective-permute-start.16 = (bf16[2,64,256]{2,1,0:T(8,128)(2,1)S(1)}, bf16[2,64,256]{2,1,0:T(8,128)(2,1)S(1)}, u32[]{:S(2)}, u32[]{:S(2)}) collective-permute-start(bf16[2,64,256]{2,1,0:T(8,128)(2,1)S(1)} %fusion.41), channel_id=1, source_target_pairs={{0,4},{1,5},{2,6},{3,7},{4,0},{5,1},{6,2},{7,3},{8,12},{9,13},{10,... | collective-permute-start | bytes 196616 | tf_op jit(solution)/shard_map/ppermute | solution.py:35
  279.1 5.7 %collective-permute-start.23 = (f32[17,256]{1,0:T(8,128)S(1)}, f32[17,256]{1,0:T(8,128)S(1)}, u32[]{:S(2)}, u32[]{:S(2)}) collective-permute-start(f32[17,256]{1,0:T(8,128)S(1)} %fusion.58), channel_id=1, source_target_pairs={{0,32},{16,48},{32,0},{48,16},{64,96},{80,112},{96,64},{112,80},{1... | collective-permute-start | bytes 52232 | tf_op jit(solution)/shard_map/ppermute | solution.py:61
  284.9 6.6 %collective-permute-start.24 = (f32[17,256]{1,0:T(8,128)S(1)}, f32[17,256]{1,0:T(8,128)S(1)}, u32[]{:S(2)}, u32[]{:S(2)}) collective-permute-start(f32[17,256]{1,0:T(8,128)S(1)} %add.177), channel_id=1, source_target_pairs={{0,64},{16,80},{32,96},{48,112},{64,0},{80,16},{96,32},{112,48},{1... | collective-permute-start | bytes 52232 | tf_op jit(solution)/shard_map/ppermute | solution.py:61
  291.5 19.3 %collective-permute-start.25 = (f32[17,256]{1,0:T(8,128)S(1)}, f32[17,256]{1,0:T(8,128)S(1)}, u32[]{:S(2)}, u32[]{:S(2)}) collective-permute-start(f32[17,256]{1,0:T(8,128)S(1)} %add.178), channel_id=1, source_target_pairs={{0,128},{16,144},{32,160},{48,176},{64,192},{80,208},{96,224},{112... | collective-permute-start | bytes 52232 | tf_op jit(solution)/shard_map/ppermute | solution.py:61
  296.3 34.5 %collective-permute-start.17 = (bf16[64,256]{1,0:T(8,128)(2,1)S(1)}, bf16[64,256]{1,0:T(8,128)(2,1)S(1)}, u32[]{:S(2)}, u32[]{:S(2)}) collective-permute-start(bf16[64,256]{1,0:T(8,128)(2,1)S(1)} %fusion.45), channel_id=1, source_target_pairs={{0,2},{1,3},{2,0},{3,1},{4,6},{5,7},{6,4},{7,5},{8,10},{9,11},{10,... | collective-permute-start | bytes 98312 | tf_op jit(solution)/shard_map/ppermute | solution.py:35
  310.8 18.7 %collective-permute-start.26 = (f32[17,256]{1,0:T(8,128)S(1)}, f32[17,256]{1,0:T(8,128)S(1)}, u32[]{:S(2)}, u32[]{:S(2)}) collective-permute-start(f32[17,256]{1,0:T(8,128)S(1)} %add.179), channel_id=1, source_target_pairs={{0,256},{16,272},{32,288},{48,304},{64,320},{80,336},{96,352},{112... | collective-permute-start | bytes 52232 | tf_op jit(solution)/shard_map/ppermute | solution.py:61
  (7 other events, 40.8 us)

commit v7 on v4

--- a/solution.py
+++ b/solution.py
@@ -20,32 +20,48 @@
     return placed.transpose(0, 2, 1, 3).reshape(side, side)
 
 
-def rep_reduce_scatter(x, wire_dtype):
+def index_bits(current, remaining, bits, values):
+    for bit, value in sorted(zip(bits, values), key=lambda pair: remaining.index(pair[0]), reverse=True):
+        current = lax.dynamic_index_in_dim(current, value, remaining.index(bit), keepdims=False)
+    return current
+
+
+def rep_reduce_scatter(x, wire_dtype, groups):
     replicas = lax.axis_size("rep")
     rep_index = lax.axis_index("rep")
     bit_count = (replicas - 1).bit_length()
     rows = x.shape[0] // replicas
     current = x.reshape((2,) * bit_count + (rows,) + x.shape[1:])
     remaining = list(reversed(range(bit_count)))
-    order = [0] + list(range(2, bit_count)) + [1] if bit_count > 2 else list(range(bit_count))
-    for bit in order:
-        axis = remaining.index(bit)
-        mine = (rep_index >> bit) & 1
-        keep = lax.dynamic_index_in_dim(current, mine, axis, keepdims=False)
-        send = lax.dynamic_index_in_dim(current, 1 - mine, axis, keepdims=False)
-        partner = [(i, i ^ (1 << bit)) for i in range(replicas)]
-        got = lax.ppermute(send.astype(wire_dtype), "rep", partner)
-        current = keep + got.astype(jnp.float32)
-        remaining.remove(bit)
+    for bits in groups:
+        mine = [(rep_index >> bit) & 1 for bit in bits]
+        total = index_bits(current, remaining, bits, mine)
+        for offset in range(1, 1 << len(bits)):
+            flips = [(offset >> k) & 1 for k in range(len(bits))]
+            mask = sum(flip << bit for flip, bit in zip(flips, bits))
+            send = index_bits(current, remaining, bits, [m ^ f for m, f in zip(mine, flips)])
+            got = lax.ppermute(send.astype(wire_dtype), "rep", [(i, i ^ mask) for i in range(replicas)])
+            total = total + got.astype(jnp.float32)
+        current = total
+        remaining = [bit for bit in remaining if bit not in bits]
     return current
 
 
-def blk_all_reduce(x):
+def blk_all_reduce(x, groups):
     blocks = lax.axis_size("blk")
-    step = 1
-    while step < blocks:
-        x = x + lax.ppermute(x, "blk", [(i, i ^ step) for i in range(blocks)])
-        step <<= 1
+    blk_index = lax.axis_index("blk")
+    for bits in groups:
+        members = 1 << len(bits)
+        mine = sum(((blk_index >> bit) & 1) << k for k, bit in enumerate(bits))
+        by_offset = [x]
+        for offset in range(1, members):
+            mask = sum(((offset >> k) & 1) << bit for k, bit in enumerate(bits))
+            by_offset.append(lax.ppermute(x, "blk", [(i, i ^ mask) for i in range(blocks)]))
+        stacked = jnp.stack(by_offset)
+        ordered = jnp.take(stacked, jnp.arange(members) ^ mine, axis=0)
+        x = ordered[0]
+        for member in range(1, members):
+            x = x + ordered[member]
     return x
 
 
@@ -111,7 +127,8 @@
         precision=lax.Precision.HIGHEST,
         preferred_element_type=jnp.float32,
     )
-    aggregate_rows = rep_reduce_scatter(aggregate, jnp.bfloat16)
+    rep_groups = [[0, 2], [3, 1]]
+    aggregate_rows = rep_reduce_scatter(aggregate, jnp.bfloat16, rep_groups)
     out, grad_rows = activation(aggregate_rows + bias, grad_out)
     grad_block = lax.all_gather(grad_rows, "rep", axis=0, tiled=True)
     weight_terms = lax.dot_general(
@@ -121,9 +138,11 @@
         precision=lax.Precision.HIGHEST,
         preferred_element_type=jnp.float32,
     )
-    weight_part = rep_reduce_scatter(weight_terms, jnp.float32)
+    weight_part = rep_reduce_scatter(weight_terms, jnp.float32, rep_groups)
     bias_part = jnp.sum(grad_block.astype(jnp.float32), axis=0)
-    totals = blk_all_reduce(jnp.concatenate([weight_part, bias_part[None, :]], axis=0))
+    totals = blk_all_reduce(
+        jnp.concatenate([weight_part, bias_part[None, :]], axis=0), [[0, 1], [2, 3, 4]]
+    )
     returned = [jnp.zeros((half_rows, partition.shape[1]), jnp.float32) for _ in range(2)]
     for slot in range(pair_slots):
         partial = lax.dot_general(
@@ -140,7 +159,7 @@
             )
             returned[half] = returned[half] + got.astype(jnp.float32)
     partial_grad = jnp.concatenate(returned, axis=0)
-    grad_hw = rep_reduce_scatter(partial_grad, jnp.bfloat16).astype(jnp.bfloat16)
+    grad_hw = rep_reduce_scatter(partial_grad, jnp.bfloat16, rep_groups).astype(jnp.bfloat16)
     grad_feats = lax.dot_general(
         grad_hw, weight, (((1,), (1,)), ((), ())), preferred_element_type=jnp.float32
     ).astype(jnp.bfloat16)

time: 328 us -> 389 us (1.19)
  the two profiles are of different devices: /device:TPU:6 before, /device:TPU:108 now
where the time goes in v7:
time: 389 us; the launch traced here: 388 us
  starting transfers between devices  221 us (57%)
  waiting for transfers between devices  103 us (26%)
  blocking collectives  42.7 us (11%)
  matrix products  10.4 us (3%)
  local copies, waits for them, and re-layouts  6.72 us (2%)
    ppermute x18, starting transfers between devices, rep_reduce_scatter(): lax.ppermute(send.astype(wire_dtype), 'rep', [(i, i ^ mask) for i in rang...  102 us
    ppermute x10, starting transfers between devices, blk_all_reduce(): lax.ppermute(x, 'blk', [(i, i ^ mask) for i in range(blocks)])  70.9 us
    ppermute x10, waiting for transfers between devices, blk_all_reduce(): lax.ppermute(x, 'blk', [(i, i ^ mask) for i in range(blocks)])  46 us
    ppermute x4, waiting for transfers between devices, body(): lax.ppermute(partition[half * half_rows:(half + 1) * half_rows], both_axe...  30.6 us
    ppermute x18, waiting for transfers between devices, rep_reduce_scatter(): lax.ppermute(send.astype(wire_dtype), 'rep', [(i, i ^ mask) for i in rang...  26.8 us
    ppermute x4, starting transfers between devices, body(): lax.ppermute(partition[half * half_rows:(half + 1) * half_rows], both_axe...  24.3 us
    ppermute x4, starting transfers between devices, body(): lax.ppermute(partial[half * half_rows:(half + 1) * half_rows], both_axes,...  23.7 us
    all_gather x1, blocking collectives, body(): partition = lax.all_gather(feats, 'rep', axis=0, tiled=True)  21.4 us
  transfers between devices with their start and end apart: 36, of which 18 were waited for; matrix products, arithmetic and copies ran while one was open for 3% of the time, Pallas kernels for 0%

profile of v7, /device:TPU:108, one launch (start us, length us, event | category | flops | bytes accessed | tf_op | source)
XLA Modules:
  0.0 388.1 jit_solution(13575103675960031687)
XLA Ops:
  0.6 21.4 %all_gather.6 = bf16[1024,256]{1,0:T(8,128)(2,1)S(1)} all-gather(bf16[64,256]{1,0:T(8,128)(2,1)} %param.8), channel_id=1, replica_groups=mesh['blk'=32,'rep'=16] {'rep'}, dimensions={0}, use_global_device_ids=true | all-gather | bytes 557056 | tf_op jit(solution)/shard_map/all_gather | solution.py:97
  22.1 10.0 %collective-permute-start.2 = (bf16[512,256]{1,0:T(8,128)(2,1)S(1)}, bf16[512,256]{1,0:T(8,128)(2,1)S(1)}, u32[]{:S(2)}, u32[]{:S(2)}) collective-permute-start(bf16[512,256]{1,0:T(8,128)(2,1)S(1)} %get-tuple-element.18), channel_id=1, source_target_pairs={{256,0},{241,1},{226,2},{211,3},{196,4},{181,5},{166,6},{151,7},{1... | collective-permute-start | bytes 786440 | tf_op jit(solution)/shard_map/ppermute | solution.py:105
  34.1 6.5 %collective-permute-start.3 = (bf16[512,256]{1,0:T(8,128)(2,1)S(1)}, bf16[512,256]{1,0:T(8,128)(2,1)S(1)}, u32[]{:S(2)}, u32[]{:S(2)}) collective-permute-start(bf16[512,256]{1,0:T(8,128)(2,1)S(1)} %get-tuple-element.19), channel_id=1, source_target_pairs={{271,0},{254,1},{237,2},{220,3},{203,4},{186,5},{169,6},{152,7},{1... | collective-permute-start | bytes 786440 | tf_op jit(solution)/shard_map/ppermute | solution.py:105
  40.6 5.8 %collective-permute-start.1 = (bf16[512,256]{1,0:T(8,128)(2,1)S(1)}, bf16[512,256]{1,0:T(8,128)(2,1)S(1)}, u32[]{:S(2)}, u32[]{:S(2)}) collective-permute-start(bf16[512,256]{1,0:T(8,128)(2,1)S(1)} %get-tuple-element.19), channel_id=1, source_target_pairs={{15,0},{510,1},{493,2},{476,3},{459,4},{442,5},{425,6},{408,7},{39... | collective-permute-start | bytes 786440 | tf_op jit(solution)/shard_map/ppermute | solution.py:105
  55.4 14.8 %collective-permute-done.3 = bf16[512,256]{1,0:T(8,128)(2,1)S(1)} collective-permute-done((bf16[512,256]{1,0:T(8,128)(2,1)S(1)}, bf16[512,256]{1,0:T(8,128)(2,1)S(1)}, u32[]{:S(2)}, u32[]{:S(2)}) %collective-permute-start.3) | collective-permute-done | bytes 262176 | tf_op jit(solution)/shard_map/ppermute | solution.py:105
  70.9 15.8 %collective-permute-done.1 = bf16[512,256]{1,0:T(8,128)(2,1)S(1)} collective-permute-done((bf16[512,256]{1,0:T(8,128)(2,1)S(1)}, bf16[512,256]{1,0:T(8,128)(2,1)S(1)}, u32[]{:S(2)}, u32[]{:S(2)}) %collective-permute-start.1) | collective-permute-done | bytes 262176 | tf_op jit(solution)/shard_map/ppermute | solution.py:105
  90.1 10.7 %collective-permute-start.5 = (bf16[2,2,64,256]{3,2,1,0:T(8,128)(2,1)S(1)}, bf16[2,2,64,256]{3,2,1,0:T(8,128)(2,1)S(1)}, u32[]{:S(2)}, u32[]{:S(2)}) collective-permute-start(bf16[2,2,64,256]{3,2,1,0:T(8,128)(2,1)S(1)} %get-tuple-element.12), channel_id=1, source_target_pairs={{0,4},{1,5},{2,6},{3,7},{4,0},{5,1},{6,2},{7,3},{8,12},{9,13},{10,... | collective-permute-start | bytes 393224 | tf_op jit(solution)/shard_map/ppermute | solution.py:43
  110.2 7.3 %collective-permute-start.9 = (bf16[64,256]{1,0:T(8,128)(2,1)S(1)}, bf16[64,256]{1,0:T(8,128)(2,1)S(1)}, u32[]{:S(2)}, u32[]{:S(2)}) collective-permute-start(bf16[64,256]{1,0:T(8,128)(2,1)S(1)} %get-tuple-element.29), channel_id=1, source_target_pairs={{0,10},{1,11},{2,8},{3,9},{4,14},{5,15},{6,12},{7,13},{8,2},{9,3},... | collective-permute-start | bytes 98312 | tf_op jit(solution)/shard_map/ppermute | solution.py:43
  120.6 4.3 %collective-permute-done.8 = bf16[64,256]{1,0:T(8,128)(2,1)S(1)} collective-permute-done((bf16[64,256]{1,0:T(8,128)(2,1)S(1)}, bf16[64,256]{1,0:T(8,128)(2,1)S(1)}, u32[]{:S(2)}, u32[]{:S(2)}) %collective-permute-start.8) | collective-permute-done | bytes 32800 | tf_op jit(solution)/shard_map/ppermute | solution.py:43
  125.5 21.3 %all_gather.7 = bf16[1024,256]{1,0:T(8,128)(2,1)S(1)} all-gather(bf16[64,256]{1,0:T(8,128)(2,1)S(1)} %get-tuple-element.20), channel_id=1, replica_groups=mesh['blk'=32,'rep'=16] {'rep'}, dimensions={0}, use_global_device_ids=true | all-gather | bytes 557056 | tf_op jit(solution)/shard_map/all_gather | solution.py:133
  161.9 4.9 %collective-permute-start.23 = (f32[16,256]{1,0:T(8,128)S(1)}, f32[16,256]{1,0:T(8,128)S(1)}, u32[]{:S(2)}, u32[]{:S(2)}) collective-permute-start(f32[16,256]{1,0:T(8,128)S(1)} %get-tuple-element.31), channel_id=1, source_target_pairs={{0,8},{1,9},{2,10},{3,11},{4,12},{5,13},{6,14},{7,15},{8,0},{9,1},... | collective-permute-start | bytes 49160 | tf_op jit(solution)/shard_map/ppermute | solution.py:43
  166.9 5.1 %collective-permute-start.25 = (f32[16,256]{1,0:T(8,128)S(1)}, f32[16,256]{1,0:T(8,128)S(1)}, u32[]{:S(2)}, u32[]{:S(2)}) collective-permute-start(f32[16,256]{1,0:T(8,128)S(1)} %get-tuple-element.32), channel_id=1, source_target_pairs={{0,10},{1,11},{2,8},{3,9},{4,14},{5,15},{6,12},{7,13},{8,2},{9,3},... | collective-permute-start | bytes 49160 | tf_op jit(solution)/shard_map/ppermute | solution.py:43
  179.1 3.5 collective-permute-start.27
  182.7 5.0 %collective-permute-start.26 = (f32[17,256]{1,0:T(8,128)S(1)}, f32[17,256]{1,0:T(8,128)S(1)}, u32[]{:S(2)}, u32[]{:S(2)}) collective-permute-start(f32[17,256]{1,0:T(8,128)S(1)} %get-tuple-element.35), channel_id=1, source_target_pairs={{0,16},{16,0},{32,48},{48,32},{64,80},{80,64},{96,112},{112,96},{1... | collective-permute-start | bytes 52232 | tf_op jit(solution)/shard_map/ppermute | solution.py:59
  195.0 8.4 %collective-permute-start.29 = (f32[17,256]{1,0:T(8,128)S(1)}, f32[17,256]{1,0:T(8,128)S(1)}, u32[]{:S(2)}, u32[]{:S(2)}) collective-permute-start(f32[17,256]{1,0:T(8,128)S(1)} %bitcast.193), channel_id=1, source_target_pairs={{0,64},{16,80},{32,96},{48,112},{64,0},{80,16},{96,32},{112,48},{1... | collective-permute-start | bytes 52232 | tf_op jit(solution)/shard_map/ppermute | solution.py:59
  206.9 5.9 %collective-permute-start.13 = (bf16[512,256]{1,0:T(8,128)(2,1)S(1)}, bf16[512,256]{1,0:T(8,128)(2,1)S(1)}, u32[]{:S(2)}, u32[]{:S(2)}) collective-permute-start(bf16[512,256]{1,0:T(8,128)(2,1)S(1)} %get-tuple-element.17), channel_id=1, source_target_pairs={{0,271},{1,254},{2,237},{3,220},{4,203},{5,186},{6,169},{7,152},{8... | collective-permute-start | bytes 786440 | tf_op jit(solution)/shard_map/ppermute | solution.py:155
  212.8 7.9 %collective-permute-start.10 = (bf16[512,256]{1,0:T(8,128)(2,1)S(1)}, bf16[512,256]{1,0:T(8,128)(2,1)S(1)}, u32[]{:S(2)}, u32[]{:S(2)}) collective-permute-start(bf16[512,256]{1,0:T(8,128)(2,1)S(1)} %get-tuple-element.14), channel_id=1, source_target_pairs={{0,0},{1,497},{2,482},{3,467},{4,452},{5,437},{6,422},{7,407},{8,3... | collective-permute-start | bytes 786440 | tf_op jit(solution)/shard_map/ppermute | solution.py:155
  220.6 6.5 %collective-permute-start.12 = (bf16[512,256]{1,0:T(8,128)(2,1)S(1)}, bf16[512,256]{1,0:T(8,128)(2,1)S(1)}, u32[]{:S(2)}, u32[]{:S(2)}) collective-permute-start(bf16[512,256]{1,0:T(8,128)(2,1)S(1)} %get-tuple-element.15), channel_id=1, source_target_pairs={{0,15},{1,510},{2,493},{3,476},{4,459},{5,442},{6,425},{7,408},{8,... | collective-permute-start | bytes 786440 | tf_op jit(solution)/shard_map/ppermute | solution.py:155
  227.2 6.4 %collective-permute-start.30 = (f32[17,256]{1,0:T(8,128)S(1)}, f32[17,256]{1,0:T(8,128)S(1)}, u32[]{:S(2)}, u32[]{:S(2)}) collective-permute-start(f32[17,256]{1,0:T(8,128)S(1)} %bitcast.194), channel_id=1, source_target_pairs={{0,128},{16,144},{32,160},{48,176},{64,192},{80,208},{96,224},{112... | collective-permute-start | bytes 52232 | tf_op jit(solution)/shard_map/ppermute | solution.py:59
  233.7 16.5 %collective-permute-done.30 = f32[17,256]{1,0:T(8,128)S(1)} collective-permute-done((f32[17,256]{1,0:T(8,128)S(1)}, f32[17,256]{1,0:T(8,128)S(1)}, u32[]{:S(2)}, u32[]{:S(2)}) %collective-permute-start.30) | collective-permute-done | bytes 17440 | tf_op jit(solution)/shard_map/ppermute | solution.py:59
  250.2 8.8 %collective-permute-start.31 = (f32[17,256]{1,0:T(8,128)S(1)}, f32[17,256]{1,0:T(8,128)S(1)}, u32[]{:S(2)}, u32[]{:S(2)}) collective-permute-start(f32[17,256]{1,0:T(8,128)S(1)} %bitcast.195), channel_id=1, source_target_pairs={{0,192},{16,208},{32,224},{48,240},{64,128},{80,144},{96,160},{112... | collective-permute-start | bytes 52232 | tf_op jit(solution)/shard_map/ppermute | solution.py:59
  259.1 11.5 %collective-permute-done.31 = f32[17,256]{1,0:T(8,128)S(1)} collective-permute-done((f32[17,256]{1,0:T(8,128)S(1)}, f32[17,256]{1,0:T(8,128)S(1)}, u32[]{:S(2)}, u32[]{:S(2)}) %collective-permute-start.31) | collective-permute-done | bytes 17440 | tf_op jit(solution)/shard_map/ppermute | solution.py:59
  270.6 11.8 %collective-permute-start.32 = (f32[17,256]{1,0:T(8,128)S(1)}, f32[17,256]{1,0:T(8,128)S(1)}, u32[]{:S(2)}, u32[]{:S(2)}) collective-permute-start(f32[17,256]{1,0:T(8,128)S(1)} %bitcast.196), channel_id=1, source_target_pairs={{0,256},{16,272},{32,288},{48,304},{64,320},{80,336},{96,352},{112... | collective-permute-start | bytes 52232 | tf_op jit(solution)/shard_map/ppermute | solution.py:59
  285.3 6.7 %collective-permute-start.33 = (f32[17,256]{1,0:T(8,128)S(1)}, f32[17,256]{1,0:T(8,128)S(1)}, u32[]{:S(2)}, u32[]{:S(2)}) collective-permute-start(f32[17,256]{1,0:T(8,128)S(1)} %bitcast.197), channel_id=1, source_target_pairs={{0,320},{16,336},{32,352},{48,368},{64,256},{80,272},{96,288},{112... | collective-permute-start | bytes 52232 | tf_op jit(solution)/shard_map/ppermute | solution.py:59
  292.1 5.9 %collective-permute-done.33 = f32[17,256]{1,0:T(8,128)S(1)} collective-permute-done((f32[17,256]{1,0:T(8,128)S(1)}, f32[17,256]{1,0:T(8,128)S(1)}, u32[]{:S(2)}, u32[]{:S(2)}) %collective-permute-start.33) | collective-permute-done | bytes 17440 | tf_op jit(solution)/shard_map/ppermute | solution.py:59
  298.0 9.5 %collective-permute-start.34 = (f32[17,256]{1,0:T(8,128)S(1)}, f32[17,256]{1,0:T(8,128)S(1)}, u32[]{:S(2)}, u32[]{:S(2)}) collective-permute-start(f32[17,256]{1,0:T(8,128)S(1)} %bitcast.198), channel_id=1, source_target_pairs={{0,384},{16,400},{32,416},{48,432},{64,448},{80,464},{96,480},{112... | collective-permute-start | bytes 52232 | tf_op jit(solution)/shard_map/ppermute | solution.py:59
  309.3 7.2 %collective-permute-start.35 = (f32[17,256]{1,0:T(8,128)S(1)}, f32[17,256]{1,0:T(8,128)S(1)}, u32[]{:S(2)}, u32[]{:S(2)}) collective-permute-start(f32[17,256]{1,0:T(8,128)S(1)} %bitcast.199), channel_id=1, source_target_pairs={{0,448},{16,464},{32,480},{48,496},{64,384},{80,400},{96,416},{112... | collective-permute-start | bytes 52232 | tf_op jit(solution)/shard_map/ppermute | solution.py:59
  316.6 4.2 %collective-permute-done.35 = f32[17,256]{1,0:T(8,128)S(1)} collective-permute-done((f32[17,256]{1,0:T(8,128)S(1)}, f32[17,256]{1,0:T(8,128)S(1)}, u32[]{:S(2)}, u32[]{:S(2)}) %collective-permute-start.35) | collective-permute-done | bytes 17440 | tf_op jit(solution)/shard_map/ppermute | solution.py:59
  323.6 28.7 %collective-permute-start.16 = (bf16[2,2,64,256]{3,2,1,0:T(8,128)(2,1)S(1)}, bf16[2,2,64,256]{3,2,1,0:T(8,128)(2,1)S(1)}, u32[]{:S(2)}, u32[]{:S(2)}) collective-permute-start(bf16[2,2,64,256]{3,2,1,0:T(8,128)(2,1)S(1)} %get-tuple-element.9), channel_id=1, source_target_pairs={{0,5},{1,4},{2,7},{3,6},{4,1},{5,0},{6,3},{7,2},{8,13},{9,12},{10,... | collective-permute-start | bytes 393224 | tf_op jit(solution)/shard_map/ppermute | solution.py:43
  356.2 3.5 collective-permute-done.15
  361.6 18.4 %collective-permute-start.19 = (bf16[64,256]{1,0:T(8,128)(2,1)S(1)}, bf16[64,256]{1,0:T(8,128)(2,1)S(1)}, u32[]{:S(2)}, u32[]{:S(2)}) collective-permute-start(bf16[64,256]{1,0:T(8,128)(2,1)S(1)} %get-tuple-element.26), channel_id=1, source_target_pairs={{0,10},{1,11},{2,8},{3,9},{4,14},{5,15},{6,12},{7,13},{8,2},{9,3},... | collective-permute-start | bytes 98312 | tf_op jit(solution)/shard_map/ppermute | solution.py:43
  383.1 4.2 %collective-permute-done.18 = bf16[64,256]{1,0:T(8,128)(2,1)S(1)} collective-permute-done((bf16[64,256]{1,0:T(8,128)(2,1)S(1)}, bf16[64,256]{1,0:T(8,128)(2,1)S(1)}, u32[]{:S(2)}, u32[]{:S(2)}) %collective-permute-start.18) | collective-permute-done | bytes 32800 | tf_op jit(solution)/shard_map/ppermute | solution.py:43
  (113 shorter events, 78.1 us)
Async XLA Ops:
  22.1 33.2 %collective-permute-start.2 = (bf16[512,256]{1,0:T(8,128)(2,1)S(1)}, bf16[512,256]{1,0:T(8,128)(2,1)S(1)}, u32[]{:S(2)}, u32[]{:S(2)}) collective-permute-start(bf16[512,256]{1,0:T(8,128)(2,1)S(1)} %get-tuple-element.18), channel_id=1, source_target_pairs={{256,0},{241,1},{226,2},{211,3},{196,4},{181,5},{166,6},{151,7},{1... | collective-permute-start | bytes 786440 | tf_op jit(solution)/shard_map/ppermute | solution.py:105
  32.2 38.7 %collective-permute-start = (bf16[512,256]{1,0:T(8,128)(2,1)S(1)}, bf16[512,256]{1,0:T(8,128)(2,1)S(1)}, u32[]{:S(2)}, u32[]{:S(2)}) collective-permute-start(bf16[512,256]{1,0:T(8,128)(2,1)S(1)} %get-tuple-element.18), channel_id=1, source_target_pairs={{0,0},{497,1},{482,2},{467,3},{452,4},{437,5},{422,6},{407,7},{392... | collective-permute-start | bytes 786440 | tf_op jit(solution)/shard_map/ppermute | solution.py:105
  34.1 36.0 %collective-permute-start.3 = (bf16[512,256]{1,0:T(8,128)(2,1)S(1)}, bf16[512,256]{1,0:T(8,128)(2,1)S(1)}, u32[]{:S(2)}, u32[]{:S(2)}) collective-permute-start(bf16[512,256]{1,0:T(8,128)(2,1)S(1)} %get-tuple-element.19), channel_id=1, source_target_pairs={{271,0},{254,1},{237,2},{220,3},{203,4},{186,5},{169,6},{152,7},{1... | collective-permute-start | bytes 786440 | tf_op jit(solution)/shard_map/ppermute | solution.py:105
  40.6 46.1 %collective-permute-start.1 = (bf16[512,256]{1,0:T(8,128)(2,1)S(1)}, bf16[512,256]{1,0:T(8,128)(2,1)S(1)}, u32[]{:S(2)}, u32[]{:S(2)}) collective-permute-start(bf16[512,256]{1,0:T(8,128)(2,1)S(1)} %get-tuple-element.19), channel_id=1, source_target_pairs={{15,0},{510,1},{493,2},{476,3},{459,4},{442,5},{425,6},{408,7},{39... | collective-permute-start | bytes 786440 | tf_op jit(solution)/shard_map/ppermute | solution.py:105
  88.1 14.8 %collective-permute-start.4 = (bf16[2,2,64,256]{3,2,1,0:T(8,128)(2,1)S(1)}, bf16[2,2,64,256]{3,2,1,0:T(8,128)(2,1)S(1)}, u32[]{:S(2)}, u32[]{:S(2)}) collective-permute-start(bf16[2,2,64,256]{3,2,1,0:T(8,128)(2,1)S(1)} %get-tuple-element.11), channel_id=1, source_target_pairs={{0,1},{1,0},{2,3},{3,2},{4,5},{5,4},{6,7},{7,6},{8,9},{9,8},{10,11... | collective-permute-start | bytes 393224 | tf_op jit(solution)/shard_map/ppermute | solution.py:43
  90.1 14.9 %collective-permute-start.5 = (bf16[2,2,64,256]{3,2,1,0:T(8,128)(2,1)S(1)}, bf16[2,2,64,256]{3,2,1,0:T(8,128)(2,1)S(1)}, u32[]{:S(2)}, u32[]{:S(2)}) collective-permute-start(bf16[2,2,64,256]{3,2,1,0:T(8,128)(2,1)S(1)} %get-tuple-element.12), channel_id=1, source_target_pairs={{0,4},{1,5},{2,6},{3,7},{4,0},{5,1},{6,2},{7,3},{8,12},{9,13},{10,... | collective-permute-start | bytes 393224 | tf_op jit(solution)/shard_map/ppermute | solution.py:43
  100.8 7.4 %collective-permute-start.6 = (bf16[2,2,64,256]{3,2,1,0:T(8,128)(2,1)S(1)}, bf16[2,2,64,256]{3,2,1,0:T(8,128)(2,1)S(1)}, u32[]{:S(2)}, u32[]{:S(2)}) collective-permute-start(bf16[2,2,64,256]{3,2,1,0:T(8,128)(2,1)S(1)} %get-tuple-element.13), channel_id=1, source_target_pairs={{0,5},{1,4},{2,7},{3,6},{4,1},{5,0},{6,3},{7,2},{8,13},{9,12},{10,... | collective-permute-start | bytes 393224 | tf_op jit(solution)/shard_map/ppermute | solution.py:43
  108.3 12.3 %collective-permute-start.7 = (bf16[64,256]{1,0:T(8,128)(2,1)S(1)}, bf16[64,256]{1,0:T(8,128)(2,1)S(1)}, u32[]{:S(2)}, u32[]{:S(2)}) collective-permute-start(bf16[64,256]{1,0:T(8,128)(2,1)S(1)} %get-tuple-element.28), channel_id=1, source_target_pairs={{0,8},{1,9},{2,10},{3,11},{4,12},{5,13},{6,14},{7,15},{8,0},{9,1},... | collective-permute-start | bytes 98312 | tf_op jit(solution)/shard_map/ppermute | solution.py:43
  110.2 10.3 %collective-permute-start.9 = (bf16[64,256]{1,0:T(8,128)(2,1)S(1)}, bf16[64,256]{1,0:T(8,128)(2,1)S(1)}, u32[]{:S(2)}, u32[]{:S(2)}) collective-permute-start(bf16[64,256]{1,0:T(8,128)(2,1)S(1)} %get-tuple-element.29), channel_id=1, source_target_pairs={{0,10},{1,11},{2,8},{3,9},{4,14},{5,15},{6,12},{7,13},{8,2},{9,3},... | collective-permute-start | bytes 98312 | tf_op jit(solution)/shard_map/ppermute | solution.py:43
  117.5 7.3 %collective-permute-start.8 = (bf16[64,256]{1,0:T(8,128)(2,1)S(1)}, bf16[64,256]{1,0:T(8,128)(2,1)S(1)}, u32[]{:S(2)}, u32[]{:S(2)}) collective-permute-start(bf16[64,256]{1,0:T(8,128)(2,1)S(1)} %get-tuple-element.30), channel_id=1, source_target_pairs={{0,2},{1,3},{2,0},{3,1},{4,6},{5,7},{6,4},{7,5},{8,10},{9,11},{10,... | collective-permute-start | bytes 98312 | tf_op jit(solution)/shard_map/ppermute | solution.py:43
  150.2 8.7 %collective-permute-start.20 = (f32[2,2,16,256]{3,2,1,0:T(8,128)S(1)}, f32[2,2,16,256]{3,2,1,0:T(8,128)S(1)}, u32[]{:S(2)}, u32[]{:S(2)}) collective-permute-start(f32[2,2,16,256]{3,2,1,0:T(8,128)S(1)} %get-tuple-element.22), channel_id=1, source_target_pairs={{0,1},{1,0},{2,3},{3,2},{4,5},{5,4},{6,7},{7,6},{8,9},{9,8},{10,11... | collective-permute-start | bytes 196616 | tf_op jit(solution)/shard_map/ppermute | solution.py:43
  161.9 12.4 %collective-permute-start.23 = (f32[16,256]{1,0:T(8,128)S(1)}, f32[16,256]{1,0:T(8,128)S(1)}, u32[]{:S(2)}, u32[]{:S(2)}) collective-permute-start(f32[16,256]{1,0:T(8,128)S(1)} %get-tuple-element.31), channel_id=1, source_target_pairs={{0,8},{1,9},{2,10},{3,11},{4,12},{5,13},{6,14},{7,15},{8,0},{9,1},... | collective-permute-start | bytes 49160 | tf_op jit(solution)/shard_map/ppermute | solution.py:43
  166.9 9.5 %collective-permute-start.25 = (f32[16,256]{1,0:T(8,128)S(1)}, f32[16,256]{1,0:T(8,128)S(1)}, u32[]{:S(2)}, u32[]{:S(2)}) collective-permute-start(f32[16,256]{1,0:T(8,128)S(1)} %get-tuple-element.32), channel_id=1, source_target_pairs={{0,10},{1,11},{2,8},{3,9},{4,14},{5,15},{6,12},{7,13},{8,2},{9,3},... | collective-permute-start | bytes 49160 | tf_op jit(solution)/shard_map/ppermute | solution.py:43
  179.1 12.0 %collective-permute-start.27 = (f32[17,256]{1,0:T(8,128)S(1)}, f32[17,256]{1,0:T(8,128)S(1)}, u32[]{:S(2)}, u32[]{:S(2)}) collective-permute-start(f32[17,256]{1,0:T(8,128)S(1)} %get-tuple-element.35), channel_id=1, source_target_pairs={{0,32},{16,48},{32,0},{48,16},{64,96},{80,112},{96,64},{112,80},{1... | collective-permute-start | bytes 52232 | tf_op jit(solution)/shard_map/ppermute | solution.py:59
  182.7 8.5 %collective-permute-start.26 = (f32[17,256]{1,0:T(8,128)S(1)}, f32[17,256]{1,0:T(8,128)S(1)}, u32[]{:S(2)}, u32[]{:S(2)}) collective-permute-start(f32[17,256]{1,0:T(8,128)S(1)} %get-tuple-element.35), channel_id=1, source_target_pairs={{0,16},{16,0},{32,48},{48,32},{64,80},{80,64},{96,112},{112,96},{1... | collective-permute-start | bytes 52232 | tf_op jit(solution)/shard_map/ppermute | solution.py:59
  195.0 32.2 %collective-permute-start.29 = (f32[17,256]{1,0:T(8,128)S(1)}, f32[17,256]{1,0:T(8,128)S(1)}, u32[]{:S(2)}, u32[]{:S(2)}) collective-permute-start(f32[17,256]{1,0:T(8,128)S(1)} %bitcast.193), channel_id=1, source_target_pairs={{0,64},{16,80},{32,96},{48,112},{64,0},{80,16},{96,32},{112,48},{1... | collective-permute-start | bytes 52232 | tf_op jit(solution)/shard_map/ppermute | solution.py:59
  203.4 117.9 %collective-permute-start.11 = (bf16[512,256]{1,0:T(8,128)(2,1)S(1)}, bf16[512,256]{1,0:T(8,128)(2,1)S(1)}, u32[]{:S(2)}, u32[]{:S(2)}) collective-permute-start(bf16[512,256]{1,0:T(8,128)(2,1)S(1)} %get-tuple-element.16), channel_id=1, source_target_pairs={{0,256},{1,241},{2,226},{3,211},{4,196},{5,181},{6,166},{7,151},{8... | collective-permute-start | bytes 786440 | tf_op jit(solution)/shard_map/ppermute | solution.py:155
  206.9 114.6 %collective-permute-start.13 = (bf16[512,256]{1,0:T(8,128)(2,1)S(1)}, bf16[512,256]{1,0:T(8,128)(2,1)S(1)}, u32[]{:S(2)}, u32[]{:S(2)}) collective-permute-start(bf16[512,256]{1,0:T(8,128)(2,1)S(1)} %get-tuple-element.17), channel_id=1, source_target_pairs={{0,271},{1,254},{2,237},{3,220},{4,203},{5,186},{6,169},{7,152},{8... | collective-permute-start | bytes 786440 | tf_op jit(solution)/shard_map/ppermute | solution.py:155
  212.8 108.6 %collective-permute-start.10 = (bf16[512,256]{1,0:T(8,128)(2,1)S(1)}, bf16[512,256]{1,0:T(8,128)(2,1)S(1)}, u32[]{:S(2)}, u32[]{:S(2)}) collective-permute-start(bf16[512,256]{1,0:T(8,128)(2,1)S(1)} %get-tuple-element.14), channel_id=1, source_target_pairs={{0,0},{1,497},{2,482},{3,467},{4,452},{5,437},{6,422},{7,407},{8,3... | collective-permute-start | bytes 786440 | tf_op jit(solution)/shard_map/ppermute | solution.py:155
  220.6 100.8 %collective-permute-start.12 = (bf16[512,256]{1,0:T(8,128)(2,1)S(1)}, bf16[512,256]{1,0:T(8,128)(2,1)S(1)}, u32[]{:S(2)}, u32[]{:S(2)}) collective-permute-start(bf16[512,256]{1,0:T(8,128)(2,1)S(1)} %get-tuple-element.15), channel_id=1, source_target_pairs={{0,15},{1,510},{2,493},{3,476},{4,459},{5,442},{6,425},{7,408},{8,... | collective-permute-start | bytes 786440 | tf_op jit(solution)/shard_map/ppermute | solution.py:155
  227.2 23.0 %collective-permute-start.30 = (f32[17,256]{1,0:T(8,128)S(1)}, f32[17,256]{1,0:T(8,128)S(1)}, u32[]{:S(2)}, u32[]{:S(2)}) collective-permute-start(f32[17,256]{1,0:T(8,128)S(1)} %bitcast.194), channel_id=1, source_target_pairs={{0,128},{16,144},{32,160},{48,176},{64,192},{80,208},{96,224},{112... | collective-permute-start | bytes 52232 | tf_op jit(solution)/shard_map/ppermute | solution.py:59
  250.2 20.4 %collective-permute-start.31 = (f32[17,256]{1,0:T(8,128)S(1)}, f32[17,256]{1,0:T(8,128)S(1)}, u32[]{:S(2)}, u32[]{:S(2)}) collective-permute-start(f32[17,256]{1,0:T(8,128)S(1)} %bitcast.195), channel_id=1, source_target_pairs={{0,192},{16,208},{32,224},{48,240},{64,128},{80,144},{96,160},{112... | collective-permute-start | bytes 52232 | tf_op jit(solution)/shard_map/ppermute | solution.py:59
  270.6 14.8 %collective-permute-start.32 = (f32[17,256]{1,0:T(8,128)S(1)}, f32[17,256]{1,0:T(8,128)S(1)}, u32[]{:S(2)}, u32[]{:S(2)}) collective-permute-start(f32[17,256]{1,0:T(8,128)S(1)} %bitcast.196), channel_id=1, source_target_pairs={{0,256},{16,272},{32,288},{48,304},{64,320},{80,336},{96,352},{112... | collective-permute-start | bytes 52232 | tf_op jit(solution)/shard_map/ppermute | solution.py:59
  285.3 12.6 %collective-permute-start.33 = (f32[17,256]{1,0:T(8,128)S(1)}, f32[17,256]{1,0:T(8,128)S(1)}, u32[]{:S(2)}, u32[]{:S(2)}) collective-permute-start(f32[17,256]{1,0:T(8,128)S(1)} %bitcast.197), channel_id=1, source_target_pairs={{0,320},{16,336},{32,352},{48,368},{64,256},{80,272},{96,288},{112... | collective-permute-start | bytes 52232 | tf_op jit(solution)/shard_map/ppermute | solution.py:59
  298.0 11.3 %collective-permute-start.34 = (f32[17,256]{1,0:T(8,128)S(1)}, f32[17,256]{1,0:T(8,128)S(1)}, u32[]{:S(2)}, u32[]{:S(2)}) collective-permute-start(f32[17,256]{1,0:T(8,128)S(1)} %bitcast.198), channel_id=1, source_target_pairs={{0,384},{16,400},{32,416},{48,432},{64,448},{80,464},{96,480},{112... | collective-permute-start | bytes 52232 | tf_op jit(solution)/shard_map/ppermute | solution.py:59
  309.3 11.4 %collective-permute-start.35 = (f32[17,256]{1,0:T(8,128)S(1)}, f32[17,256]{1,0:T(8,128)S(1)}, u32[]{:S(2)}, u32[]{:S(2)}) collective-permute-start(f32[17,256]{1,0:T(8,128)S(1)} %bitcast.199), channel_id=1, source_target_pairs={{0,448},{16,464},{32,480},{48,496},{64,384},{80,400},{96,416},{112... | collective-permute-start | bytes 52232 | tf_op jit(solution)/shard_map/ppermute | solution.py:59
  321.7 32.6 %collective-permute-start.14 = (bf16[2,2,64,256]{3,2,1,0:T(8,128)(2,1)S(1)}, bf16[2,2,64,256]{3,2,1,0:T(8,128)(2,1)S(1)}, u32[]{:S(2)}, u32[]{:S(2)}) collective-permute-start(bf16[2,2,64,256]{3,2,1,0:T(8,128)(2,1)S(1)} %get-tuple-element.8), channel_id=1, source_target_pairs={{0,1},{1,0},{2,3},{3,2},{4,5},{5,4},{6,7},{7,6},{8,9},{9,8},{10,11... | collective-permute-start | bytes 393224 | tf_op jit(solution)/shard_map/ppermute | solution.py:43
  323.6 32.5 %collective-permute-start.16 = (bf16[2,2,64,256]{3,2,1,0:T(8,128)(2,1)S(1)}, bf16[2,2,64,256]{3,2,1,0:T(8,128)(2,1)S(1)}, u32[]{:S(2)}, u32[]{:S(2)}) collective-permute-start(bf16[2,2,64,256]{3,2,1,0:T(8,128)(2,1)S(1)} %get-tuple-element.9), channel_id=1, source_target_pairs={{0,5},{1,4},{2,7},{3,6},{4,1},{5,0},{6,3},{7,2},{8,13},{9,12},{10,... | collective-permute-start | bytes 393224 | tf_op jit(solution)/shard_map/ppermute | solution.py:43
  352.3 7.3 %collective-permute-start.15 = (bf16[2,2,64,256]{3,2,1,0:T(8,128)(2,1)S(1)}, bf16[2,2,64,256]{3,2,1,0:T(8,128)(2,1)S(1)}, u32[]{:S(2)}, u32[]{:S(2)}) collective-permute-start(bf16[2,2,64,256]{3,2,1,0:T(8,128)(2,1)S(1)} %get-tuple-element.10), channel_id=1, source_target_pairs={{0,4},{1,5},{2,6},{3,7},{4,0},{5,1},{6,2},{7,3},{8,12},{9,13},{10,... | collective-permute-start | bytes 393224 | tf_op jit(solution)/shard_map/ppermute | solution.py:43
  359.7 23.4 %collective-permute-start.17 = (bf16[64,256]{1,0:T(8,128)(2,1)S(1)}, bf16[64,256]{1,0:T(8,128)(2,1)S(1)}, u32[]{:S(2)}, u32[]{:S(2)}) collective-permute-start(bf16[64,256]{1,0:T(8,128)(2,1)S(1)} %get-tuple-element.25), channel_id=1, source_target_pairs={{0,8},{1,9},{2,10},{3,11},{4,12},{5,13},{6,14},{7,15},{8,0},{9,1},... | collective-permute-start | bytes 98312 | tf_op jit(solution)/shard_map/ppermute | solution.py:43
  361.6 21.5 %collective-permute-start.19 = (bf16[64,256]{1,0:T(8,128)(2,1)S(1)}, bf16[64,256]{1,0:T(8,128)(2,1)S(1)}, u32[]{:S(2)}, u32[]{:S(2)}) collective-permute-start(bf16[64,256]{1,0:T(8,128)(2,1)S(1)} %get-tuple-element.26), channel_id=1, source_target_pairs={{0,10},{1,11},{2,8},{3,9},{4,14},{5,15},{6,12},{7,13},{8,2},{9,3},... | collective-permute-start | bytes 98312 | tf_op jit(solution)/shard_map/ppermute | solution.py:43
  380.0 7.3 %collective-permute-start.18 = (bf16[64,256]{1,0:T(8,128)(2,1)S(1)}, bf16[64,256]{1,0:T(8,128)(2,1)S(1)}, u32[]{:S(2)}, u32[]{:S(2)}) collective-permute-start(bf16[64,256]{1,0:T(8,128)(2,1)S(1)} %get-tuple-element.27), channel_id=1, source_target_pairs={{0,2},{1,3},{2,0},{3,1},{4,6},{5,7},{6,4},{7,5},{8,10},{9,11},{10,... | collective-permute-start | bytes 98312 | tf_op jit(solution)/shard_map/ppermute | solution.py:43
  (12 other events, 251.1 us)

commit v8 on v4

--- a/solution.py
+++ b/solution.py
@@ -123,7 +123,10 @@
     )
     weight_part = rep_reduce_scatter(weight_terms, jnp.float32)
     bias_part = jnp.sum(grad_block.astype(jnp.float32), axis=0)
-    totals = blk_all_reduce(jnp.concatenate([weight_part, bias_part[None, :]], axis=0))
+    gathered = lax.all_gather(jnp.concatenate([weight_part, bias_part[None, :]], axis=0), "blk")
+    totals = gathered[0]
+    for block in range(1, blocks):
+        totals = totals + gathered[block]
     returned = [jnp.zeros((half_rows, partition.shape[1]), jnp.float32) for _ in range(2)]
     for slot in range(pair_slots):
         partial = lax.dot_general(

time: 328 us -> 366 us (1.12)
  blocking collectives: 45.8 us -> 119 us
  starting transfers between devices: 140 us -> 109 us
  waiting for transfers between devices: 113 us -> 109 us
    all_gather x0 -> x1, blocking collectives: none -> 73 us  [body(): lax.all_gather(jnp.concatenate([weight_part, bias_part[None, :]], axis=0)...]
    ppermute x5 -> x0, starting transfers between devices: 30 us -> none  [blk_all_reduce(): x = x + lax.ppermute(x, 'blk', [(i, i ^ step) for i in range(blocks)])]
    ppermute x5 -> x0, waiting for transfers between devices: 6.97 us -> none  [blk_all_reduce(): x = x + lax.ppermute(x, 'blk', [(i, i ^ step) for i in range(blocks)])]
  transfers between devices with their start and end apart: 25 -> 20, of which waited for: 14 -> 12; matrix products, arithmetic and copies ran while one was open for 5% -> 4% of each run, Pallas kernels for 0% -> 0%
where the time goes in v8:
time: 366 us; the launch traced here: 364 us
  blocking collectives  119 us (33%)
  starting transfers between devices  109 us (30%)
  waiting for transfers between devices  109 us (30%)
  matrix products  11.3 us (3%)
  local copies, waits for them, and re-layouts  9.76 us (3%)
  other arithmetic  5.33 us (1%)
    all_gather x1, blocking collectives, body(): lax.all_gather(jnp.concatenate([weight_part, bias_part[None, :]], axis=0)...  73 us
    ppermute x12, starting transfers between devices, rep_reduce_scatter(): got = lax.ppermute(send.astype(wire_dtype), 'rep', partner)  65.3 us
    ppermute x4, waiting for transfers between devices, body(): lax.ppermute(partial[half * half_rows:(half + 1) * half_rows], both_axes,...  57.4 us
    ppermute x4, waiting for transfers between devices, body(): lax.ppermute(partition[half * half_rows:(half + 1) * half_rows], both_axe...  32.5 us
    ppermute x4, starting transfers between devices, body(): lax.ppermute(partition[half * half_rows:(half + 1) * half_rows], both_axe...  24.2 us
    all_gather x1, blocking collectives, body(): partition = lax.all_gather(feats, 'rep', axis=0, tiled=True)  23.2 us
    all_gather x1, blocking collectives, body(): grad_block = lax.all_gather(grad_rows, 'rep', axis=0, tiled=True)  22.6 us
    ppermute x4, starting transfers between devices, body(): lax.ppermute(partial[half * half_rows:(half + 1) * half_rows], both_axes,...  19.5 us
  transfers between devices with their start and end apart: 20, of which 12 were waited for; matrix products, arithmetic and copies ran while one was open for 4% of the time, Pallas kernels for 0%

profile of v8, /device:TPU:6, one launch (start us, length us, event | category | flops | bytes accessed | tf_op | source)
XLA Modules:
  0.0 364.3 jit_solution(9410028266810295394)
XLA Ops:
  0.6 23.2 %all_gather.12 = bf16[1024,256]{1,0:T(8,128)(2,1)S(1)} all-gather(bf16[64,256]{1,0:T(8,128)(2,1)} %param.8), channel_id=1, replica_groups=mesh['blk'=32,'rep'=16] {'rep'}, dimensions={0}, use_global_device_ids=true | all-gather | bytes 557056 | tf_op jit(solution)/shard_map/all_gather | solution.py:81
  23.9 11.4 %collective-permute-start.2 = (bf16[512,256]{1,0:T(8,128)(2,1)S(1)}, bf16[512,256]{1,0:T(8,128)(2,1)S(1)}, u32[]{:S(2)}, u32[]{:S(2)}) collective-permute-start(bf16[512,256]{1,0:T(8,128)(2,1)S(1)} %get-tuple-element.10), channel_id=1, source_target_pairs={{256,0},{241,1},{226,2},{211,3},{196,4},{181,5},{166,6},{151,7},{1... | collective-permute-start | bytes 786440 | tf_op jit(solution)/shard_map/ppermute | solution.py:89
  35.3 1.9 collective-permute-start
  37.2 8.8 %collective-permute-start.3 = (bf16[512,256]{1,0:T(8,128)(2,1)S(1)}, bf16[512,256]{1,0:T(8,128)(2,1)}, u32[]{:S(2)}, u32[]{:S(2)}) collective-permute-start(bf16[512,256]{1,0:T(8,128)(2,1)S(1)} %get-tuple-element.11), channel_id=1, source_target_pairs={{271,0},{254,1},{237,2},{220,3},{203,4},{186,5},{169,6},{152,7},{1... | collective-permute-start | bytes 786440 | tf_op jit(solution)/shard_map/ppermute | solution.py:89
  46.0 2.0 collective-permute-start.1
  50.7 4.0 %fusion.76 = (bf16[1,1,1,64,128,128]{5,4,3,2,1,0:T(8,128)(2,1)}, bf16[1,1,1,64,128,128]{5,4,3,2,1,0:T(8,128)(2,1)S(1)}) fusion(bf16[1,1,2,64,128,128]{5,4,3,2,1,0:T(8,128)(2,1)} %param.12), kind=kLoop, calls=%fused_computation.141 | loop fusion | bytes 8388608 | tf_op jit(solution)/shard_map/slice | solution.py:99
  54.8 3.3 convolution_convert_fusion.1
  59.8 6.1 %collective-permute-done.2 = bf16[512,256]{1,0:T(8,128)(2,1)S(1)} collective-permute-done((bf16[512,256]{1,0:T(8,128)(2,1)S(1)}, bf16[512,256]{1,0:T(8,128)(2,1)S(1)}, u32[]{:S(2)}, u32[]{:S(2)}) %collective-permute-start.2) | collective-permute-done | bytes 262176 | tf_op jit(solution)/shard_map/ppermute | solution.py:89
  65.9 26.3 %collective-permute-done.3 = bf16[512,256]{1,0:T(8,128)(2,1)} collective-permute-done((bf16[512,256]{1,0:T(8,128)(2,1)S(1)}, bf16[512,256]{1,0:T(8,128)(2,1)}, u32[]{:S(2)}, u32[]{:S(2)}) %collective-permute-start.3) | collective-permute-done | bytes 262176 | tf_op jit(solution)/shard_map/ppermute | solution.py:89
  95.3 1.9 collective-permute-start.4
  99.7 2.1 collective-permute-start.5
  101.7 5.6 %collective-permute-done.5 = bf16[2,2,64,256]{3,2,1,0:T(8,128)(2,1)} collective-permute-done((bf16[2,2,64,256]{3,2,1,0:T(8,128)(2,1)S(1)}, bf16[2,2,64,256]{3,2,1,0:T(8,128)(2,1)}, u32[]{:S(2)}, u32[]{:S(2)}) %collective-permute-start.5) | collective-permute-done | bytes 131104 | tf_op jit(solution)/shard_map/ppermute | solution.py:37
  109.0 15.6 %collective-permute-start.6 = (bf16[2,64,256]{2,1,0:T(8,128)(2,1)}, bf16[2,64,256]{2,1,0:T(8,128)(2,1)}, u32[]{:S(2)}, u32[]{:S(2)}) collective-permute-start(bf16[2,64,256]{2,1,0:T(8,128)(2,1)} %fusion.35), channel_id=1, source_target_pairs={{0,8},{1,9},{2,10},{3,11},{4,12},{5,13},{6,14},{7,15},{8,0},{9,1},... | collective-permute-start | bytes 196616 | tf_op jit(solution)/shard_map/ppermute | solution.py:37
  124.6 2.5 collective-permute-done.6
  128.7 8.4 %collective-permute-start.7 = (bf16[64,256]{1,0:T(8,128)(2,1)S(1)}, bf16[64,256]{1,0:T(8,128)(2,1)S(1)}, u32[]{:S(2)}, u32[]{:S(2)}) collective-permute-start(bf16[64,256]{1,0:T(8,128)(2,1)S(1)} %fusion.39), channel_id=1, source_target_pairs={{0,2},{1,3},{2,0},{3,1},{4,6},{5,7},{6,4},{7,5},{8,10},{9,11},{10,... | collective-permute-start | bytes 98312 | tf_op jit(solution)/shard_map/ppermute | solution.py:37
  140.4 22.6 %all_gather.13 = bf16[1024,256]{1,0:T(8,128)(2,1)S(1)} all-gather(bf16[64,256]{1,0:T(8,128)(2,1)S(1)} %get-tuple-element.12), channel_id=1, replica_groups=mesh['blk'=32,'rep'=16] {'rep'}, dimensions={0}, use_global_device_ids=true | all-gather | bytes 557056 | tf_op jit(solution)/shard_map/all_gather | solution.py:116
  166.6 2.3 collective-permute-start.16
  169.8 2.3 collective-permute-start.17
  172.3 1.9 collective-permute-start.9
  174.2 11.5 %collective-permute-start.11 = (bf16[512,256]{1,0:T(8,128)(2,1)S(1)}, bf16[512,256]{1,0:T(8,128)(2,1)S(1)}, u32[]{:S(2)}, u32[]{:S(2)}) collective-permute-start(bf16[512,256]{1,0:T(8,128)(2,1)S(1)} %get-tuple-element.9), channel_id=1, source_target_pairs={{0,271},{1,254},{2,237},{3,220},{4,203},{5,186},{6,169},{7,152},{8... | collective-permute-start | bytes 786440 | tf_op jit(solution)/shard_map/ppermute | solution.py:139
  185.7 2.7 collective-permute-start.8
  188.4 3.4 collective-permute-start.10
  191.9 10.8 %collective-permute-start.18 = (f32[2,16,256]{2,1,0:T(8,128)S(1)}, f32[2,16,256]{2,1,0:T(8,128)S(1)}, u32[]{:S(2)}, u32[]{:S(2)}) collective-permute-start(f32[2,16,256]{2,1,0:T(8,128)S(1)} %dynamic-slice_bitcast_fusion.2), channel_id=1, source_target_pairs={{0,8},{1,9},{2,10},{3,11},{4,12},{5,13},{6,14},{7,15},{8,0},{9,1},... | collective-permute-start | bytes 98312 | tf_op jit(solution)/shard_map/ppermute | solution.py:37
  202.7 29.3 %collective-permute-done.8 = bf16[512,256]{1,0:T(8,128)(2,1)S(1)} collective-permute-done((bf16[512,256]{1,0:T(8,128)(2,1)S(1)}, bf16[512,256]{1,0:T(8,128)(2,1)S(1)}, u32[]{:S(2)}, u32[]{:S(2)}) %collective-permute-start.8) | collective-permute-done | bytes 262176 | tf_op jit(solution)/shard_map/ppermute | solution.py:139
  232.1 28.1 %collective-permute-done.11 = bf16[512,256]{1,0:T(8,128)(2,1)S(1)} collective-permute-done((bf16[512,256]{1,0:T(8,128)(2,1)S(1)}, bf16[512,256]{1,0:T(8,128)(2,1)S(1)}, u32[]{:S(2)}, u32[]{:S(2)}) %collective-permute-start.11) | collective-permute-done | bytes 262176 | tf_op jit(solution)/shard_map/ppermute | solution.py:139
  260.4 1.9 collective-permute-start.12
  262.4 1.9 collective-permute-start.19
  266.3 3.2 collective-permute-done.19
  269.5 2.7 collective-permute-done.13
  272.3 10.4 %collective-permute-start.14 = (bf16[2,64,256]{2,1,0:T(8,128)(2,1)S(1)}, bf16[2,64,256]{2,1,0:T(8,128)(2,1)S(1)}, u32[]{:S(2)}, u32[]{:S(2)}) collective-permute-start(bf16[2,64,256]{2,1,0:T(8,128)(2,1)S(1)} %fusion.36), channel_id=1, source_target_pairs={{0,8},{1,9},{2,10},{3,11},{4,12},{5,13},{6,14},{7,15},{8,0},{9,1},... | collective-permute-start | bytes 196616 | tf_op jit(solution)/shard_map/ppermute | solution.py:37
  282.6 73.0 %all-gather.1 = f32[32,17,256]{2,1,0:T(8,128)S(1)} all-gather(f32[1,17,256]{2,1,0:T(8,128)S(1)} %maximum_bitcast_fusion), channel_id=2, replica_groups=mesh['blk'=32,'rep'=16] {'blk'}, dimensions={0}, use_global_device_ids=true | all-gather | bytes 574464 | tf_op jit(solution)/shard_map/all_gather | solution.py:126
  355.7 5.9 %collective-permute-start.15 = (bf16[64,256]{1,0:T(8,128)(2,1)S(1)}, bf16[64,256]{1,0:T(8,128)(2,1)S(1)}, u32[]{:S(2)}, u32[]{:S(2)}) collective-permute-start(bf16[64,256]{1,0:T(8,128)(2,1)S(1)} %fusion.40), channel_id=1, source_target_pairs={{0,2},{1,3},{2,0},{3,1},{4,6},{5,7},{6,4},{7,5},{8,10},{9,11},{10,... | collective-permute-start | bytes 98312 | tf_op jit(solution)/shard_map/ppermute | solution.py:37
  (79 shorter events, 26.0 us)
Async XLA Ops:
  0.6 94.0 %copy-start = (bf16[256,256]{1,0:T(8,128)(2,1)S(1)}, bf16[256,256]{1,0:T(8,128)(2,1)}, u32[]{:S(2)}) copy-start(bf16[256,256]{1,0:T(8,128)(2,1)} %param.9) | copy-start | bytes 393220
  23.9 42.0 %collective-permute-start.2 = (bf16[512,256]{1,0:T(8,128)(2,1)S(1)}, bf16[512,256]{1,0:T(8,128)(2,1)S(1)}, u32[]{:S(2)}, u32[]{:S(2)}) collective-permute-start(bf16[512,256]{1,0:T(8,128)(2,1)S(1)} %get-tuple-element.10), channel_id=1, source_target_pairs={{256,0},{241,1},{226,2},{211,3},{196,4},{181,5},{166,6},{151,7},{1... | collective-permute-start | bytes 786440 | tf_op jit(solution)/shard_map/ppermute | solution.py:89
  35.3 58.6 %collective-permute-start = (bf16[512,256]{1,0:T(8,128)(2,1)S(1)}, bf16[512,256]{1,0:T(8,128)(2,1)S(1)}, u32[]{:S(2)}, u32[]{:S(2)}) collective-permute-start(bf16[512,256]{1,0:T(8,128)(2,1)S(1)} %get-tuple-element.10), channel_id=1, source_target_pairs={{0,0},{497,1},{482,2},{467,3},{452,4},{437,5},{422,6},{407,7},{392... | collective-permute-start | bytes 786440 | tf_op jit(solution)/shard_map/ppermute | solution.py:89
  37.2 55.0 %collective-permute-start.3 = (bf16[512,256]{1,0:T(8,128)(2,1)S(1)}, bf16[512,256]{1,0:T(8,128)(2,1)}, u32[]{:S(2)}, u32[]{:S(2)}) collective-permute-start(bf16[512,256]{1,0:T(8,128)(2,1)S(1)} %get-tuple-element.11), channel_id=1, source_target_pairs={{271,0},{254,1},{237,2},{220,3},{203,4},{186,5},{169,6},{152,7},{1... | collective-permute-start | bytes 786440 | tf_op jit(solution)/shard_map/ppermute | solution.py:89
  46.0 47.9 %collective-permute-start.1 = (bf16[512,256]{1,0:T(8,128)(2,1)S(1)}, bf16[512,256]{1,0:T(8,128)(2,1)S(1)}, u32[]{:S(2)}, u32[]{:S(2)}) collective-permute-start(bf16[512,256]{1,0:T(8,128)(2,1)S(1)} %get-tuple-element.11), channel_id=1, source_target_pairs={{15,0},{510,1},{493,2},{476,3},{459,4},{442,5},{425,6},{408,7},{39... | collective-permute-start | bytes 786440 | tf_op jit(solution)/shard_map/ppermute | solution.py:89
  50.7 4.1 %copy-start.8 = (s32[1,1,2,64]{3,2,1,0:T(2,128)S(1)}, s32[1,1,2,64]{3,2,1,0:T(2,128)}, u32[]{:S(2)}) copy-start(s32[1,1,2,64]{3,2,1,0:T(2,128)} %param.14) | copy-start | bytes 1540
  50.7 4.1 %copy-start.9 = (s32[1,1,2,64]{3,2,1,0:T(2,128)S(1)}, s32[1,1,2,64]{3,2,1,0:T(2,128)}, u32[]{:S(2)}) copy-start(s32[1,1,2,64]{3,2,1,0:T(2,128)} %param.13) | copy-start | bytes 1540
  58.1 35.9 %copy-start.1 = (bf16[64,16384]{1,0:T(8,128)(2,1)}, bf16[64,16384]{1,0:T(8,128)(2,1)S(1)}, u32[]{:S(2)}) copy-start(bf16[64,16384]{1,0:T(8,128)(2,1)S(1)} %convolution_convert_fusion.1) | copy-start | bytes 6291460
  59.8 34.1 %copy-start.3 = (bf16[64,16384]{1,0:T(8,128)(2,1)}, bf16[64,16384]{1,0:T(8,128)(2,1)S(1)}, u32[]{:S(2)}) copy-start(bf16[64,16384]{1,0:T(8,128)(2,1)S(1)} %convolution_convert_fusion) | copy-start | bytes 6291460
  95.3 43.6 %copy-start.7 = (f32[256]{0:T(256)S(1)}, f32[256]{0:T(256)}, u32[]{:S(2)}) copy-start(f32[256]{0:T(256)} %param.10) | copy-start | bytes 3076
  95.3 3.4 collective-permute-start.4
  98.8 0.8 copy-start.5
  99.7 63.4 %copy-start.4 = (bf16[64,16384]{1,0:T(8,128)(2,1)S(1)}, bf16[64,16384]{1,0:T(8,128)(2,1)}, u32[]{:S(2)}) copy-start(bf16[64,16384]{1,0:T(8,128)(2,1)} %copy-done.3) | copy-start | bytes 6291460
  99.7 7.7 %collective-permute-start.5 = (bf16[2,2,64,256]{3,2,1,0:T(8,128)(2,1)S(1)}, bf16[2,2,64,256]{3,2,1,0:T(8,128)(2,1)}, u32[]{:S(2)}, u32[]{:S(2)}) collective-permute-start(bf16[2,2,64,256]{3,2,1,0:T(8,128)(2,1)S(1)} %fusion.33), channel_id=1, source_target_pairs={{0,4},{1,5},{2,6},{3,7},{4,0},{5,1},{6,2},{7,3},{8,12},{9,13},{10,... | collective-permute-start | bytes 393224 | tf_op jit(solution)/shard_map/ppermute | solution.py:37
  109.0 18.1 %collective-permute-start.6 = (bf16[2,64,256]{2,1,0:T(8,128)(2,1)}, bf16[2,64,256]{2,1,0:T(8,128)(2,1)}, u32[]{:S(2)}, u32[]{:S(2)}) collective-permute-start(bf16[2,64,256]{2,1,0:T(8,128)(2,1)} %fusion.35), channel_id=1, source_target_pairs={{0,8},{1,9},{2,10},{3,11},{4,12},{5,13},{6,14},{7,15},{8,0},{9,1},... | collective-permute-start | bytes 196616 | tf_op jit(solution)/shard_map/ppermute | solution.py:37
  128.0 0.7 copy-start.6
  128.7 10.3 %collective-permute-start.7 = (bf16[64,256]{1,0:T(8,128)(2,1)S(1)}, bf16[64,256]{1,0:T(8,128)(2,1)S(1)}, u32[]{:S(2)}, u32[]{:S(2)}) collective-permute-start(bf16[64,256]{1,0:T(8,128)(2,1)S(1)} %fusion.39), channel_id=1, source_target_pairs={{0,2},{1,3},{2,0},{3,1},{4,6},{5,7},{6,4},{7,5},{8,10},{9,11},{10,... | collective-permute-start | bytes 98312 | tf_op jit(solution)/shard_map/ppermute | solution.py:37
  163.1 1.6 copy-start.2
  166.6 3.2 collective-permute-start.16
  169.8 22.0 %collective-permute-start.17 = (f32[2,2,16,256]{3,2,1,0:T(8,128)S(1)}, f32[2,2,16,256]{3,2,1,0:T(8,128)S(1)}, u32[]{:S(2)}, u32[]{:S(2)}) collective-permute-start(f32[2,2,16,256]{3,2,1,0:T(8,128)S(1)} %dynamic-slice_bitcast_fusion.1), channel_id=1, source_target_pairs={{0,4},{1,5},{2,6},{3,7},{4,0},{5,1},{6,2},{7,3},{8,12},{9,13},{10,... | collective-permute-start | bytes 196616 | tf_op jit(solution)/shard_map/ppermute | solution.py:37
  172.3 30.4 %collective-permute-start.9 = (bf16[512,256]{1,0:T(8,128)(2,1)S(1)}, bf16[512,256]{1,0:T(8,128)(2,1)S(1)}, u32[]{:S(2)}, u32[]{:S(2)}) collective-permute-start(bf16[512,256]{1,0:T(8,128)(2,1)S(1)} %get-tuple-element.8), channel_id=1, source_target_pairs={{0,256},{1,241},{2,226},{3,211},{4,196},{5,181},{6,166},{7,151},{8... | collective-permute-start | bytes 786440 | tf_op jit(solution)/shard_map/ppermute | solution.py:139
  174.2 86.0 %collective-permute-start.11 = (bf16[512,256]{1,0:T(8,128)(2,1)S(1)}, bf16[512,256]{1,0:T(8,128)(2,1)S(1)}, u32[]{:S(2)}, u32[]{:S(2)}) collective-permute-start(bf16[512,256]{1,0:T(8,128)(2,1)S(1)} %get-tuple-element.9), channel_id=1, source_target_pairs={{0,271},{1,254},{2,237},{3,220},{4,203},{5,186},{6,169},{7,152},{8... | collective-permute-start | bytes 786440 | tf_op jit(solution)/shard_map/ppermute | solution.py:139
  185.7 46.3 %collective-permute-start.8 = (bf16[512,256]{1,0:T(8,128)(2,1)S(1)}, bf16[512,256]{1,0:T(8,128)(2,1)S(1)}, u32[]{:S(2)}, u32[]{:S(2)}) collective-permute-start(bf16[512,256]{1,0:T(8,128)(2,1)S(1)} %get-tuple-element.6), channel_id=1, source_target_pairs={{0,0},{1,497},{2,482},{3,467},{4,452},{5,437},{6,422},{7,407},{8,3... | collective-permute-start | bytes 786440 | tf_op jit(solution)/shard_map/ppermute | solution.py:139
  188.4 71.8 %collective-permute-start.10 = (bf16[512,256]{1,0:T(8,128)(2,1)S(1)}, bf16[512,256]{1,0:T(8,128)(2,1)S(1)}, u32[]{:S(2)}, u32[]{:S(2)}) collective-permute-start(bf16[512,256]{1,0:T(8,128)(2,1)S(1)} %get-tuple-element.7), channel_id=1, source_target_pairs={{0,15},{1,510},{2,493},{3,476},{4,459},{5,442},{6,425},{7,408},{8,... | collective-permute-start | bytes 786440 | tf_op jit(solution)/shard_map/ppermute | solution.py:139
  191.9 70.4 %collective-permute-start.18 = (f32[2,16,256]{2,1,0:T(8,128)S(1)}, f32[2,16,256]{2,1,0:T(8,128)S(1)}, u32[]{:S(2)}, u32[]{:S(2)}) collective-permute-start(f32[2,16,256]{2,1,0:T(8,128)S(1)} %dynamic-slice_bitcast_fusion.2), channel_id=1, source_target_pairs={{0,8},{1,9},{2,10},{3,11},{4,12},{5,13},{6,14},{7,15},{8,0},{9,1},... | collective-permute-start | bytes 98312 | tf_op jit(solution)/shard_map/ppermute | solution.py:37
  260.4 3.9 %collective-permute-start.12 = (bf16[2,2,2,64,256]{4,3,2,1,0:T(8,128)(2,1)S(1)}, bf16[2,2,2,64,256]{4,3,2,1,0:T(8,128)(2,1)S(1)}, u32[]{:S(2)}, u32[]{:S(2)}) collective-permute-start(bf16[2,2,2,64,256]{4,3,2,1,0:T(8,128)(2,1)S(1)} %fusion.31), channel_id=1, source_target_pairs={{0,1},{1,0},{2,3},{3,2},{4,5},{5,4},{6,7},{7,6},{8,9},{9,8},{10,11... | collective-permute-start | bytes 786440 | tf_op jit(solution)/shard_map/ppermute | solution.py:37
  262.4 7.1 %collective-permute-start.19 = (f32[16,256]{1,0:T(8,128)S(1)}, f32[16,256]{1,0:T(8,128)S(1)}, u32[]{:S(2)}, u32[]{:S(2)}) collective-permute-start(f32[16,256]{1,0:T(8,128)S(1)} %dynamic-slice_bitcast_fusion.3), channel_id=1, source_target_pairs={{0,2},{1,3},{2,0},{3,1},{4,6},{5,7},{6,4},{7,5},{8,10},{9,11},{10,... | collective-permute-start | bytes 49160 | tf_op jit(solution)/shard_map/ppermute | solution.py:37
  264.4 7.8 %collective-permute-start.13 = (bf16[2,2,64,256]{3,2,1,0:T(8,128)(2,1)S(1)}, bf16[2,2,64,256]{3,2,1,0:T(8,128)(2,1)S(1)}, u32[]{:S(2)}, u32[]{:S(2)}) collective-permute-start(bf16[2,2,64,256]{3,2,1,0:T(8,128)(2,1)S(1)} %fusion.34), channel_id=1, source_target_pairs={{0,4},{1,5},{2,6},{3,7},{4,0},{5,1},{6,2},{7,3},{8,12},{9,13},{10,... | collective-permute-start | bytes 393224 | tf_op jit(solution)/shard_map/ppermute | solution.py:37
  272.3 83.4 %collective-permute-start.14 = (bf16[2,64,256]{2,1,0:T(8,128)(2,1)S(1)}, bf16[2,64,256]{2,1,0:T(8,128)(2,1)S(1)}, u32[]{:S(2)}, u32[]{:S(2)}) collective-permute-start(bf16[2,64,256]{2,1,0:T(8,128)(2,1)S(1)} %fusion.36), channel_id=1, source_target_pairs={{0,8},{1,9},{2,10},{3,11},{4,12},{5,13},{6,14},{7,15},{8,0},{9,1},... | collective-permute-start | bytes 196616 | tf_op jit(solution)/shard_map/ppermute | solution.py:37
  355.7 7.8 %collective-permute-start.15 = (bf16[64,256]{1,0:T(8,128)(2,1)S(1)}, bf16[64,256]{1,0:T(8,128)(2,1)S(1)}, u32[]{:S(2)}, u32[]{:S(2)}) collective-permute-start(bf16[64,256]{1,0:T(8,128)(2,1)S(1)} %fusion.40), channel_id=1, source_target_pairs={{0,2},{1,3},{2,0},{3,1},{4,6},{5,7},{6,4},{7,5},{8,10},{9,11},{10,... | collective-permute-start | bytes 98312 | tf_op jit(solution)/shard_map/ppermute | solution.py:37

commit v9 on v4

--- a/solution.py
+++ b/solution.py
@@ -38,6 +38,22 @@
         current = keep + got.astype(jnp.float32)
         remaining.remove(bit)
     return current
+
+
+def rep_all_gather(x, order):
+    replicas = lax.axis_size("rep")
+    rep_index = lax.axis_index("rep")
+    current = x
+    held = []
+    for bit in order:
+        partner = [(i, i ^ (1 << bit)) for i in range(replicas)]
+        got = lax.ppermute(current, "rep", partner)
+        upper = ((rep_index >> bit) & 1) == 1
+        low = jnp.where(upper, got, current)
+        high = jnp.where(upper, current, got)
+        held = sorted(held + [bit], reverse=True)
+        current = jnp.stack([low, high], axis=held.index(bit))
+    return current.reshape((-1,) + x.shape[1:])
 
 
 def blk_all_reduce(x):
@@ -113,7 +129,7 @@
     )
     aggregate_rows = rep_reduce_scatter(aggregate, jnp.bfloat16)
     out, grad_rows = activation(aggregate_rows + bias, grad_out)
-    grad_block = lax.all_gather(grad_rows, "rep", axis=0, tiled=True)
+    grad_block = rep_all_gather(grad_rows, [1, 3, 2, 0])
     weight_terms = lax.dot_general(
         aggregated_feats,
         grad_block.astype(jnp.float32),

time: 328 us -> 340 us (1.037)
  waiting for transfers between devices: 113 us -> 138 us
  blocking collectives: 45.8 us -> 23.2 us
  other arithmetic: 5.3 us -> 9.15 us
    all_gather x1 -> x0, blocking collectives: 22.6 us -> none  [body(): grad_block = lax.all_gather(grad_rows, 'rep', axis=0, tiled=True)]
    ppermute x0 -> x4, waiting for transfers between devices: none -> 13.5 us  [rep_all_gather(): got = lax.ppermute(current, 'rep', partner)]
    ppermute x5, starting transfers between devices: 30 us -> 16.8 us  [blk_all_reduce(): x = x + lax.ppermute(x, 'blk', [(i, i ^ step) for i in range(blocks)])]
    ppermute x0 -> x4, starting transfers between devices: none -> 12.2 us  [rep_all_gather(): got = lax.ppermute(current, 'rep', partner)]
    ppermute x5, waiting for transfers between devices: 6.97 us -> 16.9 us  [blk_all_reduce(): x = x + lax.ppermute(x, 'blk', [(i, i ^ step) for i in range(blocks)])]
  transfers between devices with their start and end apart: 25 -> 29, of which waited for: 14 -> 19; matrix products, arithmetic and copies ran while one was open for 5% -> 5% of each run, Pallas kernels for 0% -> 0%
where the time goes in v9:
time: 340 us; the launch traced here: 339 us
  starting transfers between devices  142 us (42%)
  waiting for transfers between devices  138 us (41%)
  blocking collectives  23.2 us (7%)
  local copies, waits for them, and re-layouts  12.7 us (4%)
  matrix products  12.6 us (4%)
  other arithmetic  9.15 us (3%)
    ppermute x12, starting transfers between devices, rep_reduce_scatter(): got = lax.ppermute(send.astype(wire_dtype), 'rep', partner)  69 us
    ppermute x4, waiting for transfers between devices, body(): lax.ppermute(partial[half * half_rows:(half + 1) * half_rows], both_axes,...  59.5 us
    ppermute x4, waiting for transfers between devices, body(): lax.ppermute(partition[half * half_rows:(half + 1) * half_rows], both_axe...  31.6 us
    ppermute x4, starting transfers between devices, body(): lax.ppermute(partition[half * half_rows:(half + 1) * half_rows], both_axe...  24.2 us
    all_gather x1, blocking collectives, body(): partition = lax.all_gather(feats, 'rep', axis=0, tiled=True)  23.2 us
    ppermute x4, starting transfers between devices, body(): lax.ppermute(partial[half * half_rows:(half + 1) * half_rows], both_axes,...  19.8 us
    ppermute x5, waiting for transfers between devices, blk_all_reduce(): x = x + lax.ppermute(x, 'blk', [(i, i ^ step) for i in range(blocks)])  16.9 us
    ppermute x5, starting transfers between devices, blk_all_reduce(): x = x + lax.ppermute(x, 'blk', [(i, i ^ step) for i in range(blocks)])  16.8 us
  transfers between devices with their start and end apart: 29, of which 19 were waited for; matrix products, arithmetic and copies ran while one was open for 5% of the time, Pallas kernels for 0%

profile of v9, /device:TPU:6, one launch (start us, length us, event | category | flops | bytes accessed | tf_op | source)
XLA Modules:
  0.0 338.5 jit_solution(15023635205036248526)
XLA Ops:
  0.6 23.2 %all_gather.3 = bf16[1024,256]{1,0:T(8,128)(2,1)S(1)} all-gather(bf16[64,256]{1,0:T(8,128)(2,1)} %param.8), channel_id=1, replica_groups=mesh['blk'=32,'rep'=16] {'rep'}, dimensions={0}, use_global_device_ids=true | all-gather | bytes 557056 | tf_op jit(solution)/shard_map/all_gather | solution.py:97
  23.9 11.4 %collective-permute-start.2 = (bf16[512,256]{1,0:T(8,128)(2,1)S(1)}, bf16[512,256]{1,0:T(8,128)(2,1)}, u32[]{:S(2)}, u32[]{:S(2)}) collective-permute-start(bf16[512,256]{1,0:T(8,128)(2,1)S(1)} %get-tuple-element.12), channel_id=1, source_target_pairs={{256,0},{241,1},{226,2},{211,3},{196,4},{181,5},{166,6},{151,7},{1... | collective-permute-start | bytes 786440 | tf_op jit(solution)/shard_map/ppermute | solution.py:105
  37.2 8.8 %collective-permute-start.3 = (bf16[512,256]{1,0:T(8,128)(2,1)S(1)}, bf16[512,256]{1,0:T(8,128)(2,1)}, u32[]{:S(2)}, u32[]{:S(2)}) collective-permute-start(bf16[512,256]{1,0:T(8,128)(2,1)S(1)} %get-tuple-element.13), channel_id=1, source_target_pairs={{271,0},{254,1},{237,2},{220,3},{203,4},{186,5},{169,6},{152,7},{1... | collective-permute-start | bytes 786440 | tf_op jit(solution)/shard_map/ppermute | solution.py:105
  50.7 4.8 %fusion.54 = (bf16[1,1,1,64,128,128]{5,4,3,2,1,0:T(8,128)(2,1)}, bf16[1,1,1,64,128,128]{5,4,3,2,1,0:T(8,128)(2,1)}) fusion(bf16[1,1,2,64,128,128]{5,4,3,2,1,0:T(8,128)(2,1)} %param.12), kind=kLoop, calls=%fused_computation.100 | loop fusion | bytes 8388608 | tf_op jit(solution)/shard_map/slice | solution.py:115
  55.5 3.4 %convolution_convert_fusion.1 = bf16[64,16384]{1,0:T(8,128)(2,1)S(1)} fusion(bf16[8,8,128,128]{3,2,1,0:T(8,128)(2,1)} %bitcast.138, s32[64]{0:T(128)S(1)} %get-tuple-element.22, pred[64]{0:T(512)(128)(4,1)S(1)} %iota_compare_fusion.3), kind=kOutput, calls=%fused_computation.1 | convolution fusion | flops 135274496 | bytes 4194624 | tf_op jit(solution)/shard_map/dot_general | solution.py:13
  60.7 5.2 %collective-permute-done.2 = bf16[512,256]{1,0:T(8,128)(2,1)} collective-permute-done((bf16[512,256]{1,0:T(8,128)(2,1)S(1)}, bf16[512,256]{1,0:T(8,128)(2,1)}, u32[]{:S(2)}, u32[]{:S(2)}) %collective-permute-start.2) | collective-permute-done | bytes 262176 | tf_op jit(solution)/shard_map/ppermute | solution.py:105
  65.9 26.3 %collective-permute-done.3 = bf16[512,256]{1,0:T(8,128)(2,1)} collective-permute-done((bf16[512,256]{1,0:T(8,128)(2,1)S(1)}, bf16[512,256]{1,0:T(8,128)(2,1)}, u32[]{:S(2)}, u32[]{:S(2)}) %collective-permute-start.3) | collective-permute-done | bytes 262176 | tf_op jit(solution)/shard_map/ppermute | solution.py:105
  106.7 5.6 %collective-permute-done.5 = bf16[2,2,64,256]{3,2,1,0:T(8,128)(2,1)} collective-permute-done((bf16[2,2,64,256]{3,2,1,0:T(8,128)(2,1)S(1)}, bf16[2,2,64,256]{3,2,1,0:T(8,128)(2,1)}, u32[]{:S(2)}, u32[]{:S(2)}) %collective-permute-start.5) | collective-permute-done | bytes 131104 | tf_op jit(solution)/shard_map/ppermute | solution.py:37
  114.0 15.6 %collective-permute-start.6 = (bf16[2,64,256]{2,1,0:T(8,128)(2,1)}, bf16[2,64,256]{2,1,0:T(8,128)(2,1)}, u32[]{:S(2)}, u32[]{:S(2)}) collective-permute-start(bf16[2,64,256]{2,1,0:T(8,128)(2,1)} %fusion.35), channel_id=1, source_target_pairs={{0,8},{1,9},{2,10},{3,11},{4,12},{5,13},{6,14},{7,15},{8,0},{9,1},... | collective-permute-start | bytes 196616 | tf_op jit(solution)/shard_map/ppermute | solution.py:37
  129.5 2.5 collective-permute-done.6
  133.6 8.3 %collective-permute-start.7 = (bf16[64,256]{1,0:T(8,128)(2,1)S(1)}, bf16[64,256]{1,0:T(8,128)(2,1)S(1)}, u32[]{:S(2)}, u32[]{:S(2)}) collective-permute-start(bf16[64,256]{1,0:T(8,128)(2,1)S(1)} %fusion.39), channel_id=1, source_target_pairs={{0,2},{1,3},{2,0},{3,1},{4,6},{5,7},{6,4},{7,5},{8,10},{9,11},{10,... | collective-permute-start | bytes 98312 | tf_op jit(solution)/shard_map/ppermute | solution.py:37
  145.3 5.4 %collective-permute-start.8 = (bf16[64,256]{1,0:T(8,128)(2,1)S(1)}, bf16[64,256]{1,0:T(8,128)(2,1)S(1)}, u32[]{:S(2)}, u32[]{:S(2)}) collective-permute-start(bf16[64,256]{1,0:T(8,128)(2,1)S(1)} %get-tuple-element.16), channel_id=1, source_target_pairs={{0,2},{1,3},{2,0},{3,1},{4,6},{5,7},{6,4},{7,5},{8,10},{9,11},{10,... | collective-permute-start | bytes 98312 | tf_op jit(solution)/shard_map/ppermute | solution.py:50
  152.6 2.6 collective-permute-start.9
  155.2 5.1 %collective-permute-done.9 = bf16[2,64,256]{2,1,0:T(8,128)(2,1)S(1)} collective-permute-done((bf16[2,64,256]{2,1,0:T(8,128)(2,1)S(1)}, bf16[2,64,256]{2,1,0:T(8,128)(2,1)S(1)}, u32[]{:S(2)}, u32[]{:S(2)}) %collective-permute-start.9) | collective-permute-done | bytes 65568 | tf_op jit(solution)/shard_map/ppermute | solution.py:50
  160.9 2.3 collective-permute-start.10
  163.2 4.7 %collective-permute-done.10 = bf16[2,2,64,256]{3,2,1,0:T(8,128)(2,1)} collective-permute-done((bf16[2,2,64,256]{3,2,1,0:T(8,128)(2,1)S(1)}, bf16[2,2,64,256]{3,2,1,0:T(8,128)(2,1)}, u32[]{:S(2)}, u32[]{:S(2)}) %collective-permute-start.10) | collective-permute-done | bytes 131104 | tf_op jit(solution)/shard_map/ppermute | solution.py:50
  176.7 2.0 collective-permute-start.20
  180.0 2.3 collective-permute-start.21
  184.3 10.4 %collective-permute-start.15 = (bf16[512,256]{1,0:T(8,128)(2,1)S(1)}, bf16[512,256]{1,0:T(8,128)(2,1)S(1)}, u32[]{:S(2)}, u32[]{:S(2)}) collective-permute-start(bf16[512,256]{1,0:T(8,128)(2,1)S(1)} %get-tuple-element.9), channel_id=1, source_target_pairs={{0,271},{1,254},{2,237},{3,220},{4,203},{5,186},{6,169},{7,152},{8... | collective-permute-start | bytes 786440 | tf_op jit(solution)/shard_map/ppermute | solution.py:152
  194.7 5.6 %collective-permute-start.12 = (bf16[512,256]{1,0:T(8,128)(2,1)S(1)}, bf16[512,256]{1,0:T(8,128)(2,1)S(1)}, u32[]{:S(2)}, u32[]{:S(2)}) collective-permute-start(bf16[512,256]{1,0:T(8,128)(2,1)S(1)} %get-tuple-element.6), channel_id=1, source_target_pairs={{0,0},{1,497},{2,482},{3,467},{4,452},{5,437},{6,422},{7,407},{8,3... | collective-permute-start | bytes 786440 | tf_op jit(solution)/shard_map/ppermute | solution.py:152
  202.4 8.6 %collective-permute-start.22 = (f32[2,16,256]{2,1,0:T(8,128)S(1)}, f32[2,16,256]{2,1,0:T(8,128)S(1)}, u32[]{:S(2)}, u32[]{:S(2)}) collective-permute-start(f32[2,16,256]{2,1,0:T(8,128)S(1)} %dynamic-slice_bitcast_fusion.2), channel_id=1, source_target_pairs={{0,8},{1,9},{2,10},{3,11},{4,12},{5,13},{6,14},{7,15},{8,0},{9,1},... | collective-permute-start | bytes 98312 | tf_op jit(solution)/shard_map/ppermute | solution.py:37
  211.1 24.8 %collective-permute-done.12 = bf16[512,256]{1,0:T(8,128)(2,1)S(1)} collective-permute-done((bf16[512,256]{1,0:T(8,128)(2,1)S(1)}, bf16[512,256]{1,0:T(8,128)(2,1)S(1)}, u32[]{:S(2)}, u32[]{:S(2)}) %collective-permute-start.12) | collective-permute-done | bytes 262176 | tf_op jit(solution)/shard_map/ppermute | solution.py:152
  235.9 34.7 %collective-permute-done.15 = bf16[512,256]{1,0:T(8,128)(2,1)S(1)} collective-permute-done((bf16[512,256]{1,0:T(8,128)(2,1)S(1)}, bf16[512,256]{1,0:T(8,128)(2,1)S(1)}, u32[]{:S(2)}, u32[]{:S(2)}) %collective-permute-start.15) | collective-permute-done | bytes 262176 | tf_op jit(solution)/shard_map/ppermute | solution.py:152
  276.8 3.2 collective-permute-done.23
  279.9 2.6 collective-permute-start.24
  282.7 17.4 %collective-permute-start.18 = (bf16[2,64,256]{2,1,0:T(8,128)(2,1)S(1)}, bf16[2,64,256]{2,1,0:T(8,128)(2,1)S(1)}, u32[]{:S(2)}, u32[]{:S(2)}) collective-permute-start(bf16[2,64,256]{2,1,0:T(8,128)(2,1)S(1)} %fusion.36), channel_id=1, source_target_pairs={{0,8},{1,9},{2,10},{3,11},{4,12},{5,13},{6,14},{7,15},{8,0},{9,1},... | collective-permute-start | bytes 196616 | tf_op jit(solution)/shard_map/ppermute | solution.py:37
  302.1 3.8 %collective-permute-done.25 = f32[17,256]{1,0:T(8,128)S(1)} collective-permute-done((f32[17,256]{1,0:T(8,128)S(1)}, f32[17,256]{1,0:T(8,128)S(1)}, u32[]{:S(2)}, u32[]{:S(2)}) %collective-permute-start.25) | collective-permute-done | bytes 17440 | tf_op jit(solution)/shard_map/ppermute | solution.py:63
  307.8 4.7 %collective-permute-done.26 = f32[17,256]{1,0:T(8,128)S(1)} collective-permute-done((f32[17,256]{1,0:T(8,128)S(1)}, f32[17,256]{1,0:T(8,128)S(1)}, u32[]{:S(2)}, u32[]{:S(2)}) %collective-permute-start.26) | collective-permute-done | bytes 17440 | tf_op jit(solution)/shard_map/ppermute | solution.py:63
  314.5 5.1 %collective-permute-start.19 = (bf16[64,256]{1,0:T(8,128)(2,1)S(1)}, bf16[64,256]{1,0:T(8,128)(2,1)S(1)}, u32[]{:S(2)}, u32[]{:S(2)}) collective-permute-start(bf16[64,256]{1,0:T(8,128)(2,1)S(1)} %fusion.40), channel_id=1, source_target_pairs={{0,2},{1,3},{2,0},{3,1},{4,6},{5,7},{6,4},{7,5},{8,10},{9,11},{10,... | collective-permute-start | bytes 98312 | tf_op jit(solution)/shard_map/ppermute | solution.py:37
  319.6 2.5 collective-permute-done.27
  322.1 8.4 %collective-permute-start.28 = (f32[17,256]{1,0:T(8,128)S(1)}, f32[17,256]{1,0:T(8,128)S(1)}, u32[]{:S(2)}, u32[]{:S(2)}) collective-permute-start(f32[17,256]{1,0:T(8,128)S(1)} %add.185), channel_id=1, source_target_pairs={{0,256},{16,272},{32,288},{48,304},{64,320},{80,336},{96,352},{112... | collective-permute-start | bytes 52232 | tf_op jit(solution)/shard_map/ppermute | solution.py:63
  330.6 6.0 %collective-permute-done.28 = f32[17,256]{1,0:T(8,128)S(1)} collective-permute-done((f32[17,256]{1,0:T(8,128)S(1)}, f32[17,256]{1,0:T(8,128)S(1)}, u32[]{:S(2)}, u32[]{:S(2)}) %collective-permute-start.28) | collective-permute-done | bytes 17440 | tf_op jit(solution)/shard_map/ppermute | solution.py:63
  (114 shorter events, 59.9 us)
Async XLA Ops:
  0.6 95.8 %copy-start = (bf16[256,256]{1,0:T(8,128)(2,1)S(1)}, bf16[256,256]{1,0:T(8,128)(2,1)}, u32[]{:S(2)}) copy-start(bf16[256,256]{1,0:T(8,128)(2,1)} %param.9) | copy-start | bytes 393220
  23.9 42.0 %collective-permute-start.2 = (bf16[512,256]{1,0:T(8,128)(2,1)S(1)}, bf16[512,256]{1,0:T(8,128)(2,1)}, u32[]{:S(2)}, u32[]{:S(2)}) collective-permute-start(bf16[512,256]{1,0:T(8,128)(2,1)S(1)} %get-tuple-element.12), channel_id=1, source_target_pairs={{256,0},{241,1},{226,2},{211,3},{196,4},{181,5},{166,6},{151,7},{1... | collective-permute-start | bytes 786440 | tf_op jit(solution)/shard_map/ppermute | solution.py:105
  35.3 58.8 %collective-permute-start = (bf16[512,256]{1,0:T(8,128)(2,1)S(1)}, bf16[512,256]{1,0:T(8,128)(2,1)S(1)}, u32[]{:S(2)}, u32[]{:S(2)}) collective-permute-start(bf16[512,256]{1,0:T(8,128)(2,1)S(1)} %get-tuple-element.12), channel_id=1, source_target_pairs={{0,0},{497,1},{482,2},{467,3},{452,4},{437,5},{422,6},{407,7},{392... | collective-permute-start | bytes 786440 | tf_op jit(solution)/shard_map/ppermute | solution.py:105
  37.2 55.0 %collective-permute-start.3 = (bf16[512,256]{1,0:T(8,128)(2,1)S(1)}, bf16[512,256]{1,0:T(8,128)(2,1)}, u32[]{:S(2)}, u32[]{:S(2)}) collective-permute-start(bf16[512,256]{1,0:T(8,128)(2,1)S(1)} %get-tuple-element.13), channel_id=1, source_target_pairs={{271,0},{254,1},{237,2},{220,3},{203,4},{186,5},{169,6},{152,7},{1... | collective-permute-start | bytes 786440 | tf_op jit(solution)/shard_map/ppermute | solution.py:105
  46.0 48.0 %collective-permute-start.1 = (bf16[512,256]{1,0:T(8,128)(2,1)S(1)}, bf16[512,256]{1,0:T(8,128)(2,1)S(1)}, u32[]{:S(2)}, u32[]{:S(2)}) collective-permute-start(bf16[512,256]{1,0:T(8,128)(2,1)S(1)} %get-tuple-element.13), channel_id=1, source_target_pairs={{15,0},{510,1},{493,2},{476,3},{459,4},{442,5},{425,6},{408,7},{39... | collective-permute-start | bytes 786440 | tf_op jit(solution)/shard_map/ppermute | solution.py:105
  60.7 33.4 %copy-start.3 = (bf16[64,16384]{1,0:T(8,128)(2,1)}, bf16[64,16384]{1,0:T(8,128)(2,1)S(1)}, u32[]{:S(2)}) copy-start(bf16[64,16384]{1,0:T(8,128)(2,1)S(1)} %convolution_convert_fusion) | copy-start | bytes 6291460
  97.5 46.2 %copy-start.10 = (f32[256]{0:T(256)S(1)}, f32[256]{0:T(256)}, u32[]{:S(2)}) copy-start(f32[256]{0:T(256)} %param.10) | copy-start | bytes 3076
  99.2 3.6 %collective-permute-start.4 = (bf16[2,2,2,64,256]{4,3,2,0,1:T(8,128)(2,1)}, bf16[2,2,2,64,256]{4,3,2,0,1:T(8,128)(2,1)S(1)}, u32[]{:S(2)}, u32[]{:S(2)}) collective-permute-start(bf16[2,2,2,64,256]{4,3,2,0,1:T(8,128)(2,1)} %fusion.32), channel_id=1, source_target_pairs={{0,1},{1,0},{2,3},{3,2},{4,5},{5,4},{6,7},{7,6},{8,9},{9,8},{10,11... | collective-permute-start | bytes 786440 | tf_op jit(solution)/shard_map/ppermute | solution.py:37
  104.7 7.5 %collective-permute-start.5 = (bf16[2,2,64,256]{3,2,1,0:T(8,128)(2,1)S(1)}, bf16[2,2,64,256]{3,2,1,0:T(8,128)(2,1)}, u32[]{:S(2)}, u32[]{:S(2)}) collective-permute-start(bf16[2,2,64,256]{3,2,1,0:T(8,128)(2,1)S(1)} %fusion.33), channel_id=1, source_target_pairs={{0,4},{1,5},{2,6},{3,7},{4,0},{5,1},{6,2},{7,3},{8,12},{9,13},{10,... | collective-permute-start | bytes 393224 | tf_op jit(solution)/shard_map/ppermute | solution.py:37
  114.0 18.1 %collective-permute-start.6 = (bf16[2,64,256]{2,1,0:T(8,128)(2,1)}, bf16[2,64,256]{2,1,0:T(8,128)(2,1)}, u32[]{:S(2)}, u32[]{:S(2)}) collective-permute-start(bf16[2,64,256]{2,1,0:T(8,128)(2,1)} %fusion.35), channel_id=1, source_target_pairs={{0,8},{1,9},{2,10},{3,11},{4,12},{5,13},{6,14},{7,15},{8,0},{9,1},... | collective-permute-start | bytes 196616 | tf_op jit(solution)/shard_map/ppermute | solution.py:37
  133.6 10.2 %collective-permute-start.7 = (bf16[64,256]{1,0:T(8,128)(2,1)S(1)}, bf16[64,256]{1,0:T(8,128)(2,1)S(1)}, u32[]{:S(2)}, u32[]{:S(2)}) collective-permute-start(bf16[64,256]{1,0:T(8,128)(2,1)S(1)} %fusion.39), channel_id=1, source_target_pairs={{0,2},{1,3},{2,0},{3,1},{4,6},{5,7},{6,4},{7,5},{8,10},{9,11},{10,... | collective-permute-start | bytes 98312 | tf_op jit(solution)/shard_map/ppermute | solution.py:37
  145.3 7.3 %collective-permute-start.8 = (bf16[64,256]{1,0:T(8,128)(2,1)S(1)}, bf16[64,256]{1,0:T(8,128)(2,1)S(1)}, u32[]{:S(2)}, u32[]{:S(2)}) collective-permute-start(bf16[64,256]{1,0:T(8,128)(2,1)S(1)} %get-tuple-element.16), channel_id=1, source_target_pairs={{0,2},{1,3},{2,0},{3,1},{4,6},{5,7},{6,4},{7,5},{8,10},{9,11},{10,... | collective-permute-start | bytes 98312 | tf_op jit(solution)/shard_map/ppermute | solution.py:50
  152.6 7.7 %collective-permute-start.9 = (bf16[2,64,256]{2,1,0:T(8,128)(2,1)S(1)}, bf16[2,64,256]{2,1,0:T(8,128)(2,1)S(1)}, u32[]{:S(2)}, u32[]{:S(2)}) collective-permute-start(bf16[2,64,256]{2,1,0:T(8,128)(2,1)S(1)} %pad_maximum_fusion.4), channel_id=1, source_target_pairs={{0,8},{1,9},{2,10},{3,11},{4,12},{5,13},{6,14},{7,15},{8,0},{9,1},... | collective-permute-start | bytes 196616 | tf_op jit(solution)/shard_map/ppermute | solution.py:50
  160.9 7.0 %collective-permute-start.10 = (bf16[2,2,64,256]{3,2,1,0:T(8,128)(2,1)S(1)}, bf16[2,2,64,256]{3,2,1,0:T(8,128)(2,1)}, u32[]{:S(2)}, u32[]{:S(2)}) collective-permute-start(bf16[2,2,64,256]{3,2,1,0:T(8,128)(2,1)S(1)} %pad_maximum_fusion.3), channel_id=1, source_target_pairs={{0,4},{1,5},{2,6},{3,7},{4,0},{5,1},{6,2},{7,3},{8,12},{9,13},{10,... | collective-permute-start | bytes 393224 | tf_op jit(solution)/shard_map/ppermute | solution.py:50
  169.6 3.8 %collective-permute-start.11 = (bf16[2,2,2,64,256]{4,3,2,0,1:T(8,128)(2,1)}, bf16[2,2,2,64,256]{4,3,2,0,1:T(8,128)(2,1)}, u32[]{:S(2)}, u32[]{:S(2)}) collective-permute-start(bf16[2,2,2,64,256]{4,3,2,0,1:T(8,128)(2,1)} %pad_maximum_fusion.2), channel_id=1, source_target_pairs={{0,1},{1,0},{2,3},{3,2},{4,5},{5,4},{6,7},{7,6},{8,9},{9,8},{10,11... | collective-permute-start | bytes 786440 | tf_op jit(solution)/shard_map/ppermute | solution.py:50
  176.7 3.2 collective-permute-start.20
  180.0 22.4 %collective-permute-start.21 = (f32[2,2,16,256]{3,2,1,0:T(8,128)S(1)}, f32[2,2,16,256]{3,2,1,0:T(8,128)S(1)}, u32[]{:S(2)}, u32[]{:S(2)}) collective-permute-start(f32[2,2,16,256]{3,2,1,0:T(8,128)S(1)} %dynamic-slice_bitcast_fusion.1), channel_id=1, source_target_pairs={{0,4},{1,5},{2,6},{3,7},{4,0},{5,1},{6,2},{7,3},{8,12},{9,13},{10,... | collective-permute-start | bytes 196616 | tf_op jit(solution)/shard_map/ppermute | solution.py:37
  182.4 28.7 %collective-permute-start.13 = (bf16[512,256]{1,0:T(8,128)(2,1)S(1)}, bf16[512,256]{1,0:T(8,128)(2,1)S(1)}, u32[]{:S(2)}, u32[]{:S(2)}) collective-permute-start(bf16[512,256]{1,0:T(8,128)(2,1)S(1)} %get-tuple-element.8), channel_id=1, source_target_pairs={{0,256},{1,241},{2,226},{3,211},{4,196},{5,181},{6,166},{7,151},{8... | collective-permute-start | bytes 786440 | tf_op jit(solution)/shard_map/ppermute | solution.py:152
  184.3 86.3 %collective-permute-start.15 = (bf16[512,256]{1,0:T(8,128)(2,1)S(1)}, bf16[512,256]{1,0:T(8,128)(2,1)S(1)}, u32[]{:S(2)}, u32[]{:S(2)}) collective-permute-start(bf16[512,256]{1,0:T(8,128)(2,1)S(1)} %get-tuple-element.9), channel_id=1, source_target_pairs={{0,271},{1,254},{2,237},{3,220},{4,203},{5,186},{6,169},{7,152},{8... | collective-permute-start | bytes 786440 | tf_op jit(solution)/shard_map/ppermute | solution.py:152
  194.7 41.2 %collective-permute-start.12 = (bf16[512,256]{1,0:T(8,128)(2,1)S(1)}, bf16[512,256]{1,0:T(8,128)(2,1)S(1)}, u32[]{:S(2)}, u32[]{:S(2)}) collective-permute-start(bf16[512,256]{1,0:T(8,128)(2,1)S(1)} %get-tuple-element.6), channel_id=1, source_target_pairs={{0,0},{1,497},{2,482},{3,467},{4,452},{5,437},{6,422},{7,407},{8,3... | collective-permute-start | bytes 786440 | tf_op jit(solution)/shard_map/ppermute | solution.py:152
  200.3 70.3 %collective-permute-start.14 = (bf16[512,256]{1,0:T(8,128)(2,1)S(1)}, bf16[512,256]{1,0:T(8,128)(2,1)S(1)}, u32[]{:S(2)}, u32[]{:S(2)}) collective-permute-start(bf16[512,256]{1,0:T(8,128)(2,1)S(1)} %get-tuple-element.7), channel_id=1, source_target_pairs={{0,15},{1,510},{2,493},{3,476},{4,459},{5,442},{6,425},{7,408},{8,... | collective-permute-start | bytes 786440 | tf_op jit(solution)/shard_map/ppermute | solution.py:152
  202.4 70.3 %collective-permute-start.22 = (f32[2,16,256]{2,1,0:T(8,128)S(1)}, f32[2,16,256]{2,1,0:T(8,128)S(1)}, u32[]{:S(2)}, u32[]{:S(2)}) collective-permute-start(f32[2,16,256]{2,1,0:T(8,128)S(1)} %dynamic-slice_bitcast_fusion.2), channel_id=1, source_target_pairs={{0,8},{1,9},{2,10},{3,11},{4,12},{5,13},{6,14},{7,15},{8,0},{9,1},... | collective-permute-start | bytes 98312 | tf_op jit(solution)/shard_map/ppermute | solution.py:37
  270.8 3.9 %collective-permute-start.16 = (bf16[2,2,2,64,256]{4,3,2,1,0:T(8,128)(2,1)S(1)}, bf16[2,2,2,64,256]{4,3,2,1,0:T(8,128)(2,1)S(1)}, u32[]{:S(2)}, u32[]{:S(2)}) collective-permute-start(bf16[2,2,2,64,256]{4,3,2,1,0:T(8,128)(2,1)S(1)} %fusion.31), channel_id=1, source_target_pairs={{0,1},{1,0},{2,3},{3,2},{4,5},{5,4},{6,7},{7,6},{8,9},{9,8},{10,11... | collective-permute-start | bytes 786440 | tf_op jit(solution)/shard_map/ppermute | solution.py:37
  272.8 7.1 %collective-permute-start.23 = (f32[16,256]{1,0:T(8,128)S(1)}, f32[16,256]{1,0:T(8,128)S(1)}, u32[]{:S(2)}, u32[]{:S(2)}) collective-permute-start(f32[16,256]{1,0:T(8,128)S(1)} %dynamic-slice_bitcast_fusion.3), channel_id=1, source_target_pairs={{0,2},{1,3},{2,0},{3,1},{4,6},{5,7},{6,4},{7,5},{8,10},{9,11},{10,... | collective-permute-start | bytes 49160 | tf_op jit(solution)/shard_map/ppermute | solution.py:37
  274.8 7.8 %collective-permute-start.17 = (bf16[2,2,64,256]{3,2,1,0:T(8,128)(2,1)S(1)}, bf16[2,2,64,256]{3,2,1,0:T(8,128)(2,1)S(1)}, u32[]{:S(2)}, u32[]{:S(2)}) collective-permute-start(bf16[2,2,64,256]{3,2,1,0:T(8,128)(2,1)S(1)} %fusion.34), channel_id=1, source_target_pairs={{0,4},{1,5},{2,6},{3,7},{4,0},{5,1},{6,2},{7,3},{8,12},{9,13},{10,... | collective-permute-start | bytes 393224 | tf_op jit(solution)/shard_map/ppermute | solution.py:37
  279.9 20.2 %collective-permute-start.24 = (f32[17,256]{1,0:T(8,128)S(1)}, f32[17,256]{1,0:T(8,128)S(1)}, u32[]{:S(2)}, u32[]{:S(2)}) collective-permute-start(f32[17,256]{1,0:T(8,128)S(1)} %pad_maximum_fusion.5), channel_id=1, source_target_pairs={{0,16},{16,0},{32,48},{48,32},{64,80},{80,64},{96,112},{112,96},{1... | collective-permute-start | bytes 52232 | tf_op jit(solution)/shard_map/ppermute | solution.py:63
  282.7 31.7 %collective-permute-start.18 = (bf16[2,64,256]{2,1,0:T(8,128)(2,1)S(1)}, bf16[2,64,256]{2,1,0:T(8,128)(2,1)S(1)}, u32[]{:S(2)}, u32[]{:S(2)}) collective-permute-start(bf16[2,64,256]{2,1,0:T(8,128)(2,1)S(1)} %fusion.36), channel_id=1, source_target_pairs={{0,8},{1,9},{2,10},{3,11},{4,12},{5,13},{6,14},{7,15},{8,0},{9,1},... | collective-permute-start | bytes 196616 | tf_op jit(solution)/shard_map/ppermute | solution.py:37
  300.1 5.7 %collective-permute-start.25 = (f32[17,256]{1,0:T(8,128)S(1)}, f32[17,256]{1,0:T(8,128)S(1)}, u32[]{:S(2)}, u32[]{:S(2)}) collective-permute-start(f32[17,256]{1,0:T(8,128)S(1)} %fusion.53), channel_id=1, source_target_pairs={{0,32},{16,48},{32,0},{48,16},{64,96},{80,112},{96,64},{112,80},{1... | collective-permute-start | bytes 52232 | tf_op jit(solution)/shard_map/ppermute | solution.py:63
  305.9 6.6 %collective-permute-start.26 = (f32[17,256]{1,0:T(8,128)S(1)}, f32[17,256]{1,0:T(8,128)S(1)}, u32[]{:S(2)}, u32[]{:S(2)}) collective-permute-start(f32[17,256]{1,0:T(8,128)S(1)} %add.183), channel_id=1, source_target_pairs={{0,64},{16,80},{32,96},{48,112},{64,0},{80,16},{96,32},{112,48},{1... | collective-permute-start | bytes 52232 | tf_op jit(solution)/shard_map/ppermute | solution.py:63
  312.5 9.6 %collective-permute-start.27 = (f32[17,256]{1,0:T(8,128)S(1)}, f32[17,256]{1,0:T(8,128)S(1)}, u32[]{:S(2)}, u32[]{:S(2)}) collective-permute-start(f32[17,256]{1,0:T(8,128)S(1)} %add.184), channel_id=1, source_target_pairs={{0,128},{16,144},{32,160},{48,176},{64,192},{80,208},{96,224},{112... | collective-permute-start | bytes 52232 | tf_op jit(solution)/shard_map/ppermute | solution.py:63
  314.5 23.3 %collective-permute-start.19 = (bf16[64,256]{1,0:T(8,128)(2,1)S(1)}, bf16[64,256]{1,0:T(8,128)(2,1)S(1)}, u32[]{:S(2)}, u32[]{:S(2)}) collective-permute-start(bf16[64,256]{1,0:T(8,128)(2,1)S(1)} %fusion.40), channel_id=1, source_target_pairs={{0,2},{1,3},{2,0},{3,1},{4,6},{5,7},{6,4},{7,5},{8,10},{9,11},{10,... | collective-permute-start | bytes 98312 | tf_op jit(solution)/shard_map/ppermute | solution.py:37
  322.1 14.4 %collective-permute-start.28 = (f32[17,256]{1,0:T(8,128)S(1)}, f32[17,256]{1,0:T(8,128)S(1)}, u32[]{:S(2)}, u32[]{:S(2)}) collective-permute-start(f32[17,256]{1,0:T(8,128)S(1)} %add.185), channel_id=1, source_target_pairs={{0,256},{16,272},{32,288},{48,304},{64,320},{80,336},{96,352},{112... | collective-permute-start | bytes 52232 | tf_op jit(solution)/shard_map/ppermute | solution.py:63
  (10 other events, 20.4 us)

commit v10 on v4

--- a/solution.py
+++ b/solution.py
@@ -105,21 +105,19 @@
         aggregated_feats = aggregated_feats + jnp.dot(
             adjacency[slot], sources[slot], preferred_element_type=jnp.float32
         )
-    aggregate = jnp.dot(
-        aggregated_feats,
-        weight.astype(jnp.float32),
-        precision=lax.Precision.HIGHEST,
-        preferred_element_type=jnp.float32,
+    feats_high = aggregated_feats.astype(jnp.bfloat16)
+    feats_low = (aggregated_feats - feats_high.astype(jnp.float32)).astype(jnp.bfloat16)
+    aggregate = jnp.dot(feats_high, weight, preferred_element_type=jnp.float32) + jnp.dot(
+        feats_low, weight, preferred_element_type=jnp.float32
     )
     aggregate_rows = rep_reduce_scatter(aggregate, jnp.bfloat16)
     out, grad_rows = activation(aggregate_rows + bias, grad_out)
     grad_block = lax.all_gather(grad_rows, "rep", axis=0, tiled=True)
-    weight_terms = lax.dot_general(
-        aggregated_feats,
-        grad_block.astype(jnp.float32),
-        (((0,), (0,)), ((), ())),
-        precision=lax.Precision.HIGHEST,
-        preferred_element_type=jnp.float32,
+    weight_terms = sum(
+        lax.dot_general(
+            part, grad_block, (((0,), (0,)), ((), ())), preferred_element_type=jnp.float32
+        )
+        for part in (feats_high, feats_low)
     )
     weight_part = rep_reduce_scatter(weight_terms, jnp.float32)
     bias_part = jnp.sum(grad_block.astype(jnp.float32), axis=0)

time: 328 us -> 328 us (level)
  transfers between devices with their start and end apart: 25 -> 25, of which waited for: 14 -> 15; matrix products, arithmetic and copies ran while one was open for 5% -> 5% of each run, Pallas kernels for 0% -> 0%
where the time goes in v10:
time: 328 us; the launch traced here: 326 us
  starting transfers between devices  140 us (43%)
  waiting for transfers between devices  113 us (34%)
  blocking collectives  45.8 us (14%)
  matrix products  11 us (3%)
  local copies, waits for them, and re-layouts  9.74 us (3%)
  other arithmetic  5.3 us (2%)
    ppermute x12, starting transfers between devices, rep_reduce_scatter(): got = lax.ppermute(send.astype(wire_dtype), 'rep', partner)  66.2 us
    ppermute x4, waiting for transfers between devices, body(): lax.ppermute(partial[half * half_rows:(half + 1) * half_rows], both_axes,...  57.5 us
    ppermute x4, waiting for transfers between devices, body(): lax.ppermute(partition[half * half_rows:(half + 1) * half_rows], both_axe...  32.4 us
    ppermute x5, starting transfers between devices, blk_all_reduce(): x = x + lax.ppermute(x, 'blk', [(i, i ^ step) for i in range(blocks)])  30 us
    ppermute x4, starting transfers between devices, body(): lax.ppermute(partition[half * half_rows:(half + 1) * half_rows], both_axe...  24.2 us
    all_gather x1, blocking collectives, body(): partition = lax.all_gather(feats, 'rep', axis=0, tiled=True)  23.2 us
    all_gather x1, blocking collectives, body(): grad_block = lax.all_gather(grad_rows, 'rep', axis=0, tiled=True)  22.6 us
    ppermute x4, starting transfers between devices, body(): lax.ppermute(partial[half * half_rows:(half + 1) * half_rows], both_axes,...  19.5 us
  transfers between devices with their start and end apart: 25, of which 15 were waited for; matrix products, arithmetic and copies ran while one was open for 5% of the time, Pallas kernels for 0%

profile of v10, /device:TPU:6, one launch (start us, length us, event | category | flops | bytes accessed | tf_op | source)
XLA Modules:
  0.0 325.9 jit_solution(9450565975991193898)
XLA Ops:
  0.6 23.2 %all_gather.6 = bf16[1024,256]{1,0:T(8,128)(2,1)S(1)} all-gather(bf16[64,256]{1,0:T(8,128)(2,1)} %param.8), channel_id=1, replica_groups=mesh['blk'=32,'rep'=16] {'rep'}, dimensions={0}, use_global_device_ids=true | all-gather | bytes 557056 | tf_op jit(solution)/shard_map/all_gather | solution.py:81
  23.9 11.4 %collective-permute-start.2 = (bf16[512,256]{1,0:T(8,128)(2,1)S(1)}, bf16[512,256]{1,0:T(8,128)(2,1)S(1)}, u32[]{:S(2)}, u32[]{:S(2)}) collective-permute-start(bf16[512,256]{1,0:T(8,128)(2,1)S(1)} %get-tuple-element.10), channel_id=1, source_target_pairs={{256,0},{241,1},{226,2},{211,3},{196,4},{181,5},{166,6},{151,7},{1... | collective-permute-start | bytes 786440 | tf_op jit(solution)/shard_map/ppermute | solution.py:89
  37.2 8.8 %collective-permute-start.3 = (bf16[512,256]{1,0:T(8,128)(2,1)S(1)}, bf16[512,256]{1,0:T(8,128)(2,1)}, u32[]{:S(2)}, u32[]{:S(2)}) collective-permute-start(bf16[512,256]{1,0:T(8,128)(2,1)S(1)} %get-tuple-element.11), channel_id=1, source_target_pairs={{271,0},{254,1},{237,2},{220,3},{203,4},{186,5},{169,6},{152,7},{1... | collective-permute-start | bytes 786440 | tf_op jit(solution)/shard_map/ppermute | solution.py:89
  46.0 2.0 collective-permute-start.1
  50.7 4.0 %fusion.58 = (bf16[1,1,1,64,128,128]{5,4,3,2,1,0:T(8,128)(2,1)}, bf16[1,1,1,64,128,128]{5,4,3,2,1,0:T(8,128)(2,1)S(1)}) fusion(bf16[1,1,2,64,128,128]{5,4,3,2,1,0:T(8,128)(2,1)} %param.12), kind=kLoop, calls=%fused_computation.95 | loop fusion | bytes 8388608 | tf_op jit(solution)/shard_map/slice | solution.py:99
  54.8 3.3 %convolution_convert_fusion.1 = bf16[64,16384]{1,0:T(8,128)(2,1)S(1)} fusion(bf16[8,8,128,128]{3,2,1,0:T(8,128)(2,1)} %bitcast.112, s32[64]{0:T(128)S(1)} %get-tuple-element.14, pred[64]{0:T(512)(128)(4,1)S(1)} %iota_compare_fusion.3), kind=kOutput, calls=%fused_computation.1 | convolution fusion | flops 135274496 | bytes 4194624 | tf_op jit(solution)/shard_map/dot_general | solution.py:13
  59.8 6.1 %collective-permute-done.2 = bf16[512,256]{1,0:T(8,128)(2,1)S(1)} collective-permute-done((bf16[512,256]{1,0:T(8,128)(2,1)S(1)}, bf16[512,256]{1,0:T(8,128)(2,1)S(1)}, u32[]{:S(2)}, u32[]{:S(2)}) %collective-permute-start.2) | collective-permute-done | bytes 262176 | tf_op jit(solution)/shard_map/ppermute | solution.py:89
  65.9 26.3 %collective-permute-done.3 = bf16[512,256]{1,0:T(8,128)(2,1)} collective-permute-done((bf16[512,256]{1,0:T(8,128)(2,1)S(1)}, bf16[512,256]{1,0:T(8,128)(2,1)}, u32[]{:S(2)}, u32[]{:S(2)}) %collective-permute-start.3) | collective-permute-done | bytes 262176 | tf_op jit(solution)/shard_map/ppermute | solution.py:89
  95.3 1.9 collective-permute-start.4
  99.6 2.1 collective-permute-start.5
  101.7 5.6 %collective-permute-done.5 = bf16[2,2,64,256]{3,2,1,0:T(8,128)(2,1)} collective-permute-done((bf16[2,2,64,256]{3,2,1,0:T(8,128)(2,1)S(1)}, bf16[2,2,64,256]{3,2,1,0:T(8,128)(2,1)}, u32[]{:S(2)}, u32[]{:S(2)}) %collective-permute-start.5) | collective-permute-done | bytes 131104 | tf_op jit(solution)/shard_map/ppermute | solution.py:37
  109.0 15.6 %collective-permute-start.6 = (bf16[2,64,256]{2,1,0:T(8,128)(2,1)}, bf16[2,64,256]{2,1,0:T(8,128)(2,1)}, u32[]{:S(2)}, u32[]{:S(2)}) collective-permute-start(bf16[2,64,256]{2,1,0:T(8,128)(2,1)} %fusion.35), channel_id=1, source_target_pairs={{0,8},{1,9},{2,10},{3,11},{4,12},{5,13},{6,14},{7,15},{8,0},{9,1},... | collective-permute-start | bytes 196616 | tf_op jit(solution)/shard_map/ppermute | solution.py:37
  124.6 2.5 collective-permute-done.6
  128.6 8.4 %collective-permute-start.7 = (bf16[64,256]{1,0:T(8,128)(2,1)S(1)}, bf16[64,256]{1,0:T(8,128)(2,1)S(1)}, u32[]{:S(2)}, u32[]{:S(2)}) collective-permute-start(bf16[64,256]{1,0:T(8,128)(2,1)S(1)} %fusion.39), channel_id=1, source_target_pairs={{0,2},{1,3},{2,0},{3,1},{4,6},{5,7},{6,4},{7,5},{8,10},{9,11},{10,... | collective-permute-start | bytes 98312 | tf_op jit(solution)/shard_map/ppermute | solution.py:37
  140.4 22.6 %all_gather.7 = bf16[1024,256]{1,0:T(8,128)(2,1)S(1)} all-gather(bf16[64,256]{1,0:T(8,128)(2,1)S(1)} %get-tuple-element.12), channel_id=1, replica_groups=mesh['blk'=32,'rep'=16] {'rep'}, dimensions={0}, use_global_device_ids=true | all-gather | bytes 557056 | tf_op jit(solution)/shard_map/all_gather | solution.py:115
  166.2 2.3 collective-permute-start.16
  169.5 2.3 collective-permute-start.17
  173.9 11.5 %collective-permute-start.11 = (bf16[512,256]{1,0:T(8,128)(2,1)S(1)}, bf16[512,256]{1,0:T(8,128)(2,1)S(1)}, u32[]{:S(2)}, u32[]{:S(2)}) collective-permute-start(bf16[512,256]{1,0:T(8,128)(2,1)S(1)} %get-tuple-element.9), channel_id=1, source_target_pairs={{0,271},{1,254},{2,237},{3,220},{4,203},{5,186},{6,169},{7,152},{8... | collective-permute-start | bytes 786440 | tf_op jit(solution)/shard_map/ppermute | solution.py:134
  185.4 2.7 collective-permute-start.8
  188.0 3.4 %collective-permute-start.10 = (bf16[512,256]{1,0:T(8,128)(2,1)S(1)}, bf16[512,256]{1,0:T(8,128)(2,1)S(1)}, u32[]{:S(2)}, u32[]{:S(2)}) collective-permute-start(bf16[512,256]{1,0:T(8,128)(2,1)S(1)} %get-tuple-element.7), channel_id=1, source_target_pairs={{0,15},{1,510},{2,493},{3,476},{4,459},{5,442},{6,425},{7,408},{8,... | collective-permute-start | bytes 786440 | tf_op jit(solution)/shard_map/ppermute | solution.py:134
  191.5 10.8 %collective-permute-start.18 = (f32[2,16,256]{2,1,0:T(8,128)S(1)}, f32[2,16,256]{2,1,0:T(8,128)S(1)}, u32[]{:S(2)}, u32[]{:S(2)}) collective-permute-start(f32[2,16,256]{2,1,0:T(8,128)S(1)} %dynamic-slice_bitcast_fusion.2), channel_id=1, source_target_pairs={{0,8},{1,9},{2,10},{3,11},{4,12},{5,13},{6,14},{7,15},{8,0},{9,1},... | collective-permute-start | bytes 98312 | tf_op jit(solution)/shard_map/ppermute | solution.py:37
  202.3 29.1 %collective-permute-done.8 = bf16[512,256]{1,0:T(8,128)(2,1)S(1)} collective-permute-done((bf16[512,256]{1,0:T(8,128)(2,1)S(1)}, bf16[512,256]{1,0:T(8,128)(2,1)S(1)}, u32[]{:S(2)}, u32[]{:S(2)}) %collective-permute-start.8) | collective-permute-done | bytes 262176 | tf_op jit(solution)/shard_map/ppermute | solution.py:134
  231.5 28.4 %collective-permute-done.11 = bf16[512,256]{1,0:T(8,128)(2,1)S(1)} collective-permute-done((bf16[512,256]{1,0:T(8,128)(2,1)S(1)}, bf16[512,256]{1,0:T(8,128)(2,1)S(1)}, u32[]{:S(2)}, u32[]{:S(2)}) %collective-permute-start.11) | collective-permute-done | bytes 262176 | tf_op jit(solution)/shard_map/ppermute | solution.py:134
  266.0 3.2 collective-permute-done.19
  269.2 2.6 collective-permute-start.20
  271.9 12.1 %collective-permute-start.14 = (bf16[2,64,256]{2,1,0:T(8,128)(2,1)S(1)}, bf16[2,64,256]{2,1,0:T(8,128)(2,1)S(1)}, u32[]{:S(2)}, u32[]{:S(2)}) collective-permute-start(bf16[2,64,256]{2,1,0:T(8,128)(2,1)S(1)} %fusion.36), channel_id=1, source_target_pairs={{0,8},{1,9},{2,10},{3,11},{4,12},{5,13},{6,14},{7,15},{8,0},{9,1},... | collective-permute-start | bytes 196616 | tf_op jit(solution)/shard_map/ppermute | solution.py:37
  284.1 6.4 %collective-permute-start.21 = (f32[17,256]{1,0:T(8,128)S(1)}, f32[17,256]{1,0:T(8,128)S(1)}, u32[]{:S(2)}, u32[]{:S(2)}) collective-permute-start(f32[17,256]{1,0:T(8,128)S(1)} %fusion.57), channel_id=1, source_target_pairs={{0,32},{16,48},{32,0},{48,16},{64,96},{80,112},{96,64},{112,80},{1... | collective-permute-start | bytes 52232 | tf_op jit(solution)/shard_map/ppermute | solution.py:47
  292.3 3.4 %collective-permute-start.22 = (f32[17,256]{1,0:T(8,128)S(1)}, f32[17,256]{1,0:T(8,128)S(1)}, u32[]{:S(2)}, u32[]{:S(2)}) collective-permute-start(f32[17,256]{1,0:T(8,128)S(1)} %add.186), channel_id=1, source_target_pairs={{0,64},{16,80},{32,96},{48,112},{64,0},{80,16},{96,32},{112,48},{1... | collective-permute-start | bytes 52232 | tf_op jit(solution)/shard_map/ppermute | solution.py:47
  295.7 3.2 collective-permute-done.22
  298.9 4.1 %collective-permute-start.23 = (f32[17,256]{1,0:T(8,128)S(1)}, f32[17,256]{1,0:T(8,128)S(1)}, u32[]{:S(2)}, u32[]{:S(2)}) collective-permute-start(f32[17,256]{1,0:T(8,128)S(1)} %add.187), channel_id=1, source_target_pairs={{0,128},{16,144},{32,160},{48,176},{64,192},{80,208},{96,224},{112... | collective-permute-start | bytes 52232 | tf_op jit(solution)/shard_map/ppermute | solution.py:47
  303.1 5.0 %collective-permute-start.15 = (bf16[64,256]{1,0:T(8,128)(2,1)S(1)}, bf16[64,256]{1,0:T(8,128)(2,1)S(1)}, u32[]{:S(2)}, u32[]{:S(2)}) collective-permute-start(bf16[64,256]{1,0:T(8,128)(2,1)S(1)} %fusion.40), channel_id=1, source_target_pairs={{0,2},{1,3},{2,0},{3,1},{4,6},{5,7},{6,4},{7,5},{8,10},{9,11},{10,... | collective-permute-start | bytes 98312 | tf_op jit(solution)/shard_map/ppermute | solution.py:37
  308.5 13.6 %collective-permute-start.24 = (f32[17,256]{1,0:T(8,128)S(1)}, f32[17,256]{1,0:T(8,128)S(1)}, u32[]{:S(2)}, u32[]{:S(2)}) collective-permute-start(f32[17,256]{1,0:T(8,128)S(1)} %add.188), channel_id=1, source_target_pairs={{0,256},{16,272},{32,288},{48,304},{64,320},{80,336},{96,352},{112... | collective-permute-start | bytes 52232 | tf_op jit(solution)/shard_map/ppermute | solution.py:47
  (94 shorter events, 36.8 us)
Async XLA Ops:
  0.6 94.0 %copy-start = (bf16[256,256]{1,0:T(8,128)(2,1)S(1)}, bf16[256,256]{1,0:T(8,128)(2,1)}, u32[]{:S(2)}) copy-start(bf16[256,256]{1,0:T(8,128)(2,1)} %param.9) | copy-start | bytes 393220
  23.9 42.0 %collective-permute-start.2 = (bf16[512,256]{1,0:T(8,128)(2,1)S(1)}, bf16[512,256]{1,0:T(8,128)(2,1)S(1)}, u32[]{:S(2)}, u32[]{:S(2)}) collective-permute-start(bf16[512,256]{1,0:T(8,128)(2,1)S(1)} %get-tuple-element.10), channel_id=1, source_target_pairs={{256,0},{241,1},{226,2},{211,3},{196,4},{181,5},{166,6},{151,7},{1... | collective-permute-start | bytes 786440 | tf_op jit(solution)/shard_map/ppermute | solution.py:89
  35.3 58.6 %collective-permute-start = (bf16[512,256]{1,0:T(8,128)(2,1)S(1)}, bf16[512,256]{1,0:T(8,128)(2,1)S(1)}, u32[]{:S(2)}, u32[]{:S(2)}) collective-permute-start(bf16[512,256]{1,0:T(8,128)(2,1)S(1)} %get-tuple-element.10), channel_id=1, source_target_pairs={{0,0},{497,1},{482,2},{467,3},{452,4},{437,5},{422,6},{407,7},{392... | collective-permute-start | bytes 786440 | tf_op jit(solution)/shard_map/ppermute | solution.py:89
  37.2 55.0 %collective-permute-start.3 = (bf16[512,256]{1,0:T(8,128)(2,1)S(1)}, bf16[512,256]{1,0:T(8,128)(2,1)}, u32[]{:S(2)}, u32[]{:S(2)}) collective-permute-start(bf16[512,256]{1,0:T(8,128)(2,1)S(1)} %get-tuple-element.11), channel_id=1, source_target_pairs={{271,0},{254,1},{237,2},{220,3},{203,4},{186,5},{169,6},{152,7},{1... | collective-permute-start | bytes 786440 | tf_op jit(solution)/shard_map/ppermute | solution.py:89
  46.0 47.9 %collective-permute-start.1 = (bf16[512,256]{1,0:T(8,128)(2,1)S(1)}, bf16[512,256]{1,0:T(8,128)(2,1)S(1)}, u32[]{:S(2)}, u32[]{:S(2)}) collective-permute-start(bf16[512,256]{1,0:T(8,128)(2,1)S(1)} %get-tuple-element.11), channel_id=1, source_target_pairs={{15,0},{510,1},{493,2},{476,3},{459,4},{442,5},{425,6},{408,7},{39... | collective-permute-start | bytes 786440 | tf_op jit(solution)/shard_map/ppermute | solution.py:89
  50.7 4.1 %copy-start.8 = (s32[1,1,2,64]{3,2,1,0:T(2,128)S(1)}, s32[1,1,2,64]{3,2,1,0:T(2,128)}, u32[]{:S(2)}) copy-start(s32[1,1,2,64]{3,2,1,0:T(2,128)} %param.14) | copy-start | bytes 1540
  50.7 4.1 %copy-start.9 = (s32[1,1,2,64]{3,2,1,0:T(2,128)S(1)}, s32[1,1,2,64]{3,2,1,0:T(2,128)}, u32[]{:S(2)}) copy-start(s32[1,1,2,64]{3,2,1,0:T(2,128)} %param.13) | copy-start | bytes 1540
  58.1 35.8 %copy-start.1 = (bf16[64,16384]{1,0:T(8,128)(2,1)}, bf16[64,16384]{1,0:T(8,128)(2,1)S(1)}, u32[]{:S(2)}) copy-start(bf16[64,16384]{1,0:T(8,128)(2,1)S(1)} %convolution_convert_fusion.1) | copy-start | bytes 6291460
  59.8 34.1 %copy-start.3 = (bf16[64,16384]{1,0:T(8,128)(2,1)}, bf16[64,16384]{1,0:T(8,128)(2,1)S(1)}, u32[]{:S(2)}) copy-start(bf16[64,16384]{1,0:T(8,128)(2,1)S(1)} %convolution_convert_fusion) | copy-start | bytes 6291460
  95.2 43.6 %copy-start.7 = (f32[256]{0:T(256)S(1)}, f32[256]{0:T(256)}, u32[]{:S(2)}) copy-start(f32[256]{0:T(256)} %param.10) | copy-start | bytes 3076
  95.3 3.4 %collective-permute-start.4 = (bf16[2,2,2,64,256]{4,3,2,0,1:T(8,128)(2,1)S(1)}, bf16[2,2,2,64,256]{4,3,2,0,1:T(8,128)(2,1)S(1)}, u32[]{:S(2)}, u32[]{:S(2)}) collective-permute-start(bf16[2,2,2,64,256]{4,3,2,0,1:T(8,128)(2,1)S(1)} %fusion.32), channel_id=1, source_target_pairs={{0,1},{1,0},{2,3},{3,2},{4,5},{5,4},{6,7},{7,6},{8,9},{9,8},{10,11... | collective-permute-start | bytes 786440 | tf_op jit(solution)/shard_map/ppermute | solution.py:37
  99.6 63.5 %copy-start.4 = (bf16[64,16384]{1,0:T(8,128)(2,1)S(1)}, bf16[64,16384]{1,0:T(8,128)(2,1)}, u32[]{:S(2)}) copy-start(bf16[64,16384]{1,0:T(8,128)(2,1)} %copy-done.3) | copy-start | bytes 6291460
  99.6 7.7 %collective-permute-start.5 = (bf16[2,2,64,256]{3,2,1,0:T(8,128)(2,1)S(1)}, bf16[2,2,64,256]{3,2,1,0:T(8,128)(2,1)}, u32[]{:S(2)}, u32[]{:S(2)}) collective-permute-start(bf16[2,2,64,256]{3,2,1,0:T(8,128)(2,1)S(1)} %fusion.33), channel_id=1, source_target_pairs={{0,4},{1,5},{2,6},{3,7},{4,0},{5,1},{6,2},{7,3},{8,12},{9,13},{10,... | collective-permute-start | bytes 393224 | tf_op jit(solution)/shard_map/ppermute | solution.py:37
  109.0 18.1 %collective-permute-start.6 = (bf16[2,64,256]{2,1,0:T(8,128)(2,1)}, bf16[2,64,256]{2,1,0:T(8,128)(2,1)}, u32[]{:S(2)}, u32[]{:S(2)}) collective-permute-start(bf16[2,64,256]{2,1,0:T(8,128)(2,1)} %fusion.35), channel_id=1, source_target_pairs={{0,8},{1,9},{2,10},{3,11},{4,12},{5,13},{6,14},{7,15},{8,0},{9,1},... | collective-permute-start | bytes 196616 | tf_op jit(solution)/shard_map/ppermute | solution.py:37
  128.6 10.3 %collective-permute-start.7 = (bf16[64,256]{1,0:T(8,128)(2,1)S(1)}, bf16[64,256]{1,0:T(8,128)(2,1)S(1)}, u32[]{:S(2)}, u32[]{:S(2)}) collective-permute-start(bf16[64,256]{1,0:T(8,128)(2,1)S(1)} %fusion.39), channel_id=1, source_target_pairs={{0,2},{1,3},{2,0},{3,1},{4,6},{5,7},{6,4},{7,5},{8,10},{9,11},{10,... | collective-permute-start | bytes 98312 | tf_op jit(solution)/shard_map/ppermute | solution.py:37
  166.2 3.2 collective-permute-start.16
  169.5 22.0 %collective-permute-start.17 = (f32[2,2,16,256]{3,2,1,0:T(8,128)S(1)}, f32[2,2,16,256]{3,2,1,0:T(8,128)S(1)}, u32[]{:S(2)}, u32[]{:S(2)}) collective-permute-start(f32[2,2,16,256]{3,2,1,0:T(8,128)S(1)} %dynamic-slice_bitcast_fusion.1), channel_id=1, source_target_pairs={{0,4},{1,5},{2,6},{3,7},{4,0},{5,1},{6,2},{7,3},{8,12},{9,13},{10,... | collective-permute-start | bytes 196616 | tf_op jit(solution)/shard_map/ppermute | solution.py:37
  171.9 30.4 %collective-permute-start.9 = (bf16[512,256]{1,0:T(8,128)(2,1)S(1)}, bf16[512,256]{1,0:T(8,128)(2,1)S(1)}, u32[]{:S(2)}, u32[]{:S(2)}) collective-permute-start(bf16[512,256]{1,0:T(8,128)(2,1)S(1)} %get-tuple-element.8), channel_id=1, source_target_pairs={{0,256},{1,241},{2,226},{3,211},{4,196},{5,181},{6,166},{7,151},{8... | collective-permute-start | bytes 786440 | tf_op jit(solution)/shard_map/ppermute | solution.py:134
  173.9 86.0 %collective-permute-start.11 = (bf16[512,256]{1,0:T(8,128)(2,1)S(1)}, bf16[512,256]{1,0:T(8,128)(2,1)S(1)}, u32[]{:S(2)}, u32[]{:S(2)}) collective-permute-start(bf16[512,256]{1,0:T(8,128)(2,1)S(1)} %get-tuple-element.9), channel_id=1, source_target_pairs={{0,271},{1,254},{2,237},{3,220},{4,203},{5,186},{6,169},{7,152},{8... | collective-permute-start | bytes 786440 | tf_op jit(solution)/shard_map/ppermute | solution.py:134
  185.4 46.1 %collective-permute-start.8 = (bf16[512,256]{1,0:T(8,128)(2,1)S(1)}, bf16[512,256]{1,0:T(8,128)(2,1)S(1)}, u32[]{:S(2)}, u32[]{:S(2)}) collective-permute-start(bf16[512,256]{1,0:T(8,128)(2,1)S(1)} %get-tuple-element.6), channel_id=1, source_target_pairs={{0,0},{1,497},{2,482},{3,467},{4,452},{5,437},{6,422},{7,407},{8,3... | collective-permute-start | bytes 786440 | tf_op jit(solution)/shard_map/ppermute | solution.py:134
  188.0 71.8 %collective-permute-start.10 = (bf16[512,256]{1,0:T(8,128)(2,1)S(1)}, bf16[512,256]{1,0:T(8,128)(2,1)S(1)}, u32[]{:S(2)}, u32[]{:S(2)}) collective-permute-start(bf16[512,256]{1,0:T(8,128)(2,1)S(1)} %get-tuple-element.7), channel_id=1, source_target_pairs={{0,15},{1,510},{2,493},{3,476},{4,459},{5,442},{6,425},{7,408},{8,... | collective-permute-start | bytes 786440 | tf_op jit(solution)/shard_map/ppermute | solution.py:134
  191.5 70.5 %collective-permute-start.18 = (f32[2,16,256]{2,1,0:T(8,128)S(1)}, f32[2,16,256]{2,1,0:T(8,128)S(1)}, u32[]{:S(2)}, u32[]{:S(2)}) collective-permute-start(f32[2,16,256]{2,1,0:T(8,128)S(1)} %dynamic-slice_bitcast_fusion.2), channel_id=1, source_target_pairs={{0,8},{1,9},{2,10},{3,11},{4,12},{5,13},{6,14},{7,15},{8,0},{9,1},... | collective-permute-start | bytes 98312 | tf_op jit(solution)/shard_map/ppermute | solution.py:37
  260.1 3.9 %collective-permute-start.12 = (bf16[2,2,2,64,256]{4,3,2,1,0:T(8,128)(2,1)S(1)}, bf16[2,2,2,64,256]{4,3,2,1,0:T(8,128)(2,1)S(1)}, u32[]{:S(2)}, u32[]{:S(2)}) collective-permute-start(bf16[2,2,2,64,256]{4,3,2,1,0:T(8,128)(2,1)S(1)} %fusion.31), channel_id=1, source_target_pairs={{0,1},{1,0},{2,3},{3,2},{4,5},{5,4},{6,7},{7,6},{8,9},{9,8},{10,11... | collective-permute-start | bytes 786440 | tf_op jit(solution)/shard_map/ppermute | solution.py:37
  262.0 7.1 %collective-permute-start.19 = (f32[16,256]{1,0:T(8,128)S(1)}, f32[16,256]{1,0:T(8,128)S(1)}, u32[]{:S(2)}, u32[]{:S(2)}) collective-permute-start(f32[16,256]{1,0:T(8,128)S(1)} %dynamic-slice_bitcast_fusion.3), channel_id=1, source_target_pairs={{0,2},{1,3},{2,0},{3,1},{4,6},{5,7},{6,4},{7,5},{8,10},{9,11},{10,... | collective-permute-start | bytes 49160 | tf_op jit(solution)/shard_map/ppermute | solution.py:37
  264.1 7.8 %collective-permute-start.13 = (bf16[2,2,64,256]{3,2,1,0:T(8,128)(2,1)S(1)}, bf16[2,2,64,256]{3,2,1,0:T(8,128)(2,1)S(1)}, u32[]{:S(2)}, u32[]{:S(2)}) collective-permute-start(bf16[2,2,64,256]{3,2,1,0:T(8,128)(2,1)S(1)} %fusion.34), channel_id=1, source_target_pairs={{0,4},{1,5},{2,6},{3,7},{4,0},{5,1},{6,2},{7,3},{8,12},{9,13},{10,... | collective-permute-start | bytes 393224 | tf_op jit(solution)/shard_map/ppermute | solution.py:37
  269.2 14.9 %collective-permute-start.20 = (f32[17,256]{1,0:T(8,128)S(1)}, f32[17,256]{1,0:T(8,128)S(1)}, u32[]{:S(2)}, u32[]{:S(2)}) collective-permute-start(f32[17,256]{1,0:T(8,128)S(1)} %pad_maximum_fusion.1), channel_id=1, source_target_pairs={{0,16},{16,0},{32,48},{48,32},{64,80},{80,64},{96,112},{112,96},{1... | collective-permute-start | bytes 52232 | tf_op jit(solution)/shard_map/ppermute | solution.py:47
  271.9 31.1 %collective-permute-start.14 = (bf16[2,64,256]{2,1,0:T(8,128)(2,1)S(1)}, bf16[2,64,256]{2,1,0:T(8,128)(2,1)S(1)}, u32[]{:S(2)}, u32[]{:S(2)}) collective-permute-start(bf16[2,64,256]{2,1,0:T(8,128)(2,1)S(1)} %fusion.36), channel_id=1, source_target_pairs={{0,8},{1,9},{2,10},{3,11},{4,12},{5,13},{6,14},{7,15},{8,0},{9,1},... | collective-permute-start | bytes 196616 | tf_op jit(solution)/shard_map/ppermute | solution.py:37
  284.1 8.2 %collective-permute-start.21 = (f32[17,256]{1,0:T(8,128)S(1)}, f32[17,256]{1,0:T(8,128)S(1)}, u32[]{:S(2)}, u32[]{:S(2)}) collective-permute-start(f32[17,256]{1,0:T(8,128)S(1)} %fusion.57), channel_id=1, source_target_pairs={{0,32},{16,48},{32,0},{48,16},{64,96},{80,112},{96,64},{112,80},{1... | collective-permute-start | bytes 52232 | tf_op jit(solution)/shard_map/ppermute | solution.py:47
  292.3 6.6 %collective-permute-start.22 = (f32[17,256]{1,0:T(8,128)S(1)}, f32[17,256]{1,0:T(8,128)S(1)}, u32[]{:S(2)}, u32[]{:S(2)}) collective-permute-start(f32[17,256]{1,0:T(8,128)S(1)} %add.186), channel_id=1, source_target_pairs={{0,64},{16,80},{32,96},{48,112},{64,0},{80,16},{96,32},{112,48},{1... | collective-permute-start | bytes 52232 | tf_op jit(solution)/shard_map/ppermute | solution.py:47
  298.9 9.6 %collective-permute-start.23 = (f32[17,256]{1,0:T(8,128)S(1)}, f32[17,256]{1,0:T(8,128)S(1)}, u32[]{:S(2)}, u32[]{:S(2)}) collective-permute-start(f32[17,256]{1,0:T(8,128)S(1)} %add.187), channel_id=1, source_target_pairs={{0,128},{16,144},{32,160},{48,176},{64,192},{80,208},{96,224},{112... | collective-permute-start | bytes 52232 | tf_op jit(solution)/shard_map/ppermute | solution.py:47
  303.1 22.0 %collective-permute-start.15 = (bf16[64,256]{1,0:T(8,128)(2,1)S(1)}, bf16[64,256]{1,0:T(8,128)(2,1)S(1)}, u32[]{:S(2)}, u32[]{:S(2)}) collective-permute-start(bf16[64,256]{1,0:T(8,128)(2,1)S(1)} %fusion.40), channel_id=1, source_target_pairs={{0,2},{1,3},{2,0},{3,1},{4,6},{5,7},{6,4},{7,5},{8,10},{9,11},{10,... | collective-permute-start | bytes 98312 | tf_op jit(solution)/shard_map/ppermute | solution.py:37
  308.5 15.4 %collective-permute-start.24 = (f32[17,256]{1,0:T(8,128)S(1)}, f32[17,256]{1,0:T(8,128)S(1)}, u32[]{:S(2)}, u32[]{:S(2)}) collective-permute-start(f32[17,256]{1,0:T(8,128)S(1)} %add.188), channel_id=1, source_target_pairs={{0,256},{16,272},{32,288},{48,304},{64,320},{80,336},{96,352},{112... | collective-permute-start | bytes 52232 | tf_op jit(solution)/shard_map/ppermute | solution.py:47
  (3 other events, 3.0 us)
